TPU v7x, 128 devices: a whole 4x4x4 slice. The times are simulated.
128 devices in a mesh: store: 32 (over x, y, core), tensor: 4 (over z).
Axes of the slice: x: 4, y: 4, z: 4, core: 2. Of those that a mesh axis runs over, the one named last changes fastest.
Arguments:
- questions: bfloat16 [8192, 8192], P('store', 'tensor'), may hold values from -6 to 6
- w_query: bfloat16 [8192, 4096], P(None, 'tensor'), may hold values from -0.0625 to 0.0625
- w_key: bfloat16 [8192, 512], P(None, 'tensor'), may hold values from -0.0625 to 0.0625
- w_value: bfloat16 [8192, 512], P(None, 'tensor'), may hold values from -0.0625 to 0.0625
- passage_keys: bfloat16 [128, 512, 512], P('store', None, 'tensor'), may hold values from -240 to 240
- passage_values: bfloat16 [128, 512, 512], P('store', None, 'tensor'), may hold values from -6 to 6
- passage_ids: int32 [64, 16], P('store'), may hold values from 0 to 127, as said below
- slot_order: int32 [64, 16], P('store'), may hold values from 0 to 15, each once within a row
Outputs:
- context: bfloat16 [8192, 4096], P('store', 'tensor')
Inputs may be any that keep to these rules, and one draw needn't show every extreme that they name: `passage_ids`: passage p is stored at index p // 4 of store. Among the 32 entries of the questions of one index of store, at most 2 name passages stored at one index, and on every index some stored index is named exactly 2 times. A question may name a passage more than once.
All inputs are finite; a program needn't handle non-finite values.
Results may differ from a plain program's by a relative error of at most 0.015.
The roundings to bfloat16 on the way count: a program that leaves them out, or rounds other values in their place, can miss the bound.
Values may be sent and summed in bfloat16 or wider, within the bound.
No kernel may reach another device: no remote copies, remote signals or barrier semaphores. Data moves between devices by JAX's collectives and lax.ppermute only.
A program may use at most 192 MiB of HBM per device.

v0:
```python
import functools

import jax
import jax.numpy as jnp
from jax import lax
from jax.experimental import pallas as pl
from jax.experimental.pallas import tpu as pltpu
from jax.sharding import PartitionSpec as P

HD = 128
QLEN = 128
PLEN = 512
RETR = 16
CAP = 2


def angles(positions):
    freqs = 500000.0 ** (-(jnp.arange(HD // 2, dtype=jnp.float32) * 2.0) / HD)
    turned = positions[..., None] * freqs
    return (jnp.cos(turned), jnp.sin(turned))


def rotate(values, cosine, sine):
    half = values.shape[-1] // 2
    first = values[..., :half]
    second = values[..., half:]
    return jnp.concatenate(
        [first * cosine - second * sine, second * cosine + first * sine], axis=-1
    )


def send_kernel(loc_ref, k_ref, v_ref, c_ref, s_ref, out_ref):
    per = out_ref.shape[0]
    base = pl.program_id(0) * per

    def body(j, carry):
        loc = loc_ref[base + j]
        k = k_ref[loc].astype(jnp.float32)
        turned = pltpu.roll(k, k.shape[-1] // 2, 1)
        cos_row = c_ref[pl.ds(base + j, 1), :]
        sin_row = s_ref[pl.ds(base + j, 1), :]
        out_ref[j, 0] = (k * cos_row + turned * sin_row).astype(jnp.bfloat16)
        out_ref[j, 1] = v_ref[loc]
        return carry

    lax.fori_loop(0, per, body, 0)


def build_send(loc, cos_full, sin_full, passage_keys, passage_values):
    owners = loc.shape[0]
    stored, plen, hd = passage_keys.shape
    per = 8
    full = lambda shape: pl.BlockSpec(shape, lambda i, loc: (0,) * len(shape))
    grid_spec = pltpu.PrefetchScalarGridSpec(
        num_scalar_prefetch=1,
        grid=(owners // per,),
        in_specs=[
            full((stored, plen, hd)),
            full((stored, plen, hd)),
            full((owners, hd)),
            full((owners, hd)),
        ],
        out_specs=pl.BlockSpec((per, 2, plen, hd), lambda i, loc: (i, 0, 0, 0)),
    )
    return pl.pallas_call(
        send_kernel,
        grid_spec=grid_spec,
        out_shape=jax.ShapeDtypeStruct((owners, 2, plen, hd), jnp.bfloat16),
        compiler_params=pltpu.CompilerParams(dimension_semantics=("arbitrary",)),
        cost_estimate=pl.CostEstimate(
            flops=4 * owners * plen * hd, transcendentals=0,
            bytes_accessed=owners * plen * hd * 2 * 2 + 2 * passage_keys.size * 2,
        ),
    )(loc, passage_keys, passage_values, cos_full, sin_full)


def block_kernel(tab_ref, remap_ref, q_ref, kv_ref, m_in, l_in, a_in, m_ref, l_ref, a_ref):
    o = pl.program_id(0)

    @pl.when(o == 0)
    def _():
        m_ref[...] = m_in[...]
        l_ref[...] = l_in[...]
        a_ref[...] = a_in[...]

    qi = tab_ref[o]

    @pl.when(qi >= 0)
    def _():
        q = q_ref[qi]
        k = kv_ref[0, 0]
        v = kv_ref[0, 1]
        s = lax.dot_general(
            q, k, (((1,), (1,)), ((), ())), preferred_element_type=jnp.float32
        ) * (HD ** (-0.5))
        m = jnp.max(s, axis=1, keepdims=True)
        e = jnp.exp(s - m)
        l = jnp.sum(e, axis=1, keepdims=True)
        p = jnp.dot(e.astype(jnp.bfloat16), v, preferred_element_type=jnp.float32)
        m_old = m_ref[qi]
        m_new = jnp.maximum(m_old, m)
        w_old = jnp.exp(m_old - m_new)
        w_new = jnp.exp(m - m_new)
        l_ref[qi] = w_old * l_ref[qi] + w_new * l
        a_ref[qi] = w_old * a_ref[qi] + w_new * p
        m_ref[qi] = m_new


def attend_chunk(tab, remap, query, recv, m, l, acc):
    owners = recv.shape[0]
    nq, rows, hd = query.shape
    plen = recv.shape[2]
    full3 = lambda shape: pl.BlockSpec(shape, lambda o, t, r: (0, 0, 0))
    grid_spec = pltpu.PrefetchScalarGridSpec(
        num_scalar_prefetch=2,
        grid=(owners,),
        in_specs=[
            full3((nq, rows, hd)),
            pl.BlockSpec((1, 2, plen, hd), lambda o, t, r: (r[o], 0, 0, 0)),
            full3((nq, rows, 1)),
            full3((nq, rows, 1)),
            full3((nq, rows, hd)),
        ],
        out_specs=[full3((nq, rows, 1)), full3((nq, rows, 1)), full3((nq, rows, hd))],
    )
    flops = 4 * nq * rows * plen * hd * owners // 2
    return pl.pallas_call(
        block_kernel,
        grid_spec=grid_spec,
        out_shape=[
            jax.ShapeDtypeStruct(m.shape, jnp.float32),
            jax.ShapeDtypeStruct(l.shape, jnp.float32),
            jax.ShapeDtypeStruct(acc.shape, jnp.float32),
        ],
        input_output_aliases={4: 0, 5: 1, 6: 2},
        compiler_params=pltpu.CompilerParams(
            dimension_semantics=("arbitrary",), vmem_limit_bytes=48 * 1024 * 1024
        ),
        cost_estimate=pl.CostEstimate(
            flops=flops,
            transcendentals=nq * rows * plen * owners // 2,
            bytes_accessed=recv.size * 2 + 2 * acc.size * 4,
        ),
    )(tab, remap, query, recv, m, l, acc)


def per_device(
    questions, w_query, w_key, w_value, passage_keys, passage_values, passage_ids, slot_order
):
    kv_heads = w_key.shape[1] // HD
    q_heads = w_query.shape[1] // HD
    group = q_heads // kv_heads
    tok_rows = questions.shape[0]
    count = tok_rows // QLEN
    stored = passage_keys.shape[0]
    owners_count = lax.axis_size("store")
    me = lax.axis_index("store")

    listed = count * RETR
    my_ids = passage_ids.reshape(-1)
    my_pos = slot_order.reshape(-1)
    my_owner = my_ids // stored
    onehot = (my_owner[:, None] == jnp.arange(owners_count, dtype=jnp.int32)[None, :]).astype(
        jnp.int32
    )
    before = jnp.cumsum(onehot, axis=0) - onehot
    my_rank = jnp.sum(before * onehot, axis=1)
    hits = [onehot * (my_rank == c).astype(jnp.int32)[:, None] for c in range(CAP)]

    request = jnp.stack(
        [
            jnp.stack(
                [jnp.sum(h * (my_ids % stored)[:, None], axis=0),
                 jnp.sum(h * my_pos[:, None], axis=0)],
                axis=1,
            )
            for h in hits
        ],
        axis=1,
    )
    incoming = lax.all_to_all(request, "store", split_axis=0, concat_axis=0, tiled=True)

    sends = []
    for c in range(CAP):
        loc = incoming[:, c, 0]
        pos = incoming[:, c, 1]
        cs, sn = angles((pos * PLEN).astype(jnp.float32))
        cos_full = jnp.concatenate([cs, cs], axis=-1)
        sin_full = jnp.concatenate([-sn, sn], axis=-1)
        sends.append(build_send(loc, cos_full, sin_full, passage_keys, passage_values))

    recvs = [
        lax.all_to_all(s, "store", split_axis=0, concat_axis=0, tiled=True) for s in sends
    ]

    piece = lax.all_gather(questions, "tensor", axis=1, tiled=True)
    qf = jnp.dot(piece, w_query, preferred_element_type=jnp.float32)
    kf = jnp.dot(piece, w_key, preferred_element_type=jnp.float32)
    vf = jnp.dot(piece, w_value, preferred_element_type=jnp.float32)
    qpos = (RETR * PLEN + jnp.arange(QLEN)).astype(jnp.float32)
    cosine, sine = angles(qpos)
    cosine = cosine[None, :, None, :]
    sine = sine[None, :, None, :]
    query = rotate(qf.reshape(count, QLEN, q_heads, HD), cosine, sine).astype(jnp.bfloat16)
    self_key = rotate(kf.reshape(count, QLEN, kv_heads, HD), cosine, sine).astype(jnp.bfloat16)
    self_key = self_key.reshape(count, QLEN, HD)
    self_value = vf.astype(jnp.bfloat16).reshape(count, QLEN, HD)
    query = jnp.transpose(query, (0, 2, 1, 3))

    scale = HD ** (-0.5)
    own = jnp.einsum("qhtd,qud->qhtu", query, self_key, preferred_element_type=jnp.float32) * scale
    causal = jnp.arange(QLEN)[:, None] >= jnp.arange(QLEN)[None, :]
    own = jnp.where(causal, own, -1e30)
    own_peak = jnp.max(own, axis=-1, keepdims=True)
    own_expo = jnp.where(causal, jnp.exp(own - own_peak), 0.0)
    own_total = jnp.sum(own_expo, axis=-1, keepdims=True)
    own_part = jnp.einsum(
        "qhtu,qud->qhtd", own_expo.astype(jnp.bfloat16), self_value,
        preferred_element_type=jnp.float32,
    )
    rows = q_heads * QLEN
    m = own_peak.reshape(count, rows, 1)
    l = own_total.reshape(count, rows, 1)
    acc = own_part.reshape(count, rows, HD)
    qflat = query.reshape(count, rows, HD)

    qidx = jnp.arange(listed, dtype=jnp.int32) // RETR
    slots = jnp.arange(owners_count, dtype=jnp.int32)
    for c in range(CAP):
        hit = hits[c]
        valid = jnp.sum(hit, axis=0)
        tab = jnp.sum(hit * qidx[:, None], axis=0) + valid - 1
        remap = lax.cummax(jnp.where(valid > 0, slots, 0), axis=0)
        m, l, acc = attend_chunk(tab, remap, qflat, recvs[c], m, l, acc)

    ctx = (acc / l).reshape(count, q_heads, QLEN, HD)
    ctx = jnp.transpose(ctx, (0, 2, 1, 3)).reshape(tok_rows, q_heads * HD)
    return ctx.astype(jnp.bfloat16)


def solution(mesh):
    in_specs = (
        P("store", "tensor"),
        P(None, "tensor"),
        P(None, "tensor"),
        P(None, "tensor"),
        P("store", None, "tensor"),
        P("store", None, "tensor"),
        P("store", None),
        P("store", None),
    )
    out_specs = P("store", "tensor")
    return jax.shard_map(
        per_device, mesh=mesh, in_specs=in_specs, out_specs=out_specs, check_vma=False
    )
```

profile of v0, /device:TPU:40, one launch (start us, length us, event | category | flops | bytes accessed | tf_op | source)
XLA Modules:
  0.0 340.7 jit_solution(4737104149058959557)
XLA Ops:
  6.5 0.9 reshape.240
  9.4 7.5 %all-to-all-start = ((s32[32,2,2]{2,1,0:T(2,128)}), s32[32,2,2]{2,1,0:T(2,128)S(1)}, u32[]{:S(2)}, u32[]{:S(2)}) async-start(s32[32,2,2]{2,1,0:T(2,128)} %copy.41), calls=%async_computation | async-start | bytes 65536 | tf_op jit(solution)/shard_map/all_to_all | solution.py:181
  17.0 6.2 %all-to-all-done = s32[32,2,2]{2,1,0:T(2,128)S(1)} async-done(((s32[32,2,2]{2,1,0:T(2,128)}), s32[32,2,2]{2,1,0:T(2,128)S(1)}, u32[]{:S(2)}, u32[]{:S(2)}) %all-to-all-start) | async-done | bytes 544 | tf_op jit(solution)/shard_map/all_to_all | solution.py:181
  25.6 1.8 slice_reduce_fusion
  27.3 7.5 %shard_map.83 = bf16[32,2,512,128]{3,2,1,0:T(8,128)(2,1)} custom-call(s32[32]{0:T(128)} %get-tuple-element.17.loc_ref, bf16[4,512,128]{2,1,0:T(8,128)(2,1)} %k_ref.3, bf16[4,512,128]{2,1,0:T(8,128)(2,1)} %v_ref.3, f32[32,128]{1,0:T(8,128)} %pad_maximum_fusion.3.c_ref, f32[32,128]{1,0:T(8,128)} %pad_maximum_fusion.4.s_ref), custom_call_target="tpu_custom_call" | custom-call | flops 8388608 | bytes 9437184 | tf_op jit(solution)/shard_map/pallas_call | solution.py:65
  34.8 6.0 %all-to-all-start.2 = ((bf16[32,2,512,128]{3,2,1,0:T(8,128)(2,1)}), bf16[32,2,512,128]{3,2,1,0:T(8,128)(2,1)}, u32[]{:S(2)}, u32[]{:S(2)}) async-start(bf16[32,2,512,128]{3,2,1,0:T(8,128)(2,1)} %shard_map.83), calls=%async_computation.2 | async-start | bytes 16777216 | tf_op jit(solution)/shard_map/all_to_all | solution.py:193
  42.9 7.5 %shard_map.82 = bf16[32,2,512,128]{3,2,1,0:T(8,128)(2,1)} custom-call(s32[32]{0:T(128)} %get-tuple-element.18.loc_ref, bf16[4,512,128]{2,1,0:T(8,128)(2,1)} %k_ref.3, bf16[4,512,128]{2,1,0:T(8,128)(2,1)} %v_ref.3, f32[32,128]{1,0:T(8,128)} %pad_maximum_fusion.1.c_ref, f32[32,128]{1,0:T(8,128)} %pad_maximum_fusion.2.s_ref), custom_call_target="tpu_custom_call" | custom-call | flops 8388608 | bytes 9437184 | tf_op jit(solution)/shard_map/pallas_call | solution.py:65
  50.4 114.4 %all-to-all-done.2.kv_ref = bf16[32,2,512,128]{3,2,1,0:T(8,128)(2,1)} async-done(((bf16[32,2,512,128]{3,2,1,0:T(8,128)(2,1)}), bf16[32,2,512,128]{3,2,1,0:T(8,128)(2,1)}, u32[]{:S(2)}, u32[]{:S(2)}) %all-to-all-start.2) | async-done | bytes 8388640 | tf_op jit(solution)/shard_map/all_to_all | solution.py:193
  164.8 6.4 %all-to-all-start.1 = ((bf16[32,2,512,128]{3,2,1,0:T(8,128)(2,1)}), bf16[32,2,512,128]{3,2,1,0:T(8,128)(2,1)}, u32[]{:S(2)}, u32[]{:S(2)}) async-start(bf16[32,2,512,128]{3,2,1,0:T(8,128)(2,1)} %shard_map.82), calls=%async_computation.1 | async-start | bytes 16777216 | tf_op jit(solution)/shard_map/all_to_all | solution.py:193
  172.1 9.6 %convolution_bitcast_fusion = f32[32,8,8,128]{3,1,2,0:T(8,128)S(1)} fusion(bf16[256,8192]{1,0:T(8,128)(2,1)} %all-gather.2.cloned.1.call-done, bf16[8192,1024]{1,0:T(8,128)(2,1)} %param.9), kind=kOutput, calls=%fused_computation | convolution fusion | flops 4294967296 | bytes 22020096 | tf_op jit(solution)/shard_map/dot_general | solution.py:197
  183.0 1.1 copy-done.10
  184.1 1.3 fusion.30
  187.9 4.2 %convolution_convert_fusion = bf16[256,128]{1,0:T(8,128)(2,1)S(1)} fusion(bf16[256,8192]{1,0:T(8,128)(2,1)} %all-gather.2.cloned.1.call-done, bf16[8192,128]{1,0:T(8,128)(2,1)} %param.11), kind=kOutput, calls=%fused_computation.3 | convolution fusion | flops 536903680 | bytes 6356992 | tf_op jit(solution)/shard_map/dot_general | solution.py:199
  192.5 71.7 %shard_map.84 = (f32[2,1024,1]{2,1,0:T(8,128)S(1)}, f32[2,1024,1]{2,1,0:T(8,128)S(1)}, f32[2,1024,128]{2,1,0:T(8,128)S(1)}) custom-call(s32[32]{0:T(128)S(1)} %add_add_fusion.tab_ref, s32[32]{0:T(128)S(1)} %reduce.3.remap_ref, bf16[2,1024,128]{2,1,0:T(8,128)(2,1)S(1)} %bitcast.57, ...), custom_call_target="tpu_custom_call", output_to_operand_aliasing={{0}: (4, {}), {1}: (5, {}), {2}: (6, {})} | custom-call | flops 8589934592 | bytes 10485760 | tf_op jit(solution)/shard_map/pallas_call | solution.py:127
  264.2 1.0 copy-done.2
  265.2 1.0 copy-done.8
  266.2 29.4 %all-to-all-done.1.kv_ref = bf16[32,2,512,128]{3,2,1,0:T(8,128)(2,1)} async-done(((bf16[32,2,512,128]{3,2,1,0:T(8,128)(2,1)}), bf16[32,2,512,128]{3,2,1,0:T(8,128)(2,1)}, u32[]{:S(2)}, u32[]{:S(2)}) %all-to-all-start.1) | async-done | bytes 8388640 | tf_op jit(solution)/shard_map/all_to_all | solution.py:193
  295.6 1.2 copy-done.3
  296.9 1.0 copy-done.7
  297.9 1.2 copy-done.9
  299.1 30.6 %shard_map.85 = (f32[2,1024,1]{2,1,0:T(8,128)S(1)}, f32[2,1024,1]{2,1,0:T(8,128)S(1)}, f32[2,1024,128]{2,1,0:T(8,128)S(1)}) custom-call(s32[32]{0:T(128)S(1)} %add_add_fusion.1.tab_ref, s32[32]{0:T(128)S(1)} %reduce.remap_ref, bf16[2,1024,128]{2,1,0:T(8,128)(2,1)S(1)} %bitcast.58, ...), custom_call_target="tpu_custom_call", output_to_operand_aliasing={{0}: (4, {}), {1}: (5, {}), {2}: (6, {})} | custom-call | flops 8589934592 | bytes 10485760 | tf_op jit(solution)/shard_map/pallas_call | solution.py:127
  329.7 1.0 copy-done.4
  331.1 1.6 divide_convert_fusion
  333.0 0.9 copy.59
  (64 shorter events, 12.0 us)
Async XLA Ops:
  6.5 176.5 %copy-start = (bf16[8192,128]{1,0:T(8,128)(2,1)S(1)}, bf16[8192,128]{1,0:T(8,128)(2,1)}, u32[]{:S(2)}) copy-start(bf16[8192,128]{1,0:T(8,128)(2,1)} %param.10) | copy-start | bytes 6291460
  9.4 13.8 %all-to-all-start = ((s32[32,2,2]{2,1,0:T(2,128)}), s32[32,2,2]{2,1,0:T(2,128)S(1)}, u32[]{:S(2)}, u32[]{:S(2)}) async-start(s32[32,2,2]{2,1,0:T(2,128)} %copy.41), calls=%async_computation | async-start | bytes 65536 | tf_op jit(solution)/shard_map/all_to_all | solution.py:181
  34.8 130.0 %all-to-all-start.2 = ((bf16[32,2,512,128]{3,2,1,0:T(8,128)(2,1)}), bf16[32,2,512,128]{3,2,1,0:T(8,128)(2,1)}, u32[]{:S(2)}, u32[]{:S(2)}) async-start(bf16[32,2,512,128]{3,2,1,0:T(8,128)(2,1)} %shard_map.83), calls=%async_computation.2 | async-start | bytes 16777216 | tf_op jit(solution)/shard_map/all_to_all | solution.py:193
  40.8 131.3 %all-gather.2.cloned.1.call-start = ((), (), s32[]{:S(2)}) async-start(), calls=%async_computation.3 | async-start | bytes 5242880 | tf_op jit(solution)/shard_map/all_gather | solution.py:196
  164.8 130.8 %all-to-all-start.1 = ((bf16[32,2,512,128]{3,2,1,0:T(8,128)(2,1)}), bf16[32,2,512,128]{3,2,1,0:T(8,128)(2,1)}, u32[]{:S(2)}, u32[]{:S(2)}) async-start(bf16[32,2,512,128]{3,2,1,0:T(8,128)(2,1)} %shard_map.82), calls=%async_computation.1 | async-start | bytes 16777216 | tf_op jit(solution)/shard_map/all_to_all | solution.py:193
  181.9 2.2 copy-start.10
  184.1 1.8 copy-start.5
  185.9 1.1 copy-start.11
  187.9 4.2 %copy-start.12 = (f32[2,8,128,128]{2,3,1,0:T(8,128)S(1)}, f32[2,8,128,128]{2,3,1,0:T(8,128)}, u32[]{:S(2)}) copy-start(f32[2,8,128,128]{2,3,1,0:T(8,128)} %copy-done.11) | copy-start | bytes 3145732
  187.9 4.6 %copy-start.6 = (bf16[2,128,8,128]{3,1,2,0:T(8,128)(2,1)S(1)}, bf16[2,128,8,128]{3,1,2,0:T(8,128)(2,1)}, u32[]{:S(2)}) copy-start(bf16[2,128,8,128]{3,1,2,0:T(8,128)(2,1)} %copy-done.5) | copy-start | bytes 1572868
  264.2 1.0 copy-start.2
  265.2 1.0 copy-start.8
  295.6 1.2 copy-start.3
  296.9 1.0 copy-start.7
  297.9 1.2 copy-start.9
  299.1 34.8 %copy-start.1 = (bf16[8192,128]{1,0:T(8,128)(2,1)S(1)}, bf16[8192,128]{1,0:T(8,128)(2,1)}, u32[]{:S(2)}) copy-start(bf16[8192,128]{1,0:T(8,128)(2,1)} %param.10) | copy-start | bytes 6291460
  329.7 1.0 copy-start.4
Sparse Core Ops, SparseCore 0:
  43.3 49.5 all-gather.1
where the time goes:
time: 345 us; the launch traced here: 341 us
  waiting for transfers between devices  151 us (44%)
  Pallas kernels  117 us (34%)
  starting transfers between devices  20 us (6%)
  matrix products  15.8 us (5%)
  local copies, waits for them, and re-layouts  15.5 us (4%)
  between operations  13.7 us (4%)
  other arithmetic  7.84 us (2%)
    all_to_all x2, waiting for transfers between devices, per_device(): lax.all_to_all(s, 'store', split_axis=0, concat_axis=0, tiled=True)  144 us
    pallas_call x2, Pallas kernels, attend_chunk(): pl.pallas_call(block_kernel, grid_spec=grid_spec, out_shape=[jax.ShapeDty...  102 us
    pallas_call x2, Pallas kernels, build_send(): pl.pallas_call(send_kernel, grid_spec=grid_spec, out_shape=jax.ShapeDtype...  15 us
    all_to_all x2, starting transfers between devices, per_device(): lax.all_to_all(s, 'store', split_axis=0, concat_axis=0, tiled=True)  12.4 us
    dot_general x1, matrix products, per_device(): qf = jnp.dot(piece, w_query, preferred_element_type=jnp.float32)  9.62 us
    unnamed x28, local copies, waits for them, and re-layouts  8.71 us
    all_to_all x1, starting transfers between devices, per_device(): lax.all_to_all(request, 'store', split_axis=0, concat_axis=0, tiled=True)  7.54 us
  transfers between devices with their start and end apart: 4, of which 3 were waited for; matrix products, arithmetic and copies ran while one was open for 6% of the time, Pallas kernels for 23%

commit v1 on v0

--- a/solution.py
+++ b/solution.py
@@ -49,7 +49,7 @@
 def build_send(loc, cos_full, sin_full, passage_keys, passage_values):
     owners = loc.shape[0]
     stored, plen, hd = passage_keys.shape
-    per = 8
+    per = 4
     full = lambda shape: pl.BlockSpec(shape, lambda i, loc: (0,) * len(shape))
     grid_spec = pltpu.PrefetchScalarGridSpec(
         num_scalar_prefetch=1,
@@ -74,7 +74,11 @@
     )(loc, passage_keys, passage_values, cos_full, sin_full)
 
 
-def block_kernel(tab_ref, remap_ref, q_ref, kv_ref, m_in, l_in, a_in, m_ref, l_ref, a_ref):
+ROW_TILE = 256
+LOG2E = 1.4426950408889634
+
+
+def block_kernel(tab_ref, remap_ref, q_ref, kv_ref, m_in, l_in, a_in, m_ref, l_ref, a_ref, *out):
     o = pl.program_id(0)
 
     @pl.when(o == 0)
@@ -87,26 +91,43 @@
 
     @pl.when(qi >= 0)
     def _():
-        q = q_ref[qi]
         k = kv_ref[0, 0]
         v = kv_ref[0, 1]
-        s = lax.dot_general(
-            q, k, (((1,), (1,)), ((), ())), preferred_element_type=jnp.float32
-        ) * (HD ** (-0.5))
-        m = jnp.max(s, axis=1, keepdims=True)
-        e = jnp.exp(s - m)
-        l = jnp.sum(e, axis=1, keepdims=True)
-        p = jnp.dot(e.astype(jnp.bfloat16), v, preferred_element_type=jnp.float32)
-        m_old = m_ref[qi]
-        m_new = jnp.maximum(m_old, m)
-        w_old = jnp.exp(m_old - m_new)
-        w_new = jnp.exp(m - m_new)
-        l_ref[qi] = w_old * l_ref[qi] + w_new * l
-        a_ref[qi] = w_old * a_ref[qi] + w_new * p
-        m_ref[qi] = m_new
-
-
-def attend_chunk(tab, remap, query, recv, m, l, acc):
+        for r0 in range(0, q_ref.shape[1], ROW_TILE):
+            rows = pl.ds(r0, ROW_TILE)
+            q = q_ref[qi, rows, :]
+            s = lax.dot_general(
+                q, k, (((1,), (1,)), ((), ())), preferred_element_type=jnp.float32
+            )
+            m = jnp.max(s, axis=1, keepdims=True)
+            c = (HD ** (-0.5)) * LOG2E
+            e = jnp.exp2(s * c - m * c)
+            l = jnp.sum(e, axis=1, keepdims=True)
+            p = jnp.dot(e.astype(jnp.bfloat16), v, preferred_element_type=jnp.float32)
+            m = m * (HD ** (-0.5))
+            m_old = m_ref[qi, rows, :]
+            m_new = jnp.maximum(m_old, m)
+            w_old = jnp.exp(m_old - m_new)
+            w_new = jnp.exp(m - m_new)
+            l_ref[qi, rows, :] = w_old * l_ref[qi, rows, :] + w_new * l
+            a_ref[qi, rows, :] = w_old * a_ref[qi, rows, :] + w_new * p
+            m_ref[qi, rows, :] = m_new
+
+    if out:
+        (ctx_ref,) = out
+
+        @pl.when(o == pl.num_programs(0) - 1)
+        def _():
+            qlen = ctx_ref.shape[0] // q_ref.shape[0]
+            for j in range(q_ref.shape[0]):
+                for h in range(q_ref.shape[1] // qlen):
+                    rows = pl.ds(h * qlen, qlen)
+                    ctx_ref[pl.ds(j * qlen, qlen), pl.ds(h * HD, HD)] = (
+                        a_ref[j, rows, :] / l_ref[j, rows, :]
+                    ).astype(ctx_ref.dtype)
+
+
+def attend_chunk(tab, remap, query, recv, m, l, acc, final=False):
     owners = recv.shape[0]
     nq, rows, hd = query.shape
     plen = recv.shape[2]
@@ -121,7 +142,8 @@
             full3((nq, rows, 1)),
             full3((nq, rows, hd)),
         ],
-        out_specs=[full3((nq, rows, 1)), full3((nq, rows, 1)), full3((nq, rows, hd))],
+        out_specs=[full3((nq, rows, 1)), full3((nq, rows, 1)), full3((nq, rows, hd))]
+        + ([pl.BlockSpec((nq * QLEN, rows // QLEN * hd), lambda o, t, r: (0, 0))] if final else []),
     )
     flops = 4 * nq * rows * plen * hd * owners // 2
     return pl.pallas_call(
@@ -131,7 +153,8 @@
             jax.ShapeDtypeStruct(m.shape, jnp.float32),
             jax.ShapeDtypeStruct(l.shape, jnp.float32),
             jax.ShapeDtypeStruct(acc.shape, jnp.float32),
-        ],
+        ]
+        + ([jax.ShapeDtypeStruct((nq * QLEN, rows // QLEN * hd), jnp.bfloat16)] if final else []),
         input_output_aliases={4: 0, 5: 1, 6: 2},
         compiler_params=pltpu.CompilerParams(
             dimension_semantics=("arbitrary",), vmem_limit_bytes=48 * 1024 * 1024
@@ -231,11 +254,9 @@
         valid = jnp.sum(hit, axis=0)
         tab = jnp.sum(hit * qidx[:, None], axis=0) + valid - 1
         remap = lax.cummax(jnp.where(valid > 0, slots, 0), axis=0)
-        m, l, acc = attend_chunk(tab, remap, qflat, recvs[c], m, l, acc)
-
-    ctx = (acc / l).reshape(count, q_heads, QLEN, HD)
-    ctx = jnp.transpose(ctx, (0, 2, 1, 3)).reshape(tok_rows, q_heads * HD)
-    return ctx.astype(jnp.bfloat16)
+        outs = attend_chunk(tab, remap, qflat, recvs[c], m, l, acc, final=c == CAP - 1)
+        m, l, acc = outs[:3]
+    return outs[3]
 
 
 def solution(mesh):

time: 345 us -> 345 us (level)
  Pallas kernels: 117 us -> 123 us
    pallas_call x2, Pallas kernels: 102 us -> 106 us  [attend_chunk(): pl.pallas_call(block_kernel, grid_spec=grid_spec, out_shape=[jax.ShapeDty...]
    unnamed x28 -> x23, local copies, waits for them, and re-layouts: 8.71 us -> 8.16 us
where the time goes in v1:
time: 345 us; the launch traced here: 342 us
  waiting for transfers between devices  149 us (43%)
  Pallas kernels  123 us (36%)
  starting transfers between devices  20 us (6%)
  matrix products  15.8 us (5%)
  local copies, waits for them, and re-layouts  14.6 us (4%)
  between operations  13.7 us (4%)
  other arithmetic  5.92 us (2%)
    all_to_all x2, waiting for transfers between devices, per_device(): lax.all_to_all(s, 'store', split_axis=0, concat_axis=0, tiled=True)  142 us
    pallas_call x2, Pallas kernels, attend_chunk(): pl.pallas_call(block_kernel, grid_spec=grid_spec, out_shape=[jax.ShapeDty...  106 us
    pallas_call x2, Pallas kernels, build_send(): pl.pallas_call(send_kernel, grid_spec=grid_spec, out_shape=jax.ShapeDtype...  16.7 us
    all_to_all x2, starting transfers between devices, per_device(): lax.all_to_all(s, 'store', split_axis=0, concat_axis=0, tiled=True)  12.4 us
    dot_general x1, matrix products, per_device(): qf = jnp.dot(piece, w_query, preferred_element_type=jnp.float32)  9.62 us
    unnamed x23, local copies, waits for them, and re-layouts  8.16 us
    all_to_all x1, starting transfers between devices, per_device(): lax.all_to_all(request, 'store', split_axis=0, concat_axis=0, tiled=True)  7.54 us
  transfers between devices with their start and end apart: 4, of which 3 were waited for; matrix products, arithmetic and copies ran while one was open for 6% of the time, Pallas kernels for 23%

profile of v1, /device:TPU:40, one launch (start us, length us, event | category | flops | bytes accessed | tf_op | source)
XLA Modules:
  0.0 342.0 jit_solution(6123175294730648977)
XLA Ops:
  6.5 0.9 reshape.236
  9.4 7.5 %all-to-all-start = ((s32[32,2,2]{2,1,0:T(2,128)}), s32[32,2,2]{2,1,0:T(2,128)S(1)}, u32[]{:S(2)}, u32[]{:S(2)}) async-start(s32[32,2,2]{2,1,0:T(2,128)} %copy.38), calls=%async_computation | async-start | bytes 65536 | tf_op jit(solution)/shard_map/all_to_all | solution.py:204
  17.0 6.2 %all-to-all-done = s32[32,2,2]{2,1,0:T(2,128)S(1)} async-done(((s32[32,2,2]{2,1,0:T(2,128)}), s32[32,2,2]{2,1,0:T(2,128)S(1)}, u32[]{:S(2)}, u32[]{:S(2)}) %all-to-all-start) | async-done | bytes 544 | tf_op jit(solution)/shard_map/all_to_all | solution.py:204
  25.6 1.8 slice_reduce_fusion
  27.3 8.3 %shard_map.83 = bf16[32,2,512,128]{3,2,1,0:T(8,128)(2,1)} custom-call(s32[32]{0:T(128)} %get-tuple-element.15.loc_ref, bf16[4,512,128]{2,1,0:T(8,128)(2,1)} %k_ref.3, bf16[4,512,128]{2,1,0:T(8,128)(2,1)} %v_ref.3, f32[32,128]{1,0:T(8,128)} %pad_maximum_fusion.3.c_ref, f32[32,128]{1,0:T(8,128)} %pad_maximum_fusion.4.s_ref), custom_call_target="tpu_custom_call" | custom-call | flops 8388608 | bytes 9437184 | tf_op jit(solution)/shard_map/pallas_call | solution.py:65
  35.7 6.0 %all-to-all-start.2 = ((bf16[32,2,512,128]{3,2,1,0:T(8,128)(2,1)}), bf16[32,2,512,128]{3,2,1,0:T(8,128)(2,1)}, u32[]{:S(2)}, u32[]{:S(2)}) async-start(bf16[32,2,512,128]{3,2,1,0:T(8,128)(2,1)} %shard_map.83), calls=%async_computation.2 | async-start | bytes 16777216 | tf_op jit(solution)/shard_map/all_to_all | solution.py:216
  43.8 8.4 %shard_map.82 = bf16[32,2,512,128]{3,2,1,0:T(8,128)(2,1)} custom-call(s32[32]{0:T(128)} %get-tuple-element.16.loc_ref, bf16[4,512,128]{2,1,0:T(8,128)(2,1)} %k_ref.3, bf16[4,512,128]{2,1,0:T(8,128)(2,1)} %v_ref.3, f32[32,128]{1,0:T(8,128)} %pad_maximum_fusion.1.c_ref, f32[32,128]{1,0:T(8,128)} %pad_maximum_fusion.2.s_ref), custom_call_target="tpu_custom_call" | custom-call | flops 8388608 | bytes 9437184 | tf_op jit(solution)/shard_map/pallas_call | solution.py:65
  52.2 113.5 %all-to-all-done.2.kv_ref = bf16[32,2,512,128]{3,2,1,0:T(8,128)(2,1)} async-done(((bf16[32,2,512,128]{3,2,1,0:T(8,128)(2,1)}), bf16[32,2,512,128]{3,2,1,0:T(8,128)(2,1)}, u32[]{:S(2)}, u32[]{:S(2)}) %all-to-all-start.2) | async-done | bytes 8388640 | tf_op jit(solution)/shard_map/all_to_all | solution.py:216
  165.6 6.4 %all-to-all-start.1 = ((bf16[32,2,512,128]{3,2,1,0:T(8,128)(2,1)}), bf16[32,2,512,128]{3,2,1,0:T(8,128)(2,1)}, u32[]{:S(2)}, u32[]{:S(2)}) async-start(bf16[32,2,512,128]{3,2,1,0:T(8,128)(2,1)} %shard_map.82), calls=%async_computation.1 | async-start | bytes 16777216 | tf_op jit(solution)/shard_map/all_to_all | solution.py:216
  173.0 9.6 %convolution_bitcast_fusion = f32[32,8,8,128]{3,1,2,0:T(8,128)S(1)} fusion(bf16[256,8192]{1,0:T(8,128)(2,1)} %all-gather.2.cloned.1.call-done, bf16[8192,1024]{1,0:T(8,128)(2,1)} %param.9), kind=kOutput, calls=%fused_computation | convolution fusion | flops 4294967296 | bytes 22020096 | tf_op jit(solution)/shard_map/dot_general | solution.py:220
  183.9 1.1 copy-done.8
  185.0 1.3 fusion.30
  186.8 0.9 reshape_broadcast_in_dim.8.m_in
  188.0 0.9 reshape_broadcast_in_dim.9.l_in
  188.9 4.2 %convolution_convert_fusion = bf16[256,128]{1,0:T(8,128)(2,1)S(1)} fusion(bf16[256,8192]{1,0:T(8,128)(2,1)} %all-gather.2.cloned.1.call-done, bf16[8192,128]{1,0:T(8,128)(2,1)} %param.11), kind=kOutput, calls=%fused_computation.3 | convolution fusion | flops 536903680 | bytes 6356992 | tf_op jit(solution)/shard_map/dot_general | solution.py:222
  193.5 71.3 %shard_map.84 = (f32[2,1024,1]{2,1,0:T(8,128)S(1)}, f32[2,1024,1]{2,1,0:T(8,128)S(1)}, f32[2,1024,128]{2,1,0:T(8,128)S(1)}) custom-call(s32[32]{0:T(128)S(1)} %add_add_fusion.tab_ref, s32[32]{0:T(128)S(1)} %reduce.3.remap_ref, bf16[2,1024,128]{2,1,0:T(8,128)(2,1)S(1)} %bitcast.48, ...), custom_call_target="tpu_custom_call", output_to_operand_aliasing={{0}: (4, {}), {1}: (5, {}), {2}: (6, {})} | custom-call | flops 8589934592 | bytes 10485760 | tf_op jit(solution)/shard_map/pallas_call | solution.py:149
  264.8 1.0 copy-done.2
  265.8 1.0 copy-done.4
  266.8 1.0 copy-done.6
  267.8 28.7 %all-to-all-done.1.kv_ref = bf16[32,2,512,128]{3,2,1,0:T(8,128)(2,1)} async-done(((bf16[32,2,512,128]{3,2,1,0:T(8,128)(2,1)}), bf16[32,2,512,128]{3,2,1,0:T(8,128)(2,1)}, u32[]{:S(2)}, u32[]{:S(2)}) %all-to-all-start.1) | async-done | bytes 8388640 | tf_op jit(solution)/shard_map/all_to_all | solution.py:216
  296.5 1.2 copy-done.3
  297.7 1.2 copy-done.5
  298.9 1.2 copy-done.7
  300.2 35.0 %shard_map.85 = (f32[2,1024,1]{2,1,0:T(8,128)S(1)}, f32[2,1024,1]{2,1,0:T(8,128)S(1)}, f32[2,1024,128]{2,1,0:T(8,128)S(1)}, bf16[256,1024]{1,0:T(8,128)(2,1)}) custom-call(s32[32]{0:T(128)S(1)} %add_add_fusion.1.tab_ref, s32[32]{0:T(128)S(1)} %reduce.remap_ref, ...), custom_call_target="tpu_custom_call", output_to_operand_aliasing={{0}: (4, {}), {1}: (5, {}), {2}: (6, {})} | custom-call | flops 8589934592 | bytes 10485760 | tf_op jit(solution)/shard_map/pallas_call | solution.py:149
  (56 shorter events, 9.8 us)
Async XLA Ops:
  6.5 177.3 %copy-start = (bf16[8192,128]{1,0:T(8,128)(2,1)S(1)}, bf16[8192,128]{1,0:T(8,128)(2,1)}, u32[]{:S(2)}) copy-start(bf16[8192,128]{1,0:T(8,128)(2,1)} %param.10) | copy-start | bytes 6291460
  9.4 13.8 %all-to-all-start = ((s32[32,2,2]{2,1,0:T(2,128)}), s32[32,2,2]{2,1,0:T(2,128)S(1)}, u32[]{:S(2)}, u32[]{:S(2)}) async-start(s32[32,2,2]{2,1,0:T(2,128)} %copy.38), calls=%async_computation | async-start | bytes 65536 | tf_op jit(solution)/shard_map/all_to_all | solution.py:204
  35.7 130.0 %all-to-all-start.2 = ((bf16[32,2,512,128]{3,2,1,0:T(8,128)(2,1)}), bf16[32,2,512,128]{3,2,1,0:T(8,128)(2,1)}, u32[]{:S(2)}, u32[]{:S(2)}) async-start(bf16[32,2,512,128]{3,2,1,0:T(8,128)(2,1)} %shard_map.83), calls=%async_computation.2 | async-start | bytes 16777216 | tf_op jit(solution)/shard_map/all_to_all | solution.py:216
  41.7 131.3 %all-gather.2.cloned.1.call-start = ((), (), s32[]{:S(2)}) async-start(), calls=%async_computation.3 | async-start | bytes 5242880 | tf_op jit(solution)/shard_map/all_gather | solution.py:219
  165.6 130.8 %all-to-all-start.1 = ((bf16[32,2,512,128]{3,2,1,0:T(8,128)(2,1)}), bf16[32,2,512,128]{3,2,1,0:T(8,128)(2,1)}, u32[]{:S(2)}, u32[]{:S(2)}) async-start(bf16[32,2,512,128]{3,2,1,0:T(8,128)(2,1)} %shard_map.82), calls=%async_computation.1 | async-start | bytes 16777216 | tf_op jit(solution)/shard_map/all_to_all | solution.py:216
  182.8 2.2 copy-start.8
  186.8 1.0 copy-start.9
  188.9 4.2 %copy-start.10 = (f32[2,8,128,128]{2,3,1,0:T(8,128)S(1)}, f32[2,8,128,128]{2,3,1,0:T(8,128)}, u32[]{:S(2)}) copy-start(f32[2,8,128,128]{2,3,1,0:T(8,128)} %copy-done.9) | copy-start | bytes 3145732
  264.8 1.0 copy-start.2
  265.8 1.0 copy-start.4
  266.8 1.0 copy-start.6
  296.5 1.2 copy-start.3
  297.7 1.2 copy-start.5
  298.9 1.2 copy-start.7
  300.2 35.0 %copy-start.1 = (bf16[8192,128]{1,0:T(8,128)(2,1)S(1)}, bf16[8192,128]{1,0:T(8,128)(2,1)}, u32[]{:S(2)}) copy-start(bf16[8192,128]{1,0:T(8,128)(2,1)} %param.10) | copy-start | bytes 6291460
Sparse Core Ops, SparseCore 0:
  44.2 49.5 all-gather.1

commit v2 on v1

--- a/solution.py
+++ b/solution.py
@@ -49,7 +49,7 @@
 def build_send(loc, cos_full, sin_full, passage_keys, passage_values):
     owners = loc.shape[0]
     stored, plen, hd = passage_keys.shape
-    per = 4
+    per = 8
     full = lambda shape: pl.BlockSpec(shape, lambda i, loc: (0,) * len(shape))
     grid_spec = pltpu.PrefetchScalarGridSpec(
         num_scalar_prefetch=1,
@@ -78,7 +78,7 @@
 LOG2E = 1.4426950408889634
 
 
-def block_kernel(tab_ref, remap_ref, q_ref, kv_ref, m_in, l_in, a_in, m_ref, l_ref, a_ref, *out):
+def block_kernel(tab_ref, remap_ref, q_ref, kv_ref, m_in, l_in, a_in, m_ref, l_ref, a_ref):
     o = pl.program_id(0)
 
     @pl.when(o == 0)
@@ -113,21 +113,8 @@
             a_ref[qi, rows, :] = w_old * a_ref[qi, rows, :] + w_new * p
             m_ref[qi, rows, :] = m_new
 
-    if out:
-        (ctx_ref,) = out
-
-        @pl.when(o == pl.num_programs(0) - 1)
-        def _():
-            qlen = ctx_ref.shape[0] // q_ref.shape[0]
-            for j in range(q_ref.shape[0]):
-                for h in range(q_ref.shape[1] // qlen):
-                    rows = pl.ds(h * qlen, qlen)
-                    ctx_ref[pl.ds(j * qlen, qlen), pl.ds(h * HD, HD)] = (
-                        a_ref[j, rows, :] / l_ref[j, rows, :]
-                    ).astype(ctx_ref.dtype)
-
-
-def attend_chunk(tab, remap, query, recv, m, l, acc, final=False):
+
+def attend_chunk(tab, remap, query, recv, m, l, acc):
     owners = recv.shape[0]
     nq, rows, hd = query.shape
     plen = recv.shape[2]
@@ -142,8 +129,7 @@
             full3((nq, rows, 1)),
             full3((nq, rows, hd)),
         ],
-        out_specs=[full3((nq, rows, 1)), full3((nq, rows, 1)), full3((nq, rows, hd))]
-        + ([pl.BlockSpec((nq * QLEN, rows // QLEN * hd), lambda o, t, r: (0, 0))] if final else []),
+        out_specs=[full3((nq, rows, 1)), full3((nq, rows, 1)), full3((nq, rows, hd))],
     )
     flops = 4 * nq * rows * plen * hd * owners // 2
     return pl.pallas_call(
@@ -153,8 +139,7 @@
             jax.ShapeDtypeStruct(m.shape, jnp.float32),
             jax.ShapeDtypeStruct(l.shape, jnp.float32),
             jax.ShapeDtypeStruct(acc.shape, jnp.float32),
-        ]
-        + ([jax.ShapeDtypeStruct((nq * QLEN, rows // QLEN * hd), jnp.bfloat16)] if final else []),
+        ],
         input_output_aliases={4: 0, 5: 1, 6: 2},
         compiler_params=pltpu.CompilerParams(
             dimension_semantics=("arbitrary",), vmem_limit_bytes=48 * 1024 * 1024
@@ -254,9 +239,11 @@
         valid = jnp.sum(hit, axis=0)
         tab = jnp.sum(hit * qidx[:, None], axis=0) + valid - 1
         remap = lax.cummax(jnp.where(valid > 0, slots, 0), axis=0)
-        outs = attend_chunk(tab, remap, qflat, recvs[c], m, l, acc, final=c == CAP - 1)
-        m, l, acc = outs[:3]
-    return outs[3]
+        m, l, acc = attend_chunk(tab, remap, qflat, recvs[c], m, l, acc)
+
+    ctx = (acc / l).reshape(count, q_heads, QLEN, HD)
+    ctx = jnp.transpose(ctx, (0, 2, 1, 3)).reshape(tok_rows, q_heads * HD)
+    return ctx.astype(jnp.bfloat16)
 
 
 def solution(mesh):

time: 345 us -> 348 us (level); the launches traced: 342 us -> 341 us
  Pallas kernels: 123 us -> 119 us
    unnamed x23 -> x28, local copies, waits for them, and re-layouts: 8.16 us -> 8.71 us
  transfers between devices with their start and end apart: 4 -> 4, of which waited for: 3 -> 3; matrix products, arithmetic and copies ran while one was open for 6% -> 6% of each run, Pallas kernels for 23% -> 24%
where the time goes in v2:
time: 348 us; the launch traced here: 341 us
  waiting for transfers between devices  149 us (43%)
  Pallas kernels  119 us (34%)
  starting transfers between devices  20 us (6%)
  matrix products  15.8 us (5%)
  local copies, waits for them, and re-layouts  15.5 us (4%)
  between operations  13.7 us (4%)
  other arithmetic  7.84 us (2%)
    all_to_all x2, waiting for transfers between devices, per_device(): lax.all_to_all(s, 'store', split_axis=0, concat_axis=0, tiled=True)  142 us
    pallas_call x2, Pallas kernels, attend_chunk(): pl.pallas_call(block_kernel, grid_spec=grid_spec, out_shape=[jax.ShapeDty...  104 us
    pallas_call x2, Pallas kernels, build_send(): pl.pallas_call(send_kernel, grid_spec=grid_spec, out_shape=jax.ShapeDtype...  15 us
    all_to_all x2, starting transfers between devices, per_device(): lax.all_to_all(s, 'store', split_axis=0, concat_axis=0, tiled=True)  12.4 us
    dot_general x1, matrix products, per_device(): qf = jnp.dot(piece, w_query, preferred_element_type=jnp.float32)  9.62 us
    unnamed x28, local copies, waits for them, and re-layouts  8.71 us
    all_to_all x1, starting transfers between devices, per_device(): lax.all_to_all(request, 'store', split_axis=0, concat_axis=0, tiled=True)  7.54 us
  transfers between devices with their start and end apart: 4, of which 3 were waited for; matrix products, arithmetic and copies ran while one was open for 6% of the time, Pallas kernels for 24%

profile of v2, /device:TPU:40, one launch (start us, length us, event | category | flops | bytes accessed | tf_op | source)
XLA Modules:
  0.0 341.2 jit_solution(377220325925581112)
XLA Ops:
  6.5 0.9 reshape.240
  9.4 7.5 %all-to-all-start = ((s32[32,2,2]{2,1,0:T(2,128)}), s32[32,2,2]{2,1,0:T(2,128)S(1)}, u32[]{:S(2)}, u32[]{:S(2)}) async-start(s32[32,2,2]{2,1,0:T(2,128)} %copy.41), calls=%async_computation | async-start | bytes 65536 | tf_op jit(solution)/shard_map/all_to_all | solution.py:189
  17.0 6.2 %all-to-all-done = s32[32,2,2]{2,1,0:T(2,128)S(1)} async-done(((s32[32,2,2]{2,1,0:T(2,128)}), s32[32,2,2]{2,1,0:T(2,128)S(1)}, u32[]{:S(2)}, u32[]{:S(2)}) %all-to-all-start) | async-done | bytes 544 | tf_op jit(solution)/shard_map/all_to_all | solution.py:189
  25.6 1.8 slice_reduce_fusion
  27.3 7.5 %shard_map.83 = bf16[32,2,512,128]{3,2,1,0:T(8,128)(2,1)} custom-call(s32[32]{0:T(128)} %get-tuple-element.17.loc_ref, bf16[4,512,128]{2,1,0:T(8,128)(2,1)} %k_ref.3, bf16[4,512,128]{2,1,0:T(8,128)(2,1)} %v_ref.3, f32[32,128]{1,0:T(8,128)} %pad_maximum_fusion.3.c_ref, f32[32,128]{1,0:T(8,128)} %pad_maximum_fusion.4.s_ref), custom_call_target="tpu_custom_call" | custom-call | flops 8388608 | bytes 9437184 | tf_op jit(solution)/shard_map/pallas_call | solution.py:65
  34.8 6.0 %all-to-all-start.2 = ((bf16[32,2,512,128]{3,2,1,0:T(8,128)(2,1)}), bf16[32,2,512,128]{3,2,1,0:T(8,128)(2,1)}, u32[]{:S(2)}, u32[]{:S(2)}) async-start(bf16[32,2,512,128]{3,2,1,0:T(8,128)(2,1)} %shard_map.83), calls=%async_computation.2 | async-start | bytes 16777216 | tf_op jit(solution)/shard_map/all_to_all | solution.py:201
  42.9 7.5 %shard_map.82 = bf16[32,2,512,128]{3,2,1,0:T(8,128)(2,1)} custom-call(s32[32]{0:T(128)} %get-tuple-element.18.loc_ref, bf16[4,512,128]{2,1,0:T(8,128)(2,1)} %k_ref.3, bf16[4,512,128]{2,1,0:T(8,128)(2,1)} %v_ref.3, f32[32,128]{1,0:T(8,128)} %pad_maximum_fusion.1.c_ref, f32[32,128]{1,0:T(8,128)} %pad_maximum_fusion.2.s_ref), custom_call_target="tpu_custom_call" | custom-call | flops 8388608 | bytes 9437184 | tf_op jit(solution)/shard_map/pallas_call | solution.py:65
  50.4 114.4 %all-to-all-done.2.kv_ref = bf16[32,2,512,128]{3,2,1,0:T(8,128)(2,1)} async-done(((bf16[32,2,512,128]{3,2,1,0:T(8,128)(2,1)}), bf16[32,2,512,128]{3,2,1,0:T(8,128)(2,1)}, u32[]{:S(2)}, u32[]{:S(2)}) %all-to-all-start.2) | async-done | bytes 8388640 | tf_op jit(solution)/shard_map/all_to_all | solution.py:201
  164.8 6.4 %all-to-all-start.1 = ((bf16[32,2,512,128]{3,2,1,0:T(8,128)(2,1)}), bf16[32,2,512,128]{3,2,1,0:T(8,128)(2,1)}, u32[]{:S(2)}, u32[]{:S(2)}) async-start(bf16[32,2,512,128]{3,2,1,0:T(8,128)(2,1)} %shard_map.82), calls=%async_computation.1 | async-start | bytes 16777216 | tf_op jit(solution)/shard_map/all_to_all | solution.py:201
  172.1 9.6 %convolution_bitcast_fusion = f32[32,8,8,128]{3,1,2,0:T(8,128)S(1)} fusion(bf16[256,8192]{1,0:T(8,128)(2,1)} %all-gather.2.cloned.1.call-done, bf16[8192,1024]{1,0:T(8,128)(2,1)} %param.9), kind=kOutput, calls=%fused_computation | convolution fusion | flops 4294967296 | bytes 22020096 | tf_op jit(solution)/shard_map/dot_general | solution.py:205
  183.0 1.1 copy-done.10
  184.1 1.3 fusion.30
  187.9 4.2 %convolution_convert_fusion = bf16[256,128]{1,0:T(8,128)(2,1)S(1)} fusion(bf16[256,8192]{1,0:T(8,128)(2,1)} %all-gather.2.cloned.1.call-done, bf16[8192,128]{1,0:T(8,128)(2,1)} %param.11), kind=kOutput, calls=%fused_computation.3 | convolution fusion | flops 536903680 | bytes 6356992 | tf_op jit(solution)/shard_map/dot_general | solution.py:207
  192.5 73.1 %shard_map.84 = (f32[2,1024,1]{2,1,0:T(8,128)S(1)}, f32[2,1024,1]{2,1,0:T(8,128)S(1)}, f32[2,1024,128]{2,1,0:T(8,128)S(1)}) custom-call(s32[32]{0:T(128)S(1)} %add_add_fusion.tab_ref, s32[32]{0:T(128)S(1)} %reduce.3.remap_ref, bf16[2,1024,128]{2,1,0:T(8,128)(2,1)S(1)} %bitcast.57, ...), custom_call_target="tpu_custom_call", output_to_operand_aliasing={{0}: (4, {}), {1}: (5, {}), {2}: (6, {})} | custom-call | flops 8589934592 | bytes 10485760 | tf_op jit(solution)/shard_map/pallas_call | solution.py:135
  265.6 1.0 copy-done.2
  266.7 1.0 copy-done.8
  267.6 28.0 %all-to-all-done.1.kv_ref = bf16[32,2,512,128]{3,2,1,0:T(8,128)(2,1)} async-done(((bf16[32,2,512,128]{3,2,1,0:T(8,128)(2,1)}), bf16[32,2,512,128]{3,2,1,0:T(8,128)(2,1)}, u32[]{:S(2)}, u32[]{:S(2)}) %all-to-all-start.1) | async-done | bytes 8388640 | tf_op jit(solution)/shard_map/all_to_all | solution.py:201
  295.6 1.2 copy-done.3
  296.9 1.0 copy-done.7
  297.9 1.2 copy-done.9
  299.1 31.0 %shard_map.85 = (f32[2,1024,1]{2,1,0:T(8,128)S(1)}, f32[2,1024,1]{2,1,0:T(8,128)S(1)}, f32[2,1024,128]{2,1,0:T(8,128)S(1)}) custom-call(s32[32]{0:T(128)S(1)} %add_add_fusion.1.tab_ref, s32[32]{0:T(128)S(1)} %reduce.remap_ref, bf16[2,1024,128]{2,1,0:T(8,128)(2,1)S(1)} %bitcast.58, ...), custom_call_target="tpu_custom_call", output_to_operand_aliasing={{0}: (4, {}), {1}: (5, {}), {2}: (6, {})} | custom-call | flops 8589934592 | bytes 10485760 | tf_op jit(solution)/shard_map/pallas_call | solution.py:135
  330.2 1.0 copy-done.4
  331.5 1.6 divide_convert_fusion
  333.4 0.9 copy.59
  (64 shorter events, 12.0 us)
Async XLA Ops:
  6.5 176.5 %copy-start = (bf16[8192,128]{1,0:T(8,128)(2,1)S(1)}, bf16[8192,128]{1,0:T(8,128)(2,1)}, u32[]{:S(2)}) copy-start(bf16[8192,128]{1,0:T(8,128)(2,1)} %param.10) | copy-start | bytes 6291460
  9.4 13.8 %all-to-all-start = ((s32[32,2,2]{2,1,0:T(2,128)}), s32[32,2,2]{2,1,0:T(2,128)S(1)}, u32[]{:S(2)}, u32[]{:S(2)}) async-start(s32[32,2,2]{2,1,0:T(2,128)} %copy.41), calls=%async_computation | async-start | bytes 65536 | tf_op jit(solution)/shard_map/all_to_all | solution.py:189
  34.8 130.0 %all-to-all-start.2 = ((bf16[32,2,512,128]{3,2,1,0:T(8,128)(2,1)}), bf16[32,2,512,128]{3,2,1,0:T(8,128)(2,1)}, u32[]{:S(2)}, u32[]{:S(2)}) async-start(bf16[32,2,512,128]{3,2,1,0:T(8,128)(2,1)} %shard_map.83), calls=%async_computation.2 | async-start | bytes 16777216 | tf_op jit(solution)/shard_map/all_to_all | solution.py:201
  40.8 131.3 %all-gather.2.cloned.1.call-start = ((), (), s32[]{:S(2)}) async-start(), calls=%async_computation.3 | async-start | bytes 5242880 | tf_op jit(solution)/shard_map/all_gather | solution.py:204
  164.8 130.8 %all-to-all-start.1 = ((bf16[32,2,512,128]{3,2,1,0:T(8,128)(2,1)}), bf16[32,2,512,128]{3,2,1,0:T(8,128)(2,1)}, u32[]{:S(2)}, u32[]{:S(2)}) async-start(bf16[32,2,512,128]{3,2,1,0:T(8,128)(2,1)} %shard_map.82), calls=%async_computation.1 | async-start | bytes 16777216 | tf_op jit(solution)/shard_map/all_to_all | solution.py:201
  181.9 2.2 copy-start.10
  184.1 1.8 copy-start.5
  185.9 1.1 copy-start.11
  187.9 4.2 %copy-start.12 = (f32[2,8,128,128]{2,3,1,0:T(8,128)S(1)}, f32[2,8,128,128]{2,3,1,0:T(8,128)}, u32[]{:S(2)}) copy-start(f32[2,8,128,128]{2,3,1,0:T(8,128)} %copy-done.11) | copy-start | bytes 3145732
  187.9 4.6 %copy-start.6 = (bf16[2,128,8,128]{3,1,2,0:T(8,128)(2,1)S(1)}, bf16[2,128,8,128]{3,1,2,0:T(8,128)(2,1)}, u32[]{:S(2)}) copy-start(bf16[2,128,8,128]{3,1,2,0:T(8,128)(2,1)} %copy-done.5) | copy-start | bytes 1572868
  265.6 1.0 copy-start.2
  266.6 1.0 copy-start.8
  295.6 1.2 copy-start.3
  296.9 1.0 copy-start.7
  297.9 1.2 copy-start.9
  299.1 35.2 %copy-start.1 = (bf16[8192,128]{1,0:T(8,128)(2,1)S(1)}, bf16[8192,128]{1,0:T(8,128)(2,1)}, u32[]{:S(2)}) copy-start(bf16[8192,128]{1,0:T(8,128)(2,1)} %param.10) | copy-start | bytes 6291460
  330.2 1.0 copy-start.4
Sparse Core Ops, SparseCore 0:
  43.3 49.5 all-gather.1

commit v3 on v2

--- a/solution.py
+++ b/solution.py
@@ -74,7 +74,7 @@
     )(loc, passage_keys, passage_values, cos_full, sin_full)
 
 
-ROW_TILE = 256
+ROW_TILE = 1024
 LOG2E = 1.4426950408889634
 
 
@@ -93,43 +93,43 @@
     def _():
         k = kv_ref[0, 0]
         v = kv_ref[0, 1]
-        for r0 in range(0, q_ref.shape[1], ROW_TILE):
-            rows = pl.ds(r0, ROW_TILE)
-            q = q_ref[qi, rows, :]
-            s = lax.dot_general(
-                q, k, (((1,), (1,)), ((), ())), preferred_element_type=jnp.float32
+        c = (HD ** (-0.5)) * LOG2E
+        for r0 in range(0, q_ref.shape[2], ROW_TILE):
+            cols = pl.ds(r0, ROW_TILE)
+            s = jnp.dot(k, q_ref[qi, :, cols], preferred_element_type=jnp.float32)
+            m = jnp.max(s, axis=0, keepdims=True)
+            e = jnp.exp2(s * c - m * c)
+            l = jnp.sum(e, axis=0, keepdims=True)
+            p = lax.dot_general(
+                v, e.astype(jnp.bfloat16), (((0,), (0,)), ((), ())),
+                preferred_element_type=jnp.float32,
             )
-            m = jnp.max(s, axis=1, keepdims=True)
-            c = (HD ** (-0.5)) * LOG2E
-            e = jnp.exp2(s * c - m * c)
-            l = jnp.sum(e, axis=1, keepdims=True)
-            p = jnp.dot(e.astype(jnp.bfloat16), v, preferred_element_type=jnp.float32)
             m = m * (HD ** (-0.5))
-            m_old = m_ref[qi, rows, :]
+            m_old = m_ref[qi, :, cols]
             m_new = jnp.maximum(m_old, m)
             w_old = jnp.exp(m_old - m_new)
             w_new = jnp.exp(m - m_new)
-            l_ref[qi, rows, :] = w_old * l_ref[qi, rows, :] + w_new * l
-            a_ref[qi, rows, :] = w_old * a_ref[qi, rows, :] + w_new * p
-            m_ref[qi, rows, :] = m_new
-
-
-def attend_chunk(tab, remap, query, recv, m, l, acc):
+            l_ref[qi, :, cols] = w_old * l_ref[qi, :, cols] + w_new * l
+            a_ref[qi, :, cols] = w_old * a_ref[qi, :, cols] + w_new * p
+            m_ref[qi, :, cols] = m_new
+
+
+def attend_chunk(tab, remap, query_t, recv, m, l, acc):
     owners = recv.shape[0]
-    nq, rows, hd = query.shape
+    nq, hd, rows = query_t.shape
     plen = recv.shape[2]
     full3 = lambda shape: pl.BlockSpec(shape, lambda o, t, r: (0, 0, 0))
     grid_spec = pltpu.PrefetchScalarGridSpec(
         num_scalar_prefetch=2,
         grid=(owners,),
         in_specs=[
-            full3((nq, rows, hd)),
+            full3((nq, hd, rows)),
             pl.BlockSpec((1, 2, plen, hd), lambda o, t, r: (r[o], 0, 0, 0)),
-            full3((nq, rows, 1)),
-            full3((nq, rows, 1)),
-            full3((nq, rows, hd)),
-        ],
-        out_specs=[full3((nq, rows, 1)), full3((nq, rows, 1)), full3((nq, rows, hd))],
+            full3((nq, 1, rows)),
+            full3((nq, 1, rows)),
+            full3((nq, hd, rows)),
+        ],
+        out_specs=[full3((nq, 1, rows)), full3((nq, 1, rows)), full3((nq, hd, rows))],
     )
     flops = 4 * nq * rows * plen * hd * owners // 2
     return pl.pallas_call(
@@ -149,7 +149,7 @@
             transcendentals=nq * rows * plen * owners // 2,
             bytes_accessed=recv.size * 2 + 2 * acc.size * 4,
         ),
-    )(tab, remap, query, recv, m, l, acc)
+    )(tab, remap, query_t, recv, m, l, acc)
 
 
 def per_device(
@@ -227,10 +227,10 @@
         preferred_element_type=jnp.float32,
     )
     rows = q_heads * QLEN
-    m = own_peak.reshape(count, rows, 1)
-    l = own_total.reshape(count, rows, 1)
-    acc = own_part.reshape(count, rows, HD)
-    qflat = query.reshape(count, rows, HD)
+    m = own_peak.reshape(count, 1, rows)
+    l = own_total.reshape(count, 1, rows)
+    acc = jnp.transpose(own_part, (0, 3, 1, 2)).reshape(count, HD, rows)
+    query_t = jnp.transpose(query, (0, 3, 1, 2)).reshape(count, HD, rows)
 
     qidx = jnp.arange(listed, dtype=jnp.int32) // RETR
     slots = jnp.arange(owners_count, dtype=jnp.int32)
@@ -239,10 +239,10 @@
         valid = jnp.sum(hit, axis=0)
         tab = jnp.sum(hit * qidx[:, None], axis=0) + valid - 1
         remap = lax.cummax(jnp.where(valid > 0, slots, 0), axis=0)
-        m, l, acc = attend_chunk(tab, remap, qflat, recvs[c], m, l, acc)
-
-    ctx = (acc / l).reshape(count, q_heads, QLEN, HD)
-    ctx = jnp.transpose(ctx, (0, 2, 1, 3)).reshape(tok_rows, q_heads * HD)
+        m, l, acc = attend_chunk(tab, remap, query_t, recvs[c], m, l, acc)
+
+    ctx = (acc / l).reshape(count, HD, q_heads, QLEN)
+    ctx = jnp.transpose(ctx, (0, 3, 2, 1)).reshape(tok_rows, q_heads * HD)
     return ctx.astype(jnp.bfloat16)
 
 

time: 348 us -> 325 us (0.934)
  Pallas kernels: 119 us -> 62.7 us
  waiting for transfers between devices: 149 us -> 194 us
  local copies, waits for them, and re-layouts: 15.5 us -> 10.3 us
    pallas_call x2, Pallas kernels: 104 us -> 47.7 us  [attend_chunk(): pl.pallas_call(block_kernel, grid_spec=grid_spec, out_shape=[jax.ShapeDty...]
    all_to_all x2, waiting for transfers between devices: 142 us -> 187 us  [per_device(): lax.all_to_all(s, 'store', split_axis=0, concat_axis=0, tiled=True)]
    unnamed x28 -> x20, local copies, waits for them, and re-layouts: 8.71 us -> 3.37 us
  transfers between devices with their start and end apart: 4 -> 4, of which waited for: 3 -> 3; matrix products, arithmetic and copies ran while one was open for 6% -> 6% of each run, Pallas kernels for 24% -> 12%
where the time goes in v3:
time: 325 us; the launch traced here: 320 us
  waiting for transfers between devices  194 us (60%)
  Pallas kernels  62.7 us (19%)
  starting transfers between devices  20 us (6%)
  matrix products  13.8 us (4%)
  between operations  13.7 us (4%)
  local copies, waits for them, and re-layouts  10.3 us (3%)
  other arithmetic  6.02 us (2%)
    all_to_all x2, waiting for transfers between devices, per_device(): lax.all_to_all(s, 'store', split_axis=0, concat_axis=0, tiled=True)  187 us
    pallas_call x2, Pallas kernels, attend_chunk(): pl.pallas_call(block_kernel, grid_spec=grid_spec, out_shape=[jax.ShapeDty...  47.7 us
    pallas_call x2, Pallas kernels, build_send(): pl.pallas_call(send_kernel, grid_spec=grid_spec, out_shape=jax.ShapeDtype...  15 us
    all_to_all x2, starting transfers between devices, per_device(): lax.all_to_all(s, 'store', split_axis=0, concat_axis=0, tiled=True)  12.4 us
    dot_general x1, matrix products, per_device(): qf = jnp.dot(piece, w_query, preferred_element_type=jnp.float32)  9.44 us
    all_to_all x1, starting transfers between devices, per_device(): lax.all_to_all(request, 'store', split_axis=0, concat_axis=0, tiled=True)  7.54 us
  transfers between devices with their start and end apart: 4, of which 3 were waited for; matrix products, arithmetic and copies ran while one was open for 6% of the time, Pallas kernels for 12%

profile of v3, /device:TPU:40, one launch (start us, length us, event | category | flops | bytes accessed | tf_op | source)
XLA Modules:
  0.0 320.4 jit_solution(1291214853291298340)
XLA Ops:
  6.5 0.9 reshape.240
  7.8 0.8 mul.282
  8.7 0.7 copy.44
  9.4 7.5 %all-to-all-start = ((s32[32,2,2]{2,1,0:T(2,128)}), s32[32,2,2]{2,1,0:T(2,128)S(1)}, u32[]{:S(2)}, u32[]{:S(2)}) async-start(s32[32,2,2]{2,1,0:T(2,128)} %copy.44), calls=%async_computation | async-start | bytes 65536 | tf_op jit(solution)/shard_map/all_to_all | solution.py:189
  17.0 6.2 %all-to-all-done = s32[32,2,2]{2,1,0:T(2,128)S(1)} async-done(((s32[32,2,2]{2,1,0:T(2,128)}), s32[32,2,2]{2,1,0:T(2,128)S(1)}, u32[]{:S(2)}, u32[]{:S(2)}) %all-to-all-start) | async-done | bytes 544 | tf_op jit(solution)/shard_map/all_to_all | solution.py:189
  23.2 0.8 fusion.23
  24.2 0.7 pad_maximum_fusion.3.c_ref
  25.6 1.8 slice_reduce_fusion
  27.3 7.5 %shard_map.83 = bf16[32,2,512,128]{3,2,1,0:T(8,128)(2,1)} custom-call(s32[32]{0:T(128)} %get-tuple-element.17.loc_ref, bf16[4,512,128]{2,1,0:T(8,128)(2,1)} %k_ref.3, bf16[4,512,128]{2,1,0:T(8,128)(2,1)} %v_ref.3, f32[32,128]{1,0:T(8,128)} %pad_maximum_fusion.3.c_ref, f32[32,128]{1,0:T(8,128)} %pad_maximum_fusion.4.s_ref), custom_call_target="tpu_custom_call" | custom-call | flops 8388608 | bytes 9437184 | tf_op jit(solution)/shard_map/pallas_call | solution.py:65
  34.8 6.0 %all-to-all-start.2 = ((bf16[32,2,512,128]{3,2,1,0:T(8,128)(2,1)}), bf16[32,2,512,128]{3,2,1,0:T(8,128)(2,1)}, u32[]{:S(2)}, u32[]{:S(2)}) async-start(bf16[32,2,512,128]{3,2,1,0:T(8,128)(2,1)} %shard_map.83), calls=%async_computation.2 | async-start | bytes 16777216 | tf_op jit(solution)/shard_map/all_to_all | solution.py:201
  42.9 7.5 %shard_map.82 = bf16[32,2,512,128]{3,2,1,0:T(8,128)(2,1)} custom-call(s32[32]{0:T(128)} %get-tuple-element.18.loc_ref, bf16[4,512,128]{2,1,0:T(8,128)(2,1)} %k_ref.3, bf16[4,512,128]{2,1,0:T(8,128)(2,1)} %v_ref.3, f32[32,128]{1,0:T(8,128)} %pad_maximum_fusion.1.c_ref, f32[32,128]{1,0:T(8,128)} %pad_maximum_fusion.2.s_ref), custom_call_target="tpu_custom_call" | custom-call | flops 8388608 | bytes 9437184 | tf_op jit(solution)/shard_map/pallas_call | solution.py:65
  50.4 114.4 %all-to-all-done.2.kv_ref = bf16[32,2,512,128]{3,2,1,0:T(8,128)(2,1)} async-done(((bf16[32,2,512,128]{3,2,1,0:T(8,128)(2,1)}), bf16[32,2,512,128]{3,2,1,0:T(8,128)(2,1)}, u32[]{:S(2)}, u32[]{:S(2)}) %all-to-all-start.2) | async-done | bytes 8388640 | tf_op jit(solution)/shard_map/all_to_all | solution.py:201
  164.8 6.4 %all-to-all-start.1 = ((bf16[32,2,512,128]{3,2,1,0:T(8,128)(2,1)}), bf16[32,2,512,128]{3,2,1,0:T(8,128)(2,1)}, u32[]{:S(2)}, u32[]{:S(2)}) async-start(bf16[32,2,512,128]{3,2,1,0:T(8,128)(2,1)} %shard_map.82), calls=%async_computation.1 | async-start | bytes 16777216 | tf_op jit(solution)/shard_map/all_to_all | solution.py:201
  172.1 9.4 %convolution_bitcast_fusion = f32[32,8,8,128]{3,1,2,0:T(8,128)S(1)} fusion(bf16[256,8192]{1,0:T(8,128)(2,1)} %all-gather.2.cloned.1.call-done, bf16[8192,1024]{1,0:T(8,128)(2,1)} %param.9), kind=kOutput, calls=%fused_computation | convolution fusion | flops 4294967296 | bytes 22020096 | tf_op jit(solution)/shard_map/dot_general | solution.py:205
  182.9 1.1 copy-done.4
  184.0 1.3 fusion.30
  185.8 1.2 convolution_convert_fusion
  187.0 1.4 fusion.3
  188.5 1.6 copy.53.a_in
  190.5 32.5 %shard_map.84 = (f32[2,1,1024]{2,1,0:T(1,128)S(1)}, f32[2,1,1024]{2,1,0:T(1,128)S(1)}, f32[2,128,1024]{2,1,0:T(8,128)S(1)}) custom-call(s32[32]{0:T(128)S(1)} %add_add_fusion.tab_ref, s32[32]{0:T(128)S(1)} %reduce.3.remap_ref, bf16[2,128,1024]{2,1,0:T(8,128)(2,1)S(1)} %copy.52.q_ref, ...), custom_call_target="tpu_custom_call", output_to_operand_aliasing={{0}: (4, {}), {1}: (5, {}), {2}: (6, {})} | custom-call | flops 8589934592 | bytes 10485760 | tf_op jit(solution)/shard_map/pallas_call | solution.py:135
  223.0 72.7 %all-to-all-done.1.kv_ref = bf16[32,2,512,128]{3,2,1,0:T(8,128)(2,1)} async-done(((bf16[32,2,512,128]{3,2,1,0:T(8,128)(2,1)}), bf16[32,2,512,128]{3,2,1,0:T(8,128)(2,1)}, u32[]{:S(2)}, u32[]{:S(2)}) %all-to-all-start.1) | async-done | bytes 8388640 | tf_op jit(solution)/shard_map/all_to_all | solution.py:201
  295.6 1.0 copy-done.3
  296.7 15.2 %shard_map.85 = (f32[2,1,1024]{2,1,0:T(1,128)S(1)}, f32[2,1,1024]{2,1,0:T(1,128)S(1)}, f32[2,128,1024]{2,1,0:T(8,128)S(1)}) custom-call(s32[32]{0:T(128)S(1)} %add_add_fusion.1.tab_ref, s32[32]{0:T(128)S(1)} %reduce.remap_ref, bf16[2,128,1024]{2,1,0:T(8,128)(2,1)S(1)} %copy-done.3, ...), custom_call_target="tpu_custom_call", output_to_operand_aliasing={{0}: (4, {}), {1}: (5, {}), {2}: (6, {})} | custom-call | flops 8589934592 | bytes 10485760 | tf_op jit(solution)/shard_map/pallas_call | solution.py:135
  312.6 0.9 copy.66
  (56 shorter events, 7.1 us)
Async XLA Ops:
  6.5 176.3 %copy-start = (bf16[8192,128]{1,0:T(8,128)(2,1)S(1)}, bf16[8192,128]{1,0:T(8,128)(2,1)}, u32[]{:S(2)}) copy-start(bf16[8192,128]{1,0:T(8,128)(2,1)} %param.10) | copy-start | bytes 6291460
  9.4 13.8 %all-to-all-start = ((s32[32,2,2]{2,1,0:T(2,128)}), s32[32,2,2]{2,1,0:T(2,128)S(1)}, u32[]{:S(2)}, u32[]{:S(2)}) async-start(s32[32,2,2]{2,1,0:T(2,128)} %copy.44), calls=%async_computation | async-start | bytes 65536 | tf_op jit(solution)/shard_map/all_to_all | solution.py:189
  34.8 130.0 %all-to-all-start.2 = ((bf16[32,2,512,128]{3,2,1,0:T(8,128)(2,1)}), bf16[32,2,512,128]{3,2,1,0:T(8,128)(2,1)}, u32[]{:S(2)}, u32[]{:S(2)}) async-start(bf16[32,2,512,128]{3,2,1,0:T(8,128)(2,1)} %shard_map.83), calls=%async_computation.2 | async-start | bytes 16777216 | tf_op jit(solution)/shard_map/all_to_all | solution.py:201
  40.8 131.3 %all-gather.2.cloned.1.call-start = ((), (), s32[]{:S(2)}) async-start(), calls=%async_computation.3 | async-start | bytes 5242880 | tf_op jit(solution)/shard_map/all_gather | solution.py:204
  164.8 130.8 %all-to-all-start.1 = ((bf16[32,2,512,128]{3,2,1,0:T(8,128)(2,1)}), bf16[32,2,512,128]{3,2,1,0:T(8,128)(2,1)}, u32[]{:S(2)}, u32[]{:S(2)}) async-start(bf16[32,2,512,128]{3,2,1,0:T(8,128)(2,1)} %shard_map.82), calls=%async_computation.1 | async-start | bytes 16777216 | tf_op jit(solution)/shard_map/all_to_all | solution.py:201
  181.8 2.2 copy-start.4
  184.0 1.8 copy-start.5
  184.0 1.8 copy-start.7
  187.0 3.0 copy-start.6
  190.2 32.7 %copy-start.2 = (bf16[2,128,1024]{2,1,0:T(8,128)(2,1)}, bf16[2,128,1024]{2,1,0:T(8,128)(2,1)S(1)}, u32[]{:S(2)}) copy-start(bf16[2,128,1024]{2,1,0:T(8,128)(2,1)S(1)} %copy.52.q_ref) | copy-start | bytes 1572868
  295.6 1.0 copy-start.3
  296.7 16.8 %copy-start.1 = (bf16[8192,128]{1,0:T(8,128)(2,1)S(1)}, bf16[8192,128]{1,0:T(8,128)(2,1)}, u32[]{:S(2)}) copy-start(bf16[8192,128]{1,0:T(8,128)(2,1)} %param.10) | copy-start | bytes 6291460
Sparse Core Ops, SparseCore 0:
  43.3 49.5 all-gather.1

commit v4 on v3

--- a/solution.py
+++ b/solution.py
@@ -152,6 +152,47 @@
     )(tab, remap, query_t, recv, m, l, acc)
 
 
+def translations(n):
+    if n == 32:
+        dims = (4, 4, 2)
+    else:
+        dims = (n,)
+    moves = []
+    for t in range(n):
+        rest, parts = t, []
+        for d in reversed(dims):
+            parts.append(rest % d)
+            rest //= d
+        parts = parts[::-1]
+
+        def dest(i, parts=parts):
+            rest, coords = i, []
+            for d in reversed(dims):
+                coords.append(rest % d)
+                rest //= d
+            coords = coords[::-1]
+            out = 0
+            for c, p, d in zip(coords, parts, dims):
+                out = out * d + (c + p) % d
+            return out
+
+        moves.append([dest(i) for i in range(n)])
+    return moves
+
+
+def exchange(send, moves, me):
+    n = send.shape[0]
+    got = []
+    for t, dest in enumerate(moves):
+        target = jnp.asarray(dest, jnp.int32)[me]
+        piece = lax.dynamic_index_in_dim(send, target, 0, keepdims=False)
+        if t == 0:
+            got.append(piece)
+        else:
+            got.append(lax.ppermute(piece, "store", [(i, dest[i]) for i in range(n)]))
+    return jnp.stack(got)
+
+
 def per_device(
     questions, w_query, w_key, w_value, passage_keys, passage_values, passage_ids, slot_order
 ):
@@ -197,9 +238,18 @@
         sin_full = jnp.concatenate([-sn, sn], axis=-1)
         sends.append(build_send(loc, cos_full, sin_full, passage_keys, passage_values))
 
+    moves = translations(owners_count)
     recvs = [
-        lax.all_to_all(s, "store", split_axis=0, concat_axis=0, tiled=True) for s in sends
+        lax.all_to_all(sends[0], "store", split_axis=0, concat_axis=0, tiled=True),
+        exchange(sends[1], moves, me),
     ]
+    src = []
+    for dest in moves:
+        inv = [0] * owners_count
+        for i, j in enumerate(dest):
+            inv[j] = i
+        src.append(inv)
+    src_of = jnp.asarray(src, jnp.int32)[:, me]
 
     piece = lax.all_gather(questions, "tensor", axis=1, tiled=True)
     qf = jnp.dot(piece, w_query, preferred_element_type=jnp.float32)
@@ -236,6 +286,8 @@
     slots = jnp.arange(owners_count, dtype=jnp.int32)
     for c in range(CAP):
         hit = hits[c]
+        if c == 1:
+            hit = hit[:, src_of]
         valid = jnp.sum(hit, axis=0)
         tab = jnp.sum(hit * qidx[:, None], axis=0) + valid - 1
         remap = lax.cummax(jnp.where(valid > 0, slots, 0), axis=0)

time: 325 us -> 505 us (1.55)
  local copies, waits for them, and re-layouts: 10.3 us -> 85.9 us
  between operations: 13.7 us -> 72.3 us
  starting transfers between devices: 20 us -> 49.9 us
  waiting for transfers between devices: 194 us -> 204 us
    ppermute x0 -> x31, waiting for transfers between devices: none -> 204 us  [exchange(): got.append(lax.ppermute(piece, 'store', [(i, dest[i]) for i in range(n)]))]
    all_to_all x2 -> x1, waiting for transfers between devices: 187 us -> 0.01 us  [per_device(): lax.all_to_all(sends[0], 'store', split_axis=0, concat_axis=0, tiled=True)]
    dynamic_slice x0 -> x31, local copies, waits for them, and re-layouts: none -> 39.7 us  [exchange(): target = jnp.asarray(dest, jnp.int32)[me]]
    ppermute x0 -> x31, starting transfers between devices: none -> 34.9 us  [exchange(): got.append(lax.ppermute(piece, 'store', [(i, dest[i]) for i in range(n)]))]
    unnamed x20 -> x64, local copies, waits for them, and re-layouts: 3.37 us -> 27.7 us
    squeeze x0 -> x2, local copies, waits for them, and re-layouts: none -> 8.53 us  [exchange(): piece = lax.dynamic_index_in_dim(send, target, 0, keepdims=False)]
    all_to_all x1, waiting for transfers between devices: 6.19 us -> 0.01 us  [per_device(): lax.all_to_all(request, 'store', split_axis=0, concat_axis=0, tiled=True)]
    all_to_all x2 -> x1, starting transfers between devices: 12.4 us -> 7.52 us  [per_device(): lax.all_to_all(sends[0], 'store', split_axis=0, concat_axis=0, tiled=True)]
  transfers between devices with their start and end apart: 4 -> 34, of which waited for: 3 -> 24; matrix products, arithmetic and copies ran while one was open for 6% -> 21% of each run, Pallas kernels for 12% -> 3%
where the time goes in v4:
time: 505 us; the launch traced here: 500 us
  waiting for transfers between devices  204 us (40%)
  local copies, waits for them, and re-layouts  85.9 us (17%)
  between operations  72.3 us (14%)
  Pallas kernels  63.4 us (13%)
  starting transfers between devices  49.9 us (10%)
  matrix products  16.1 us (3%)
  other arithmetic  8.06 us (2%)
    ppermute x31, waiting for transfers between devices, exchange(): got.append(lax.ppermute(piece, 'store', [(i, dest[i]) for i in range(n)]))  204 us
    pallas_call x2, Pallas kernels, attend_chunk(): pl.pallas_call(block_kernel, grid_spec=grid_spec, out_shape=[jax.ShapeDty...  48.5 us
    dynamic_slice x31, local copies, waits for them, and re-layouts, exchange(): target = jnp.asarray(dest, jnp.int32)[me]  39.7 us
    ppermute x31, starting transfers between devices, exchange(): got.append(lax.ppermute(piece, 'store', [(i, dest[i]) for i in range(n)]))  34.9 us
    unnamed x64, local copies, waits for them, and re-layouts  27.7 us
    pallas_call x2, Pallas kernels, build_send(): pl.pallas_call(send_kernel, grid_spec=grid_spec, out_shape=jax.ShapeDtype...  14.9 us
  transfers between devices with their start and end apart: 34, of which 24 were waited for; matrix products, arithmetic and copies ran while one was open for 21% of the time, Pallas kernels for 3%

profile of v4, /device:TPU:40, one launch (start us, length us, event | category | flops | bytes accessed | tf_op | source)
XLA Modules:
  0.0 500.0 jit_solution(6423819706076663531)
XLA Ops:
  10.0 7.5 %all-to-all-start = ((s32[32,2,2]{2,1,0:T(2,128)}), s32[32,2,2]{2,1,0:T(2,128)S(1)}, u32[]{:S(2)}, u32[]{:S(2)}) async-start(s32[32,2,2]{2,1,0:T(2,128)} %copy.81), calls=%async_computation | async-start | bytes 65536 | tf_op jit(solution)/shard_map/all_to_all | solution.py:230
  122.3 7.5 %shard_map.379 = bf16[32,2,512,128]{3,2,1,0:T(8,128)(2,1)} custom-call(s32[32]{0:T(128)} %get-tuple-element.18.loc_ref, bf16[4,512,128]{2,1,0:T(8,128)(2,1)} %k_ref.3, bf16[4,512,128]{2,1,0:T(8,128)(2,1)} %v_ref.3, f32[32,128]{1,0:T(8,128)} %pad_maximum_fusion.1.c_ref, f32[32,128]{1,0:T(8,128)} %pad_maximum_fusion.2.s_ref), custom_call_target="tpu_custom_call" | custom-call | flops 8388608 | bytes 9437184 | tf_op jit(solution)/shard_map/pallas_call | solution.py:65
  133.8 4.7 dynamic-slice_bitcast_fusion
  147.4 7.5 %shard_map.380 = bf16[32,2,512,128]{3,2,1,0:T(8,128)(2,1)} custom-call(s32[32]{0:T(128)} %get-tuple-element.17.loc_ref, bf16[4,512,128]{2,1,0:T(8,128)(2,1)} %k_ref.3, bf16[4,512,128]{2,1,0:T(8,128)(2,1)} %v_ref.3, f32[32,128]{1,0:T(8,128)} %pad_maximum_fusion.3.c_ref, f32[32,128]{1,0:T(8,128)} %pad_maximum_fusion.4.s_ref), custom_call_target="tpu_custom_call" | custom-call | flops 8388608 | bytes 9437184 | tf_op jit(solution)/shard_map/pallas_call | solution.py:65
  154.8 7.5 %all-to-all-start.1 = ((bf16[32,2,512,128]{3,2,1,0:T(8,128)(2,1)}), bf16[32,2,512,128]{3,2,1,0:T(8,128)(2,1)}, u32[]{:S(2)}, u32[]{:S(2)}) async-start(bf16[32,2,512,128]{3,2,1,0:T(8,128)(2,1)} %shard_map.380), calls=%async_computation.1 | async-start | bytes 16777216 | tf_op jit(solution)/shard_map/all_to_all | solution.py:243
  168.2 100.1 %collective-permute-done.2 = bf16[2,512,128]{2,1,0:T(8,128)(2,1)S(1)} collective-permute-done((bf16[2,512,128]{2,1,0:T(8,128)(2,1)}, bf16[2,512,128]{2,1,0:T(8,128)(2,1)S(1)}, u32[]{:S(2)}, u32[]{:S(2)}) %collective-permute-start.2) | collective-permute-done | bytes 262176 | tf_op jit(solution)/shard_map/ppermute | solution.py:192
  269.0 5.2 %collective-permute-start.5 = (bf16[2,512,128]{2,1,0:T(8,128)(2,1)}, bf16[2,512,128]{2,1,0:T(8,128)(2,1)S(1)}, u32[]{:S(2)}, u32[]{:S(2)}) collective-permute-start(bf16[2,512,128]{2,1,0:T(8,128)(2,1)} %get-tuple-element.52), channel_id=1, source_target_pairs={{0,24},{4,28},{8,0},{12,4},{16,8},{20,12},{24,16},{28,20},{32,56},... | collective-permute-start | bytes 786440 | tf_op jit(solution)/shard_map/ppermute | solution.py:192
  275.0 4.7 collective-permute-done.4
  280.4 5.5 %collective-permute-done.5 = bf16[2,512,128]{2,1,0:T(8,128)(2,1)S(1)} collective-permute-done((bf16[2,512,128]{2,1,0:T(8,128)(2,1)}, bf16[2,512,128]{2,1,0:T(8,128)(2,1)S(1)}, u32[]{:S(2)}, u32[]{:S(2)}) %collective-permute-start.5) | collective-permute-done | bytes 262176 | tf_op jit(solution)/shard_map/ppermute | solution.py:192
  286.6 4.8 collective-permute-done.6
  296.1 5.1 %collective-permute-done.8 = bf16[2,512,128]{2,1,0:T(8,128)(2,1)S(1)} collective-permute-done((bf16[2,512,128]{2,1,0:T(8,128)(2,1)}, bf16[2,512,128]{2,1,0:T(8,128)(2,1)S(1)}, u32[]{:S(2)}, u32[]{:S(2)}) %collective-permute-start.8) | collective-permute-done | bytes 262176 | tf_op jit(solution)/shard_map/ppermute | solution.py:192
  301.9 7.1 %collective-permute-done.9 = bf16[2,512,128]{2,1,0:T(8,128)(2,1)S(1)} collective-permute-done((bf16[2,512,128]{2,1,0:T(8,128)(2,1)}, bf16[2,512,128]{2,1,0:T(8,128)(2,1)S(1)}, u32[]{:S(2)}, u32[]{:S(2)}) %collective-permute-start.9) | collective-permute-done | bytes 262176 | tf_op jit(solution)/shard_map/ppermute | solution.py:192
  309.8 4.2 collective-permute-done.10
  314.7 5.8 %collective-permute-done.11 = bf16[2,512,128]{2,1,0:T(8,128)(2,1)S(1)} collective-permute-done((bf16[2,512,128]{2,1,0:T(8,128)(2,1)}, bf16[2,512,128]{2,1,0:T(8,128)(2,1)S(1)}, u32[]{:S(2)}, u32[]{:S(2)}) %collective-permute-start.11) | collective-permute-done | bytes 262176 | tf_op jit(solution)/shard_map/ppermute | solution.py:192
  321.3 4.8 collective-permute-done.12
  326.8 5.8 %collective-permute-done.13 = bf16[2,512,128]{2,1,0:T(8,128)(2,1)S(1)} collective-permute-done((bf16[2,512,128]{2,1,0:T(8,128)(2,1)}, bf16[2,512,128]{2,1,0:T(8,128)(2,1)S(1)}, u32[]{:S(2)}, u32[]{:S(2)}) %collective-permute-start.13) | collective-permute-done | bytes 262176 | tf_op jit(solution)/shard_map/ppermute | solution.py:192
  333.4 8.9 %collective-permute-done.14 = bf16[2,512,128]{2,1,0:T(8,128)(2,1)S(1)} collective-permute-done((bf16[2,512,128]{2,1,0:T(8,128)(2,1)}, bf16[2,512,128]{2,1,0:T(8,128)(2,1)S(1)}, u32[]{:S(2)}, u32[]{:S(2)}) %collective-permute-start.14) | collective-permute-done | bytes 262176 | tf_op jit(solution)/shard_map/ppermute | solution.py:192
  353.8 5.6 %collective-permute-done.17 = bf16[2,512,128]{2,1,0:T(8,128)(2,1)S(1)} collective-permute-done((bf16[2,512,128]{2,1,0:T(8,128)(2,1)}, bf16[2,512,128]{2,1,0:T(8,128)(2,1)S(1)}, u32[]{:S(2)}, u32[]{:S(2)}) %collective-permute-start.17) | collective-permute-done | bytes 262176 | tf_op jit(solution)/shard_map/ppermute | solution.py:192
  365.6 5.9 %collective-permute-done.19 = bf16[2,512,128]{2,1,0:T(8,128)(2,1)S(1)} collective-permute-done((bf16[2,512,128]{2,1,0:T(8,128)(2,1)S(1)}, bf16[2,512,128]{2,1,0:T(8,128)(2,1)S(1)}, u32[]{:S(2)}, u32[]{:S(2)}) %collective-permute-start.19) | collective-permute-done | bytes 262176 | tf_op jit(solution)/shard_map/ppermute | solution.py:192
  378.7 4.4 collective-permute-done.21
  407.2 7.4 %collective-permute-done.27 = bf16[2,512,128]{2,1,0:T(8,128)(2,1)S(1)} collective-permute-done((bf16[2,512,128]{2,1,0:T(8,128)(2,1)S(1)}, bf16[2,512,128]{2,1,0:T(8,128)(2,1)S(1)}, u32[]{:S(2)}, u32[]{:S(2)}) %collective-permute-start.27) | collective-permute-done | bytes 262176 | tf_op jit(solution)/shard_map/ppermute | solution.py:192
  420.3 9.5 %convolution_bitcast_fusion = f32[32,8,8,128]{3,1,2,0:T(8,128)S(1)} fusion(bf16[256,8192]{1,0:T(8,128)(2,1)} %all-gather.2.cloned.1.call-done, bf16[8192,1024]{1,0:T(8,128)(2,1)} %param.42), kind=kOutput, calls=%fused_computation.1 | convolution fusion | flops 4294967296 | bytes 22020096 | tf_op jit(solution)/shard_map/dot_general | solution.py:255
  443.0 30.6 %shard_map.381 = (f32[2,1,1024]{2,1,0:T(1,128)S(1)}, f32[2,1,1024]{2,1,0:T(1,128)S(1)}, f32[2,128,1024]{2,1,0:T(8,128)S(1)}) custom-call(s32[32]{0:T(128)S(1)} %add_add_fusion.tab_ref, s32[32]{0:T(128)S(1)} %reduce.6.remap_ref, bf16[2,128,1024]{2,1,0:T(8,128)(2,1)S(1)} %copy-done.1, ...), custom_call_target="tpu_custom_call", output_to_operand_aliasing={{0}: (4, {}), {1}: (5, {}), {2}: (6, {})} | custom-call | flops 8589934592 | bytes 10485760 | tf_op jit(solution)/shard_map/pallas_call | solution.py:135
  473.5 18.0 %shard_map.382 = (f32[2,1,1024]{2,1,0:T(1,128)S(1)}, f32[2,1,1024]{2,1,0:T(1,128)S(1)}, f32[2,128,1024]{2,1,0:T(8,128)S(1)}) custom-call(s32[32]{0:T(128)S(1)} %add_add_fusion.1.tab_ref, s32[32]{0:T(128)S(1)} %reduce.3.remap_ref, bf16[2,128,1024]{2,1,0:T(8,128)(2,1)S(1)} %copy-done.2, ...), custom_call_target="tpu_custom_call", output_to_operand_aliasing={{0}: (4, {}), {1}: (5, {}), {2}: (6, {})} | custom-call | flops 8589934592 | bytes 10485760 | tf_op jit(solution)/shard_map/pallas_call | solution.py:135
  (199 shorter events, 149.7 us)
Async XLA Ops:
  6.5 413.8 %all-gather.2.cloned.1.call-start = ((), (), s32[]{:S(2)}) async-start(), calls=%async_computation.2 | async-start | bytes 5242880 | tf_op jit(solution)/shard_map/all_gather | solution.py:254
  10.0 108.1 %all-to-all-start = ((s32[32,2,2]{2,1,0:T(2,128)}), s32[32,2,2]{2,1,0:T(2,128)S(1)}, u32[]{:S(2)}, u32[]{:S(2)}) async-start(s32[32,2,2]{2,1,0:T(2,128)} %copy.81), calls=%async_computation | async-start | bytes 65536 | tf_op jit(solution)/shard_map/all_to_all | solution.py:230
  133.6 28.8 %collective-permute-start = (bf16[2,512,128]{2,1,0:T(8,128)(2,1)}, bf16[2,512,128]{2,1,0:T(8,128)(2,1)}, u32[]{:S(2)}, u32[]{:S(2)}) collective-permute-start(bf16[2,512,128]{2,1,0:T(8,128)(2,1)} %get-tuple-element.57), channel_id=1, source_target_pairs={{0,4},{4,0},{8,12},{12,8},{16,20},{20,16},{24,28},{28,24},{32,36},... | collective-permute-start | bytes 786440 | tf_op jit(solution)/shard_map/ppermute | solution.py:192
  138.5 280.1 %collective-permute-start.30 = (bf16[2,512,128]{2,1,0:T(8,128)(2,1)S(1)}, bf16[2,512,128]{2,1,0:T(8,128)(2,1)}, u32[]{:S(2)}, u32[]{:S(2)}) collective-permute-start(bf16[2,512,128]{2,1,0:T(8,128)(2,1)S(1)} %get-tuple-element.27), channel_id=1, source_target_pairs={{0,124},{4,120},{8,100},{12,96},{16,108},{20,104},{24,116},{28,112... | collective-permute-start | bytes 786440 | tf_op jit(solution)/shard_map/ppermute | solution.py:192
  141.3 275.7 %collective-permute-start.29 = (bf16[2,512,128]{2,1,0:T(8,128)(2,1)S(1)}, bf16[2,512,128]{2,1,0:T(8,128)(2,1)}, u32[]{:S(2)}, u32[]{:S(2)}) collective-permute-start(bf16[2,512,128]{2,1,0:T(8,128)(2,1)S(1)} %get-tuple-element.28), channel_id=1, source_target_pairs={{0,120},{4,124},{8,96},{12,100},{16,104},{20,108},{24,112},{28,116... | collective-permute-start | bytes 786440 | tf_op jit(solution)/shard_map/ppermute | solution.py:192
  144.2 271.0 %collective-permute-start.28 = (bf16[2,512,128]{2,1,0:T(8,128)(2,1)S(1)}, bf16[2,512,128]{2,1,0:T(8,128)(2,1)}, u32[]{:S(2)}, u32[]{:S(2)}) collective-permute-start(bf16[2,512,128]{2,1,0:T(8,128)(2,1)S(1)} %get-tuple-element.29), channel_id=1, source_target_pairs={{0,116},{4,112},{8,124},{12,120},{16,100},{20,96},{24,108},{28,104... | collective-permute-start | bytes 786440 | tf_op jit(solution)/shard_map/ppermute | solution.py:192
  144.2 21.2 %collective-permute-start.1 = (bf16[2,512,128]{2,1,0:T(8,128)(2,1)}, bf16[2,512,128]{2,1,0:T(8,128)(2,1)}, u32[]{:S(2)}, u32[]{:S(2)}) collective-permute-start(bf16[2,512,128]{2,1,0:T(8,128)(2,1)} %get-tuple-element.56), channel_id=1, source_target_pairs={{0,8},{4,12},{8,16},{12,20},{16,24},{20,28},{24,0},{28,4},{32,40},... | collective-permute-start | bytes 786440 | tf_op jit(solution)/shard_map/ppermute | solution.py:192
  154.8 287.1 %all-to-all-start.1 = ((bf16[32,2,512,128]{3,2,1,0:T(8,128)(2,1)}), bf16[32,2,512,128]{3,2,1,0:T(8,128)(2,1)}, u32[]{:S(2)}, u32[]{:S(2)}) async-start(bf16[32,2,512,128]{3,2,1,0:T(8,128)(2,1)} %shard_map.380), calls=%async_computation.1 | async-start | bytes 16777216 | tf_op jit(solution)/shard_map/all_to_all | solution.py:243
  162.5 105.8 %collective-permute-start.2 = (bf16[2,512,128]{2,1,0:T(8,128)(2,1)}, bf16[2,512,128]{2,1,0:T(8,128)(2,1)S(1)}, u32[]{:S(2)}, u32[]{:S(2)}) collective-permute-start(bf16[2,512,128]{2,1,0:T(8,128)(2,1)} %get-tuple-element.55), channel_id=1, source_target_pairs={{0,12},{4,8},{8,20},{12,16},{16,28},{20,24},{24,4},{28,0},{32,44},... | collective-permute-start | bytes 786440 | tf_op jit(solution)/shard_map/ppermute | solution.py:192
  165.4 103.6 %collective-permute-start.3 = (bf16[2,512,128]{2,1,0:T(8,128)(2,1)}, bf16[2,512,128]{2,1,0:T(8,128)(2,1)S(1)}, u32[]{:S(2)}, u32[]{:S(2)}) collective-permute-start(bf16[2,512,128]{2,1,0:T(8,128)(2,1)} %get-tuple-element.54), channel_id=1, source_target_pairs={{0,16},{4,20},{8,24},{12,28},{16,0},{20,4},{24,8},{28,12},{32,48},... | collective-permute-start | bytes 786440 | tf_op jit(solution)/shard_map/ppermute | solution.py:192
  269.0 16.8 %collective-permute-start.5 = (bf16[2,512,128]{2,1,0:T(8,128)(2,1)}, bf16[2,512,128]{2,1,0:T(8,128)(2,1)S(1)}, u32[]{:S(2)}, u32[]{:S(2)}) collective-permute-start(bf16[2,512,128]{2,1,0:T(8,128)(2,1)} %get-tuple-element.52), channel_id=1, source_target_pairs={{0,24},{4,28},{8,0},{12,4},{16,8},{20,12},{24,16},{28,20},{32,56},... | collective-permute-start | bytes 786440 | tf_op jit(solution)/shard_map/ppermute | solution.py:192
  279.7 11.7 %collective-permute-start.6 = (bf16[2,512,128]{2,1,0:T(8,128)(2,1)}, bf16[2,512,128]{2,1,0:T(8,128)(2,1)S(1)}, u32[]{:S(2)}, u32[]{:S(2)}) collective-permute-start(bf16[2,512,128]{2,1,0:T(8,128)(2,1)} %get-tuple-element.51), channel_id=1, source_target_pairs={{0,28},{4,24},{8,4},{12,0},{16,12},{20,8},{24,20},{28,16},{32,60},... | collective-permute-start | bytes 786440 | tf_op jit(solution)/shard_map/ppermute | solution.py:192
  295.4 13.6 %collective-permute-start.9 = (bf16[2,512,128]{2,1,0:T(8,128)(2,1)}, bf16[2,512,128]{2,1,0:T(8,128)(2,1)S(1)}, u32[]{:S(2)}, u32[]{:S(2)}) collective-permute-start(bf16[2,512,128]{2,1,0:T(8,128)(2,1)} %get-tuple-element.48), channel_id=1, source_target_pairs={{0,40},{4,44},{8,48},{12,52},{16,56},{20,60},{24,32},{28,36},{32,7... | collective-permute-start | bytes 786440 | tf_op jit(solution)/shard_map/ppermute | solution.py:192
  301.2 12.8 %collective-permute-start.10 = (bf16[2,512,128]{2,1,0:T(8,128)(2,1)}, bf16[2,512,128]{2,1,0:T(8,128)(2,1)S(1)}, u32[]{:S(2)}, u32[]{:S(2)}) collective-permute-start(bf16[2,512,128]{2,1,0:T(8,128)(2,1)} %get-tuple-element.47), channel_id=1, source_target_pairs={{0,44},{4,40},{8,52},{12,48},{16,60},{20,56},{24,36},{28,32},{32,7... | collective-permute-start | bytes 786440 | tf_op jit(solution)/shard_map/ppermute | solution.py:192
  314.0 12.0 %collective-permute-start.12 = (bf16[2,512,128]{2,1,0:T(8,128)(2,1)}, bf16[2,512,128]{2,1,0:T(8,128)(2,1)S(1)}, u32[]{:S(2)}, u32[]{:S(2)}) collective-permute-start(bf16[2,512,128]{2,1,0:T(8,128)(2,1)} %get-tuple-element.45), channel_id=1, source_target_pairs={{0,52},{4,48},{8,60},{12,56},{16,36},{20,32},{24,44},{28,40},{32,8... | collective-permute-start | bytes 786440 | tf_op jit(solution)/shard_map/ppermute | solution.py:192
  320.5 12.1 %collective-permute-start.13 = (bf16[2,512,128]{2,1,0:T(8,128)(2,1)}, bf16[2,512,128]{2,1,0:T(8,128)(2,1)S(1)}, u32[]{:S(2)}, u32[]{:S(2)}) collective-permute-start(bf16[2,512,128]{2,1,0:T(8,128)(2,1)} %get-tuple-element.44), channel_id=1, source_target_pairs={{0,56},{4,60},{8,32},{12,36},{16,40},{20,44},{24,48},{28,52},{32,8... | collective-permute-start | bytes 786440 | tf_op jit(solution)/shard_map/ppermute | solution.py:192
  326.0 16.2 %collective-permute-start.14 = (bf16[2,512,128]{2,1,0:T(8,128)(2,1)}, bf16[2,512,128]{2,1,0:T(8,128)(2,1)S(1)}, u32[]{:S(2)}, u32[]{:S(2)}) collective-permute-start(bf16[2,512,128]{2,1,0:T(8,128)(2,1)} %get-tuple-element.43), channel_id=1, source_target_pairs={{0,60},{4,56},{8,36},{12,32},{16,44},{20,40},{24,52},{28,48},{32,9... | collective-permute-start | bytes 786440 | tf_op jit(solution)/shard_map/ppermute | solution.py:192
  343.0 16.4 %collective-permute-start.17 = (bf16[2,512,128]{2,1,0:T(8,128)(2,1)}, bf16[2,512,128]{2,1,0:T(8,128)(2,1)S(1)}, u32[]{:S(2)}, u32[]{:S(2)}) collective-permute-start(bf16[2,512,128]{2,1,0:T(8,128)(2,1)} %get-tuple-element.40), channel_id=1, source_target_pairs={{0,72},{4,76},{8,80},{12,84},{16,88},{20,92},{24,64},{28,68},{32,1... | collective-permute-start | bytes 786440 | tf_op jit(solution)/shard_map/ppermute | solution.py:192
  351.7 11.5 %collective-permute-start.18 = (bf16[2,512,128]{2,1,0:T(8,128)(2,1)S(1)}, bf16[2,512,128]{2,1,0:T(8,128)(2,1)S(1)}, u32[]{:S(2)}, u32[]{:S(2)}) collective-permute-start(bf16[2,512,128]{2,1,0:T(8,128)(2,1)S(1)} %copy-done.14), channel_id=1, source_target_pairs={{0,76},{4,72},{8,84},{12,80},{16,92},{20,88},{24,68},{28,64},{32,1... | collective-permute-start | bytes 786440 | tf_op jit(solution)/shard_map/ppermute | solution.py:192
  359.4 12.1 %collective-permute-start.19 = (bf16[2,512,128]{2,1,0:T(8,128)(2,1)S(1)}, bf16[2,512,128]{2,1,0:T(8,128)(2,1)S(1)}, u32[]{:S(2)}, u32[]{:S(2)}) collective-permute-start(bf16[2,512,128]{2,1,0:T(8,128)(2,1)S(1)} %copy-done.13), channel_id=1, source_target_pairs={{0,80},{4,84},{8,88},{12,92},{16,64},{20,68},{24,72},{28,76},{32,1... | collective-permute-start | bytes 786440 | tf_op jit(solution)/shard_map/ppermute | solution.py:192
  363.2 12.6 %collective-permute-start.20 = (bf16[2,512,128]{2,1,0:T(8,128)(2,1)S(1)}, bf16[2,512,128]{2,1,0:T(8,128)(2,1)S(1)}, u32[]{:S(2)}, u32[]{:S(2)}) collective-permute-start(bf16[2,512,128]{2,1,0:T(8,128)(2,1)S(1)} %copy-done.12), channel_id=1, source_target_pairs={{0,84},{4,80},{8,92},{12,88},{16,68},{20,64},{24,76},{28,72},{32,1... | collective-permute-start | bytes 786440 | tf_op jit(solution)/shard_map/ppermute | solution.py:192
  371.5 11.6 %collective-permute-start.21 = (bf16[2,512,128]{2,1,0:T(8,128)(2,1)S(1)}, bf16[2,512,128]{2,1,0:T(8,128)(2,1)S(1)}, u32[]{:S(2)}, u32[]{:S(2)}) collective-permute-start(bf16[2,512,128]{2,1,0:T(8,128)(2,1)S(1)} %copy-done.11), channel_id=1, source_target_pairs={{0,88},{4,92},{8,64},{12,68},{16,72},{20,76},{24,80},{28,84},{32,1... | collective-permute-start | bytes 786440 | tf_op jit(solution)/shard_map/ppermute | solution.py:192
  390.0 12.7 %collective-permute-start.25 = (bf16[2,512,128]{2,1,0:T(8,128)(2,1)S(1)}, bf16[2,512,128]{2,1,0:T(8,128)(2,1)S(1)}, u32[]{:S(2)}, u32[]{:S(2)}) collective-permute-start(bf16[2,512,128]{2,1,0:T(8,128)(2,1)S(1)} %copy-done.7), channel_id=1, source_target_pairs={{0,104},{4,108},{8,112},{12,116},{16,120},{20,124},{24,96},{28,100... | collective-permute-start | bytes 786440 | tf_op jit(solution)/shard_map/ppermute | solution.py:192
  402.7 11.8 %collective-permute-start.27 = (bf16[2,512,128]{2,1,0:T(8,128)(2,1)S(1)}, bf16[2,512,128]{2,1,0:T(8,128)(2,1)S(1)}, u32[]{:S(2)}, u32[]{:S(2)}) collective-permute-start(bf16[2,512,128]{2,1,0:T(8,128)(2,1)S(1)} %get-tuple-element.30), channel_id=1, source_target_pairs={{0,112},{4,116},{8,120},{12,124},{16,96},{20,100},{24,104},{28,108... | collective-permute-start | bytes 786440 | tf_op jit(solution)/shard_map/ppermute | solution.py:192
  (25 other events, 2483.2 us)
Sparse Core Ops, SparseCore 0:
  9.0 49.6 all-gather.1

commit v5 on v3

--- a/solution.py
+++ b/solution.py
@@ -115,7 +115,7 @@
 
 
 def attend_chunk(tab, remap, query_t, recv, m, l, acc):
-    owners = recv.shape[0]
+    owners = tab.shape[0]
     nq, hd, rows = query_t.shape
     plen = recv.shape[2]
     full3 = lambda shape: pl.BlockSpec(shape, lambda o, t, r: (0, 0, 0))
@@ -238,7 +238,10 @@
         hit = hits[c]
         valid = jnp.sum(hit, axis=0)
         tab = jnp.sum(hit * qidx[:, None], axis=0) + valid - 1
-        remap = lax.cummax(jnp.where(valid > 0, slots, 0), axis=0)
+        steps = owners_count if c == 0 else min(owners_count, listed // CAP)
+        order = jnp.argsort(1 - valid, stable=True).astype(jnp.int32)[:steps]
+        tab = tab[order]
+        remap = lax.cummax(jnp.where(tab >= 0, order, 0), axis=0)
         m, l, acc = attend_chunk(tab, remap, query_t, recvs[c], m, l, acc)
 
     ctx = (acc / l).reshape(count, HD, q_heads, QLEN)

time: 325 us -> 318 us (0.978)
  Pallas kernels: 62.7 us -> 52.2 us
  other arithmetic: 6.02 us -> 10.5 us
  local copies, waits for them, and re-layouts: 10.3 us -> 14.5 us
    pallas_call x2, Pallas kernels: 47.7 us -> 37.2 us  [attend_chunk(): pl.pallas_call(block_kernel, grid_spec=grid_spec, out_shape=[jax.ShapeDty...]
  transfers between devices with their start and end apart: 4 -> 4, of which waited for: 3 -> 3; matrix products, arithmetic and copies ran while one was open for 6% -> 9% of each run, Pallas kernels for 12% -> 11%
where the time goes in v5:
time: 318 us; the launch traced here: 315 us
  waiting for transfers between devices  191 us (60%)
  Pallas kernels  52.2 us (16%)
  starting transfers between devices  20 us (6%)
  local copies, waits for them, and re-layouts  14.5 us (5%)
  matrix products  13.7 us (4%)
  between operations  13.7 us (4%)
  other arithmetic  10.5 us (3%)
    all_to_all x2, waiting for transfers between devices, per_device(): lax.all_to_all(s, 'store', split_axis=0, concat_axis=0, tiled=True)  184 us
    pallas_call x2, Pallas kernels, attend_chunk(): pl.pallas_call(block_kernel, grid_spec=grid_spec, out_shape=[jax.ShapeDty...  37.2 us
    pallas_call x2, Pallas kernels, build_send(): pl.pallas_call(send_kernel, grid_spec=grid_spec, out_shape=jax.ShapeDtype...  15 us
    all_to_all x2, starting transfers between devices, per_device(): lax.all_to_all(s, 'store', split_axis=0, concat_axis=0, tiled=True)  12.4 us
    dot_general x1, matrix products, per_device(): qf = jnp.dot(piece, w_query, preferred_element_type=jnp.float32)  9.44 us
    all_to_all x1, starting transfers between devices, per_device(): lax.all_to_all(request, 'store', split_axis=0, concat_axis=0, tiled=True)  7.54 us
  transfers between devices with their start and end apart: 4, of which 3 were waited for; matrix products, arithmetic and copies ran while one was open for 9% of the time, Pallas kernels for 11%

profile of v5, /device:TPU:40, one launch (start us, length us, event | category | flops | bytes accessed | tf_op | source)
XLA Modules:
  0.0 315.4 jit_solution(16350723599031350503)
XLA Ops:
  6.5 0.9 reshape.220
  9.4 7.5 %all-to-all-start = ((s32[32,2,2]{2,1,0:T(2,128)}), s32[32,2,2]{2,1,0:T(2,128)S(1)}, u32[]{:S(2)}, u32[]{:S(2)}) async-start(s32[32,2,2]{2,1,0:T(2,128)} %copy.44), calls=%async_computation | async-start | bytes 65536 | tf_op jit(solution)/shard_map/all_to_all | solution.py:189
  17.0 6.2 %all-to-all-done = s32[32,2,2]{2,1,0:T(2,128)S(1)} async-done(((s32[32,2,2]{2,1,0:T(2,128)}), s32[32,2,2]{2,1,0:T(2,128)S(1)}, u32[]{:S(2)}, u32[]{:S(2)}) %all-to-all-start) | async-done | bytes 544 | tf_op jit(solution)/shard_map/all_to_all | solution.py:189
  25.6 1.8 slice_reduce_fusion
  27.3 7.5 %shard_map.83 = bf16[32,2,512,128]{3,2,1,0:T(8,128)(2,1)} custom-call(s32[32]{0:T(128)} %get-tuple-element.21.loc_ref, bf16[4,512,128]{2,1,0:T(8,128)(2,1)} %k_ref.3, bf16[4,512,128]{2,1,0:T(8,128)(2,1)} %v_ref.3, f32[32,128]{1,0:T(8,128)} %pad_maximum_fusion.3.c_ref, f32[32,128]{1,0:T(8,128)} %pad_maximum_fusion.4.s_ref), custom_call_target="tpu_custom_call" | custom-call | flops 8388608 | bytes 9437184 | tf_op jit(solution)/shard_map/pallas_call | solution.py:65
  34.8 6.0 %all-to-all-start.2 = ((bf16[32,2,512,128]{3,2,1,0:T(8,128)(2,1)}), bf16[32,2,512,128]{3,2,1,0:T(8,128)(2,1)}, u32[]{:S(2)}, u32[]{:S(2)}) async-start(bf16[32,2,512,128]{3,2,1,0:T(8,128)(2,1)} %shard_map.83), calls=%async_computation.2 | async-start | bytes 16777216 | tf_op jit(solution)/shard_map/all_to_all | solution.py:201
  42.9 7.5 %shard_map.82 = bf16[32,2,512,128]{3,2,1,0:T(8,128)(2,1)} custom-call(s32[32]{0:T(128)} %get-tuple-element.22.loc_ref, bf16[4,512,128]{2,1,0:T(8,128)(2,1)} %k_ref.3, bf16[4,512,128]{2,1,0:T(8,128)(2,1)} %v_ref.3, f32[32,128]{1,0:T(8,128)} %pad_maximum_fusion.1.c_ref, f32[32,128]{1,0:T(8,128)} %pad_maximum_fusion.2.s_ref), custom_call_target="tpu_custom_call" | custom-call | flops 8388608 | bytes 9437184 | tf_op jit(solution)/shard_map/pallas_call | solution.py:65
  50.4 114.4 %all-to-all-done.2.kv_ref = bf16[32,2,512,128]{3,2,1,0:T(8,128)(2,1)} async-done(((bf16[32,2,512,128]{3,2,1,0:T(8,128)(2,1)}), bf16[32,2,512,128]{3,2,1,0:T(8,128)(2,1)}, u32[]{:S(2)}, u32[]{:S(2)}) %all-to-all-start.2) | async-done | bytes 8388640 | tf_op jit(solution)/shard_map/all_to_all | solution.py:201
  164.8 6.4 %all-to-all-start.1 = ((bf16[32,2,512,128]{3,2,1,0:T(8,128)(2,1)}), bf16[32,2,512,128]{3,2,1,0:T(8,128)(2,1)}, u32[]{:S(2)}, u32[]{:S(2)}) async-start(bf16[32,2,512,128]{3,2,1,0:T(8,128)(2,1)} %shard_map.82), calls=%async_computation.1 | async-start | bytes 16777216 | tf_op jit(solution)/shard_map/all_to_all | solution.py:201
  171.2 1.6 sort.32
  173.8 1.6 sort.31
  176.7 9.4 %convolution_bitcast_fusion = f32[32,8,8,128]{3,1,2,0:T(8,128)S(1)} fusion(bf16[256,8192]{1,0:T(8,128)(2,1)} %all-gather.2.cloned.1.call-done, bf16[8192,1024]{1,0:T(8,128)(2,1)} %param.9), kind=kOutput, calls=%fused_computation.2 | convolution fusion | flops 4294967296 | bytes 22020096 | tf_op jit(solution)/shard_map/dot_general | solution.py:205
  187.5 1.1 copy-done.3
  188.6 1.3 fusion.32
  190.4 1.2 convolution_convert_fusion
  191.6 1.4 fusion.3
  193.0 1.6 copy.53.a_in
  194.5 2.0 copy.52.q_ref
  196.6 1.4 fusion.2
  198.0 1.0 copy-done.1
  199.0 26.9 %shard_map.84 = (f32[2,1,1024]{2,1,0:T(1,128)S(1)}, f32[2,1,1024]{2,1,0:T(1,128)S(1)}, f32[2,128,1024]{2,1,0:T(8,128)S(1)}) custom-call(s32[32]{0:T(128)S(1)} %gather_fusion.1, s32[32]{0:T(128)S(1)} %reduce.3.remap_ref, bf16[2,128,1024]{2,1,0:T(8,128)(2,1)S(1)} %copy-done.1, ...), custom_call_target="tpu_custom_call", output_to_operand_aliasing={{0}: (4, {}), {1}: (5, {}), {2}: (6, {})} | custom-call | flops 8589934592 | bytes 10485760 | tf_op jit(solution)/shard_map/pallas_call | solution.py:135
  226.0 69.7 %all-to-all-done.1.kv_ref = bf16[32,2,512,128]{3,2,1,0:T(8,128)(2,1)} async-done(((bf16[32,2,512,128]{3,2,1,0:T(8,128)(2,1)}), bf16[32,2,512,128]{3,2,1,0:T(8,128)(2,1)}, u32[]{:S(2)}, u32[]{:S(2)}) %all-to-all-start.1) | async-done | bytes 8388640 | tf_op jit(solution)/shard_map/all_to_all | solution.py:201
  295.6 1.0 copy-done.2
  296.7 10.2 %shard_map.85 = (f32[2,1,1024]{2,1,0:T(1,128)S(1)}, f32[2,1,1024]{2,1,0:T(1,128)S(1)}, f32[2,128,1024]{2,1,0:T(8,128)S(1)}) custom-call(s32[16]{0:T(128)S(1)} %gather_fusion, s32[16]{0:T(128)S(1)} %reduce.remap_ref, bf16[2,128,1024]{2,1,0:T(8,128)(2,1)S(1)} %copy-done.2, ...), custom_call_target="tpu_custom_call", output_to_operand_aliasing={{0}: (4, {}), {1}: (5, {}), {2}: (6, {})} | custom-call | flops 4294967296 | bytes 10485760 | tf_op jit(solution)/shard_map/pallas_call | solution.py:135
  (64 shorter events, 12.0 us)
Async XLA Ops:
  6.5 180.9 %copy-start = (bf16[8192,128]{1,0:T(8,128)(2,1)S(1)}, bf16[8192,128]{1,0:T(8,128)(2,1)}, u32[]{:S(2)}) copy-start(bf16[8192,128]{1,0:T(8,128)(2,1)} %param.10) | copy-start | bytes 6291460
  9.4 13.8 %all-to-all-start = ((s32[32,2,2]{2,1,0:T(2,128)}), s32[32,2,2]{2,1,0:T(2,128)S(1)}, u32[]{:S(2)}, u32[]{:S(2)}) async-start(s32[32,2,2]{2,1,0:T(2,128)} %copy.44), calls=%async_computation | async-start | bytes 65536 | tf_op jit(solution)/shard_map/all_to_all | solution.py:189
  34.8 130.0 %all-to-all-start.2 = ((bf16[32,2,512,128]{3,2,1,0:T(8,128)(2,1)}), bf16[32,2,512,128]{3,2,1,0:T(8,128)(2,1)}, u32[]{:S(2)}, u32[]{:S(2)}) async-start(bf16[32,2,512,128]{3,2,1,0:T(8,128)(2,1)} %shard_map.83), calls=%async_computation.2 | async-start | bytes 16777216 | tf_op jit(solution)/shard_map/all_to_all | solution.py:201
  40.8 135.9 %all-gather.2.cloned.1.call-start = ((), (), s32[]{:S(2)}) async-start(), calls=%async_computation.3 | async-start | bytes 5242880 | tf_op jit(solution)/shard_map/all_gather | solution.py:204
  164.8 130.8 %all-to-all-start.1 = ((bf16[32,2,512,128]{3,2,1,0:T(8,128)(2,1)}), bf16[32,2,512,128]{3,2,1,0:T(8,128)(2,1)}, u32[]{:S(2)}, u32[]{:S(2)}) async-start(bf16[32,2,512,128]{3,2,1,0:T(8,128)(2,1)} %shard_map.82), calls=%async_computation.1 | async-start | bytes 16777216 | tf_op jit(solution)/shard_map/all_to_all | solution.py:201
  186.4 2.2 copy-start.3
  188.6 1.8 copy-start.5
  188.6 1.8 copy-start.6
  190.4 2.6 copy-start.4
  198.0 1.0 copy-start.1
  295.6 1.0 copy-start.2
Sparse Core Ops, SparseCore 0:
  43.3 49.5 all-gather.1

commit v6 on v5

--- a/solution.py
+++ b/solution.py
@@ -78,7 +78,7 @@
 LOG2E = 1.4426950408889634
 
 
-def block_kernel(tab_ref, remap_ref, q_ref, kv_ref, m_in, l_in, a_in, m_ref, l_ref, a_ref):
+def block_kernel(tab_ref, remap_ref, q_ref, kv0_ref, kv1_ref, m_in, l_in, a_in, m_ref, l_ref, a_ref):
     o = pl.program_id(0)
 
     @pl.when(o == 0)
@@ -87,35 +87,36 @@
         l_ref[...] = l_in[...]
         a_ref[...] = a_in[...]
 
-    qi = tab_ref[o]
-
-    @pl.when(qi >= 0)
-    def _():
-        k = kv_ref[0, 0]
-        v = kv_ref[0, 1]
-        c = (HD ** (-0.5)) * LOG2E
-        for r0 in range(0, q_ref.shape[2], ROW_TILE):
-            cols = pl.ds(r0, ROW_TILE)
-            s = jnp.dot(k, q_ref[qi, :, cols], preferred_element_type=jnp.float32)
-            m = jnp.max(s, axis=0, keepdims=True)
-            e = jnp.exp2(s * c - m * c)
-            l = jnp.sum(e, axis=0, keepdims=True)
-            p = lax.dot_general(
-                v, e.astype(jnp.bfloat16), (((0,), (0,)), ((), ())),
-                preferred_element_type=jnp.float32,
-            )
-            m = m * (HD ** (-0.5))
-            m_old = m_ref[qi, :, cols]
-            m_new = jnp.maximum(m_old, m)
-            w_old = jnp.exp(m_old - m_new)
-            w_new = jnp.exp(m - m_new)
-            l_ref[qi, :, cols] = w_old * l_ref[qi, :, cols] + w_new * l
-            a_ref[qi, :, cols] = w_old * a_ref[qi, :, cols] + w_new * p
-            m_ref[qi, :, cols] = m_new
+    c = (HD ** (-0.5)) * LOG2E
+    for j, kv_ref in enumerate((kv0_ref, kv1_ref)):
+        qi = tab_ref[2 * o + j]
+
+        @pl.when(qi >= 0)
+        def _():
+            k = kv_ref[0, 0]
+            v = kv_ref[0, 1]
+            for r0 in range(0, q_ref.shape[2], ROW_TILE):
+                cols = pl.ds(r0, ROW_TILE)
+                s = jnp.dot(k, q_ref[qi, :, cols], preferred_element_type=jnp.float32)
+                m = jnp.max(s, axis=0, keepdims=True)
+                e = jnp.exp2(s * c - m * c)
+                l = jnp.sum(e, axis=0, keepdims=True)
+                p = lax.dot_general(
+                    v, e.astype(jnp.bfloat16), (((0,), (0,)), ((), ())),
+                    preferred_element_type=jnp.float32,
+                )
+                m = m * (HD ** (-0.5))
+                m_old = m_ref[qi, :, cols]
+                m_new = jnp.maximum(m_old, m)
+                w_old = jnp.exp(m_old - m_new)
+                w_new = jnp.exp(m - m_new)
+                l_ref[qi, :, cols] = w_old * l_ref[qi, :, cols] + w_new * l
+                a_ref[qi, :, cols] = w_old * a_ref[qi, :, cols] + w_new * p
+                m_ref[qi, :, cols] = m_new
 
 
 def attend_chunk(tab, remap, query_t, recv, m, l, acc):
-    owners = tab.shape[0]
+    owners = tab.shape[0] // 2
     nq, hd, rows = query_t.shape
     plen = recv.shape[2]
     full3 = lambda shape: pl.BlockSpec(shape, lambda o, t, r: (0, 0, 0))
@@ -124,14 +125,15 @@
         grid=(owners,),
         in_specs=[
             full3((nq, hd, rows)),
-            pl.BlockSpec((1, 2, plen, hd), lambda o, t, r: (r[o], 0, 0, 0)),
+            pl.BlockSpec((1, 2, plen, hd), lambda o, t, r: (r[2 * o], 0, 0, 0)),
+            pl.BlockSpec((1, 2, plen, hd), lambda o, t, r: (r[2 * o + 1], 0, 0, 0)),
             full3((nq, 1, rows)),
             full3((nq, 1, rows)),
             full3((nq, hd, rows)),
         ],
         out_specs=[full3((nq, 1, rows)), full3((nq, 1, rows)), full3((nq, hd, rows))],
     )
-    flops = 4 * nq * rows * plen * hd * owners // 2
+    flops = 4 * nq * rows * plen * hd * owners
     return pl.pallas_call(
         block_kernel,
         grid_spec=grid_spec,
@@ -140,16 +142,16 @@
             jax.ShapeDtypeStruct(l.shape, jnp.float32),
             jax.ShapeDtypeStruct(acc.shape, jnp.float32),
         ],
-        input_output_aliases={4: 0, 5: 1, 6: 2},
+        input_output_aliases={5: 0, 6: 1, 7: 2},
         compiler_params=pltpu.CompilerParams(
             dimension_semantics=("arbitrary",), vmem_limit_bytes=48 * 1024 * 1024
         ),
         cost_estimate=pl.CostEstimate(
             flops=flops,
-            transcendentals=nq * rows * plen * owners // 2,
+            transcendentals=nq * rows * plen * owners,
             bytes_accessed=recv.size * 2 + 2 * acc.size * 4,
         ),
-    )(tab, remap, query_t, recv, m, l, acc)
+    )(tab, remap, query_t, recv, recv, m, l, acc)
 
 
 def per_device(

time: 318 us -> 318 us (level)
  transfers between devices with their start and end apart: 4 -> 4, of which waited for: 3 -> 3; matrix products, arithmetic and copies ran while one was open for 9% -> 8% of each run, Pallas kernels for 11% -> 10%
where the time goes in v6:
time: 318 us
  waiting for transfers between devices  194 us (61%)
  Pallas kernels  52.1 us (16%)
  starting transfers between devices  20 us (6%)
  local copies, waits for them, and re-layouts  14.5 us (5%)
  matrix products  13.7 us (4%)
  between operations  13.7 us (4%)
  other arithmetic  10.5 us (3%)
    all_to_all x2, waiting for transfers between devices, per_device(): lax.all_to_all(s, 'store', split_axis=0, concat_axis=0, tiled=True)  187 us
    pallas_call x2, Pallas kernels, attend_chunk(): pl.pallas_call(block_kernel, grid_spec=grid_spec, out_shape=[jax.ShapeDty...  37.1 us
    pallas_call x2, Pallas kernels, build_send(): pl.pallas_call(send_kernel, grid_spec=grid_spec, out_shape=jax.ShapeDtype...  15 us
    all_to_all x2, starting transfers between devices, per_device(): lax.all_to_all(s, 'store', split_axis=0, concat_axis=0, tiled=True)  12.4 us
    dot_general x1, matrix products, per_device(): qf = jnp.dot(piece, w_query, preferred_element_type=jnp.float32)  9.44 us
    all_to_all x1, starting transfers between devices, per_device(): lax.all_to_all(request, 'store', split_axis=0, concat_axis=0, tiled=True)  7.54 us
  transfers between devices with their start and end apart: 4, of which 3 were waited for; matrix products, arithmetic and copies ran while one was open for 8% of the time, Pallas kernels for 10%

profile of v6, /device:TPU:40, one launch (start us, length us, event | category | flops | bytes accessed | tf_op | source)
XLA Modules:
  0.0 318.4 jit_solution(17462805866261214511)
XLA Ops:
  6.5 0.9 reshape.220
  9.4 7.5 %all-to-all-start = ((s32[32,2,2]{2,1,0:T(2,128)}), s32[32,2,2]{2,1,0:T(2,128)S(1)}, u32[]{:S(2)}, u32[]{:S(2)}) async-start(s32[32,2,2]{2,1,0:T(2,128)} %copy.44), calls=%async_computation | async-start | bytes 65536 | tf_op jit(solution)/shard_map/all_to_all | solution.py:191
  17.0 6.2 %all-to-all-done = s32[32,2,2]{2,1,0:T(2,128)S(1)} async-done(((s32[32,2,2]{2,1,0:T(2,128)}), s32[32,2,2]{2,1,0:T(2,128)S(1)}, u32[]{:S(2)}, u32[]{:S(2)}) %all-to-all-start) | async-done | bytes 544 | tf_op jit(solution)/shard_map/all_to_all | solution.py:191
  25.6 1.8 slice_reduce_fusion
  27.3 7.5 %shard_map.83 = bf16[32,2,512,128]{3,2,1,0:T(8,128)(2,1)} custom-call(s32[32]{0:T(128)} %get-tuple-element.21.loc_ref, bf16[4,512,128]{2,1,0:T(8,128)(2,1)} %k_ref.3, bf16[4,512,128]{2,1,0:T(8,128)(2,1)} %v_ref.3, f32[32,128]{1,0:T(8,128)} %pad_maximum_fusion.3.c_ref, f32[32,128]{1,0:T(8,128)} %pad_maximum_fusion.4.s_ref), custom_call_target="tpu_custom_call" | custom-call | flops 8388608 | bytes 9437184 | tf_op jit(solution)/shard_map/pallas_call | solution.py:65
  34.8 6.0 %all-to-all-start.2 = ((bf16[32,2,512,128]{3,2,1,0:T(8,128)(2,1)}), bf16[32,2,512,128]{3,2,1,0:T(8,128)(2,1)}, u32[]{:S(2)}, u32[]{:S(2)}) async-start(bf16[32,2,512,128]{3,2,1,0:T(8,128)(2,1)} %shard_map.83), calls=%async_computation.2 | async-start | bytes 16777216 | tf_op jit(solution)/shard_map/all_to_all | solution.py:203
  42.9 7.5 %shard_map.82 = bf16[32,2,512,128]{3,2,1,0:T(8,128)(2,1)} custom-call(s32[32]{0:T(128)} %get-tuple-element.22.loc_ref, bf16[4,512,128]{2,1,0:T(8,128)(2,1)} %k_ref.3, bf16[4,512,128]{2,1,0:T(8,128)(2,1)} %v_ref.3, f32[32,128]{1,0:T(8,128)} %pad_maximum_fusion.1.c_ref, f32[32,128]{1,0:T(8,128)} %pad_maximum_fusion.2.s_ref), custom_call_target="tpu_custom_call" | custom-call | flops 8388608 | bytes 9437184 | tf_op jit(solution)/shard_map/pallas_call | solution.py:65
  50.4 114.4 %all-to-all-done.2.kv0_ref.kv1_ref = bf16[32,2,512,128]{3,2,1,0:T(8,128)(2,1)} async-done(((bf16[32,2,512,128]{3,2,1,0:T(8,128)(2,1)}), bf16[32,2,512,128]{3,2,1,0:T(8,128)(2,1)}, u32[]{:S(2)}, u32[]{:S(2)}) %all-to-all-start.2) | async-done | bytes 8388640 | tf_op jit(solution)/shard_map/all_to_all | solution.py:203
  164.8 6.4 %all-to-all-start.1 = ((bf16[32,2,512,128]{3,2,1,0:T(8,128)(2,1)}), bf16[32,2,512,128]{3,2,1,0:T(8,128)(2,1)}, u32[]{:S(2)}, u32[]{:S(2)}) async-start(bf16[32,2,512,128]{3,2,1,0:T(8,128)(2,1)} %shard_map.82), calls=%async_computation.1 | async-start | bytes 16777216 | tf_op jit(solution)/shard_map/all_to_all | solution.py:203
  171.2 1.6 sort.32
  173.8 1.6 sort.31
  176.7 9.4 %convolution_bitcast_fusion = f32[32,8,8,128]{3,1,2,0:T(8,128)S(1)} fusion(bf16[256,8192]{1,0:T(8,128)(2,1)} %all-gather.2.cloned.1.call-done, bf16[8192,1024]{1,0:T(8,128)(2,1)} %param.9), kind=kOutput, calls=%fused_computation.2 | convolution fusion | flops 4294967296 | bytes 22020096 | tf_op jit(solution)/shard_map/dot_general | solution.py:207
  187.5 1.1 copy-done.3
  188.6 1.3 fusion.32
  190.4 1.2 convolution_convert_fusion
  191.6 1.4 fusion.3
  193.0 1.6 copy.53.a_in
  194.5 2.0 copy.52.q_ref
  196.6 1.4 fusion.2
  198.0 1.0 copy-done.1
  199.0 23.8 %shard_map.84 = (f32[2,1,1024]{2,1,0:T(1,128)S(1)}, f32[2,1,1024]{2,1,0:T(1,128)S(1)}, f32[2,128,1024]{2,1,0:T(8,128)S(1)}) custom-call(s32[32]{0:T(128)S(1)} %gather_fusion.1, s32[32]{0:T(128)S(1)} %reduce.3.remap_ref, bf16[2,128,1024]{2,1,0:T(8,128)(2,1)S(1)} %copy-done.1, ...), custom_call_target="tpu_custom_call", output_to_operand_aliasing={{0}: (5, {}), {1}: (6, {}), {2}: (7, {})} | custom-call | flops 8589934592 | bytes 10485760 | tf_op jit(solution)/shard_map/pallas_call | solution.py:137
  222.9 72.8 %all-to-all-done.1.kv0_ref.kv1_ref = bf16[32,2,512,128]{3,2,1,0:T(8,128)(2,1)} async-done(((bf16[32,2,512,128]{3,2,1,0:T(8,128)(2,1)}), bf16[32,2,512,128]{3,2,1,0:T(8,128)(2,1)}, u32[]{:S(2)}, u32[]{:S(2)}) %all-to-all-start.1) | async-done | bytes 8388640 | tf_op jit(solution)/shard_map/all_to_all | solution.py:203
  295.6 1.0 copy-done.2
  296.7 13.3 %shard_map.85 = (f32[2,1,1024]{2,1,0:T(1,128)S(1)}, f32[2,1,1024]{2,1,0:T(1,128)S(1)}, f32[2,128,1024]{2,1,0:T(8,128)S(1)}) custom-call(s32[16]{0:T(128)S(1)} %gather_fusion, s32[16]{0:T(128)S(1)} %reduce.remap_ref, bf16[2,128,1024]{2,1,0:T(8,128)(2,1)S(1)} %copy-done.2, ...), custom_call_target="tpu_custom_call", output_to_operand_aliasing={{0}: (5, {}), {1}: (6, {}), {2}: (7, {})} | custom-call | flops 4294967296 | bytes 10485760 | tf_op jit(solution)/shard_map/pallas_call | solution.py:137
  (64 shorter events, 12.0 us)
Async XLA Ops:
  6.5 180.9 %copy-start = (bf16[8192,128]{1,0:T(8,128)(2,1)S(1)}, bf16[8192,128]{1,0:T(8,128)(2,1)}, u32[]{:S(2)}) copy-start(bf16[8192,128]{1,0:T(8,128)(2,1)} %param.10) | copy-start | bytes 6291460
  9.4 13.8 %all-to-all-start = ((s32[32,2,2]{2,1,0:T(2,128)}), s32[32,2,2]{2,1,0:T(2,128)S(1)}, u32[]{:S(2)}, u32[]{:S(2)}) async-start(s32[32,2,2]{2,1,0:T(2,128)} %copy.44), calls=%async_computation | async-start | bytes 65536 | tf_op jit(solution)/shard_map/all_to_all | solution.py:191
  34.8 130.0 %all-to-all-start.2 = ((bf16[32,2,512,128]{3,2,1,0:T(8,128)(2,1)}), bf16[32,2,512,128]{3,2,1,0:T(8,128)(2,1)}, u32[]{:S(2)}, u32[]{:S(2)}) async-start(bf16[32,2,512,128]{3,2,1,0:T(8,128)(2,1)} %shard_map.83), calls=%async_computation.2 | async-start | bytes 16777216 | tf_op jit(solution)/shard_map/all_to_all | solution.py:203
  40.8 135.9 %all-gather.2.cloned.1.call-start = ((), (), s32[]{:S(2)}) async-start(), calls=%async_computation.3 | async-start | bytes 5242880 | tf_op jit(solution)/shard_map/all_gather | solution.py:206
  164.8 130.8 %all-to-all-start.1 = ((bf16[32,2,512,128]{3,2,1,0:T(8,128)(2,1)}), bf16[32,2,512,128]{3,2,1,0:T(8,128)(2,1)}, u32[]{:S(2)}, u32[]{:S(2)}) async-start(bf16[32,2,512,128]{3,2,1,0:T(8,128)(2,1)} %shard_map.82), calls=%async_computation.1 | async-start | bytes 16777216 | tf_op jit(solution)/shard_map/all_to_all | solution.py:203
  186.4 2.2 copy-start.3
  188.6 1.8 copy-start.5
  188.6 1.8 copy-start.6
  190.4 2.6 copy-start.4
  198.0 1.0 copy-start.1
  295.6 1.0 copy-start.2
Sparse Core Ops, SparseCore 0:
  43.3 49.5 all-gather.1

commit v7 on v6

--- a/solution.py
+++ b/solution.py
@@ -203,7 +203,18 @@
         lax.all_to_all(s, "store", split_axis=0, concat_axis=0, tiled=True) for s in sends
     ]
 
-    piece = lax.all_gather(questions, "tensor", axis=1, tiled=True)
+    parts = lax.axis_size("tensor")
+    zi = lax.axis_index("tensor")
+    got = [questions] + [
+        lax.ppermute(questions, "tensor", [(i, (i + sh) % parts) for i in range(parts)])
+        for sh in range(1, parts)
+    ]
+    got = jnp.stack(got)
+    order = (zi - jnp.arange(parts, dtype=jnp.int32)) % parts
+    piece = jnp.concatenate(
+        [lax.dynamic_index_in_dim(got, order[j], 0, keepdims=False) for j in range(parts)],
+        axis=1,
+    )
     qf = jnp.dot(piece, w_query, preferred_element_type=jnp.float32)
     kf = jnp.dot(piece, w_key, preferred_element_type=jnp.float32)
     vf = jnp.dot(piece, w_value, preferred_element_type=jnp.float32)

time: 318 us -> 304 us (0.956)
  waiting for transfers between devices: 194 us -> 174 us
  starting transfers between devices: 20 us -> 25.7 us
  between operations: 13.7 us -> 8.05 us
    all_to_all x2, waiting for transfers between devices: 187 us -> 168 us  [per_device(): lax.all_to_all(s, 'store', split_axis=0, concat_axis=0, tiled=True)]
    ppermute x0 -> x3, starting transfers between devices: none -> 5.68 us  [per_device(): lax.ppermute(questions, 'tensor', [(i, (i + sh) % parts) for i in range(p...]
  transfers between devices with their start and end apart: 4 -> 6, of which waited for: 3 -> 3; matrix products, arithmetic and copies ran while one was open for 8% -> 10% of each run, Pallas kernels for 10% -> 11%
where the time goes in v7:
time: 304 us; the launch traced here: 302 us
  waiting for transfers between devices  174 us (57%)
  Pallas kernels  52.3 us (17%)
  starting transfers between devices  25.7 us (8%)
  matrix products  15 us (5%)
  local copies, waits for them, and re-layouts  14.4 us (5%)
  other arithmetic  12.6 us (4%)
  between operations  8.05 us (3%)
    all_to_all x2, waiting for transfers between devices, per_device(): lax.all_to_all(s, 'store', split_axis=0, concat_axis=0, tiled=True)  168 us
    pallas_call x2, Pallas kernels, attend_chunk(): pl.pallas_call(block_kernel, grid_spec=grid_spec, out_shape=[jax.ShapeDty...  37.3 us
    pallas_call x2, Pallas kernels, build_send(): pl.pallas_call(send_kernel, grid_spec=grid_spec, out_shape=jax.ShapeDtype...  15 us
    all_to_all x2, starting transfers between devices, per_device(): lax.all_to_all(s, 'store', split_axis=0, concat_axis=0, tiled=True)  12.5 us
    dot_general x1, matrix products, per_device(): qf = jnp.dot(piece, w_query, preferred_element_type=jnp.float32)  10.4 us
    all_to_all x1, starting transfers between devices, per_device(): lax.all_to_all(request, 'store', split_axis=0, concat_axis=0, tiled=True)  7.54 us
    all_to_all x1, waiting for transfers between devices, per_device(): lax.all_to_all(request, 'store', split_axis=0, concat_axis=0, tiled=True)  6.19 us
  transfers between devices with their start and end apart: 6, of which 3 were waited for; matrix products, arithmetic and copies ran while one was open for 10% of the time, Pallas kernels for 11%

profile of v7, /device:TPU:40, one launch (start us, length us, event | category | flops | bytes accessed | tf_op | source)
XLA Modules:
  0.0 302.4 jit_solution(16826909973459865505)
XLA Ops:
  2.9 7.5 %all-to-all-start = ((s32[32,2,2]{2,1,0:T(2,128)}), s32[32,2,2]{2,1,0:T(2,128)S(1)}, u32[]{:S(2)}, u32[]{:S(2)}) async-start(s32[32,2,2]{2,1,0:T(2,128)} %copy.44), calls=%async_computation | async-start | bytes 65536 | tf_op jit(solution)/shard_map/all_to_all | solution.py:191
  10.4 6.2 %all-to-all-done = s32[32,2,2]{2,1,0:T(2,128)S(1)} async-done(((s32[32,2,2]{2,1,0:T(2,128)}), s32[32,2,2]{2,1,0:T(2,128)S(1)}, u32[]{:S(2)}, u32[]{:S(2)}) %all-to-all-start) | async-done | bytes 544 | tf_op jit(solution)/shard_map/all_to_all | solution.py:191
  19.0 1.8 slice_reduce_fusion
  20.8 7.5 %shard_map.83 = bf16[32,2,512,128]{3,2,1,0:T(8,128)(2,1)} custom-call(s32[32]{0:T(128)} %get-tuple-element.21.loc_ref, bf16[4,512,128]{2,1,0:T(8,128)(2,1)} %k_ref.3, bf16[4,512,128]{2,1,0:T(8,128)(2,1)} %v_ref.3, f32[32,128]{1,0:T(8,128)} %pad_maximum_fusion.5.c_ref, f32[32,128]{1,0:T(8,128)} %pad_maximum_fusion.6.s_ref), custom_call_target="tpu_custom_call" | custom-call | flops 8388608 | bytes 9437184 | tf_op jit(solution)/shard_map/pallas_call | solution.py:65
  28.3 6.1 %all-to-all-start.2 = ((bf16[32,2,512,128]{3,2,1,0:T(8,128)(2,1)}), bf16[32,2,512,128]{3,2,1,0:T(8,128)(2,1)}, u32[]{:S(2)}, u32[]{:S(2)}) async-start(bf16[32,2,512,128]{3,2,1,0:T(8,128)(2,1)} %shard_map.83), calls=%async_computation.2 | async-start | bytes 16777216 | tf_op jit(solution)/shard_map/all_to_all | solution.py:203
  34.4 2.0 collective-permute-start
  36.4 1.2 collective-permute-start.1
  37.6 2.5 collective-permute-start.2
  41.5 7.5 %shard_map.82 = bf16[32,2,512,128]{3,2,1,0:T(8,128)(2,1)} custom-call(s32[32]{0:T(128)} %get-tuple-element.22.loc_ref, bf16[4,512,128]{2,1,0:T(8,128)(2,1)} %k_ref.3, bf16[4,512,128]{2,1,0:T(8,128)(2,1)} %v_ref.3, f32[32,128]{1,0:T(8,128)} %pad_maximum_fusion.3.c_ref, f32[32,128]{1,0:T(8,128)} %pad_maximum_fusion.4.s_ref), custom_call_target="tpu_custom_call" | custom-call | flops 8388608 | bytes 9437184 | tf_op jit(solution)/shard_map/pallas_call | solution.py:65
  49.0 109.4 %all-to-all-done.2.kv0_ref.kv1_ref = bf16[32,2,512,128]{3,2,1,0:T(8,128)(2,1)} async-done(((bf16[32,2,512,128]{3,2,1,0:T(8,128)(2,1)}), bf16[32,2,512,128]{3,2,1,0:T(8,128)(2,1)}, u32[]{:S(2)}, u32[]{:S(2)}) %all-to-all-start.2) | async-done | bytes 8388640 | tf_op jit(solution)/shard_map/all_to_all | solution.py:203
  158.4 6.4 %all-to-all-start.1 = ((bf16[32,2,512,128]{3,2,1,0:T(8,128)(2,1)}), bf16[32,2,512,128]{3,2,1,0:T(8,128)(2,1)}, u32[]{:S(2)}, u32[]{:S(2)}) async-start(bf16[32,2,512,128]{3,2,1,0:T(8,128)(2,1)} %shard_map.82), calls=%async_computation.1 | async-start | bytes 16777216 | tf_op jit(solution)/shard_map/all_to_all | solution.py:203
  164.8 1.6 sort.32
  173.2 1.6 sort.31
  178.7 2.1 pad_maximum_fusion
  181.1 10.4 %convolution_bitcast_fusion = f32[32,8,8,128]{3,1,2,0:T(8,128)S(1)} fusion(bf16[8192,1024]{1,0:T(8,128)(2,1)} %param.9, bf16[256,2048]{1,0:T(8,128)(2,1)S(1)} %get-tuple-element.32, bf16[256,2048]{1,0:T(8,128)(2,1)S(1)} %get-tuple-element.33, bf16[256,2048]{1,0:T(8,128)(2,1)S(1)} %get-tuple-element.34, bf16[256,2048]{1,0:T(8,128)(2,1)S(1)} %get-tuple-element.31), kind=kOutput, calls=%fused_computation.4 | convolution fusion | flops 4311744512 | bytes 22020096 | tf_op jit(solution)/shard_map/dot_general | solution.py:218
  192.8 1.5 fusion.31
  194.8 1.4 convolution_convert_fusion
  196.3 1.3 fusion.3
  197.6 1.6 copy.53.a_in
  199.2 2.0 copy.52.q_ref
  201.2 1.4 fusion.2
  203.7 26.9 %shard_map.84 = (f32[2,1,1024]{2,1,0:T(1,128)S(1)}, f32[2,1,1024]{2,1,0:T(1,128)S(1)}, f32[2,128,1024]{2,1,0:T(8,128)S(1)}) custom-call(s32[32]{0:T(128)S(1)} %gather_fusion.1, s32[32]{0:T(128)S(1)} %reduce.3.remap_ref, bf16[2,128,1024]{2,1,0:T(8,128)(2,1)S(1)} %copy-done.1, ...), custom_call_target="tpu_custom_call", output_to_operand_aliasing={{0}: (5, {}), {1}: (6, {}), {2}: (7, {})} | custom-call | flops 8589934592 | bytes 10485760 | tf_op jit(solution)/shard_map/pallas_call | solution.py:137
  230.6 58.7 %all-to-all-done.1.kv0_ref.kv1_ref = bf16[32,2,512,128]{3,2,1,0:T(8,128)(2,1)} async-done(((bf16[32,2,512,128]{3,2,1,0:T(8,128)(2,1)}), bf16[32,2,512,128]{3,2,1,0:T(8,128)(2,1)}, u32[]{:S(2)}, u32[]{:S(2)}) %all-to-all-start.1) | async-done | bytes 8388640 | tf_op jit(solution)/shard_map/all_to_all | solution.py:203
  290.3 10.5 %shard_map.85 = (f32[2,1,1024]{2,1,0:T(1,128)S(1)}, f32[2,1,1024]{2,1,0:T(1,128)S(1)}, f32[2,128,1024]{2,1,0:T(8,128)S(1)}) custom-call(s32[16]{0:T(128)S(1)} %gather_fusion, s32[16]{0:T(128)S(1)} %reduce.remap_ref, bf16[2,128,1024]{2,1,0:T(8,128)(2,1)S(1)} %copy-done.2, ...), custom_call_target="tpu_custom_call", output_to_operand_aliasing={{0}: (5, {}), {1}: (6, {}), {2}: (7, {})} | custom-call | flops 4294967296 | bytes 10485760 | tf_op jit(solution)/shard_map/pallas_call | solution.py:137
  (72 shorter events, 15.2 us)
Async XLA Ops:
  0.0 192.8 %copy-start = (bf16[8192,128]{1,0:T(8,128)(2,1)S(1)}, bf16[8192,128]{1,0:T(8,128)(2,1)}, u32[]{:S(2)}) copy-start(bf16[8192,128]{1,0:T(8,128)(2,1)} %param.10) | copy-start | bytes 6291460
  2.9 13.8 %all-to-all-start = ((s32[32,2,2]{2,1,0:T(2,128)}), s32[32,2,2]{2,1,0:T(2,128)S(1)}, u32[]{:S(2)}, u32[]{:S(2)}) async-start(s32[32,2,2]{2,1,0:T(2,128)} %copy.44), calls=%async_computation | async-start | bytes 65536 | tf_op jit(solution)/shard_map/all_to_all | solution.py:191
  28.3 6.1 %copy-start.5 = (bf16[256,2048]{1,0:T(8,128)(2,1)S(1)}, bf16[256,2048]{1,0:T(8,128)(2,1)}, u32[]{:S(2)}) copy-start(bf16[256,2048]{1,0:T(8,128)(2,1)} %param.8) | copy-start | bytes 3145732
  28.3 130.1 %all-to-all-start.2 = ((bf16[32,2,512,128]{3,2,1,0:T(8,128)(2,1)}), bf16[32,2,512,128]{3,2,1,0:T(8,128)(2,1)}, u32[]{:S(2)}, u32[]{:S(2)}) async-start(bf16[32,2,512,128]{3,2,1,0:T(8,128)(2,1)} %shard_map.83), calls=%async_computation.2 | async-start | bytes 16777216 | tf_op jit(solution)/shard_map/all_to_all | solution.py:203
  34.4 144.2 %collective-permute-start = (bf16[256,2048]{1,0:T(8,128)(2,1)S(1)}, bf16[256,2048]{1,0:T(8,128)(2,1)}, u32[]{:S(2)}, u32[]{:S(2)}) collective-permute-start(bf16[256,2048]{1,0:T(8,128)(2,1)S(1)} %copy-done.5), channel_id=1, source_target_pairs={{0,1},{1,2},{2,3},{3,0},{4,5},{5,6},{6,7},{7,4},{8,9},{9,10},{10,1... | collective-permute-start | bytes 3145736 | tf_op jit(solution)/shard_map/ppermute | solution.py:209
  36.4 142.2 %collective-permute-start.1 = (bf16[256,2048]{1,0:T(8,128)(2,1)S(1)}, bf16[256,2048]{1,0:T(8,128)(2,1)}, u32[]{:S(2)}, u32[]{:S(2)}) collective-permute-start(bf16[256,2048]{1,0:T(8,128)(2,1)S(1)} %copy-done.5), channel_id=1, source_target_pairs={{0,2},{1,3},{2,0},{3,1},{4,6},{5,7},{6,4},{7,5},{8,10},{9,11},{10,... | collective-permute-start | bytes 3145736 | tf_op jit(solution)/shard_map/ppermute | solution.py:209
  37.6 141.1 %collective-permute-start.2 = (bf16[256,2048]{1,0:T(8,128)(2,1)S(1)}, bf16[256,2048]{1,0:T(8,128)(2,1)}, u32[]{:S(2)}, u32[]{:S(2)}) collective-permute-start(bf16[256,2048]{1,0:T(8,128)(2,1)S(1)} %copy-done.5), channel_id=1, source_target_pairs={{0,3},{1,0},{2,1},{3,2},{4,7},{5,4},{6,5},{7,6},{8,11},{9,8},{10,9... | collective-permute-start | bytes 3145736 | tf_op jit(solution)/shard_map/ppermute | solution.py:209
  158.4 130.8 %all-to-all-start.1 = ((bf16[32,2,512,128]{3,2,1,0:T(8,128)(2,1)}), bf16[32,2,512,128]{3,2,1,0:T(8,128)(2,1)}, u32[]{:S(2)}, u32[]{:S(2)}) async-start(bf16[32,2,512,128]{3,2,1,0:T(8,128)(2,1)} %shard_map.82), calls=%async_computation.1 | async-start | bytes 16777216 | tf_op jit(solution)/shard_map/all_to_all | solution.py:203
  192.8 1.7 copy-start.4
  192.8 2.0 copy-start.6
  194.8 1.4 copy-start.3
  202.7 1.0 copy-start.1
  289.2 1.0 copy-start.2

commit v8 on v7

--- a/solution.py
+++ b/solution.py
@@ -29,16 +29,18 @@
     )
 
 
-def send_kernel(loc_ref, k_ref, v_ref, c_ref, s_ref, out_ref):
+def send_kernel(slot, req_ref, k_ref, v_ref, c_ref, s_ref, out_ref):
     per = out_ref.shape[0]
     base = pl.program_id(0) * per
 
     def body(j, carry):
-        loc = loc_ref[base + j]
+        at = ((base + j) * CAP + slot) * 2
+        loc = req_ref[at]
+        pos = req_ref[at + 1]
         k = k_ref[loc].astype(jnp.float32)
         turned = pltpu.roll(k, k.shape[-1] // 2, 1)
-        cos_row = c_ref[pl.ds(base + j, 1), :]
-        sin_row = s_ref[pl.ds(base + j, 1), :]
+        cos_row = c_ref[pl.ds(pos, 1), :]
+        sin_row = s_ref[pl.ds(pos, 1), :]
         out_ref[j, 0] = (k * cos_row + turned * sin_row).astype(jnp.bfloat16)
         out_ref[j, 1] = v_ref[loc]
         return carry
@@ -46,24 +48,24 @@
     lax.fori_loop(0, per, body, 0)
 
 
-def build_send(loc, cos_full, sin_full, passage_keys, passage_values):
-    owners = loc.shape[0]
+def build_send(slot, req, cos_tab, sin_tab, passage_keys, passage_values):
+    owners = req.shape[0] // (CAP * 2)
     stored, plen, hd = passage_keys.shape
     per = 8
-    full = lambda shape: pl.BlockSpec(shape, lambda i, loc: (0,) * len(shape))
+    full = lambda shape: pl.BlockSpec(shape, lambda i, req: (0,) * len(shape))
     grid_spec = pltpu.PrefetchScalarGridSpec(
         num_scalar_prefetch=1,
         grid=(owners // per,),
         in_specs=[
             full((stored, plen, hd)),
             full((stored, plen, hd)),
-            full((owners, hd)),
-            full((owners, hd)),
-        ],
-        out_specs=pl.BlockSpec((per, 2, plen, hd), lambda i, loc: (i, 0, 0, 0)),
+            full(cos_tab.shape),
+            full(sin_tab.shape),
+        ],
+        out_specs=pl.BlockSpec((per, 2, plen, hd), lambda i, req: (i, 0, 0, 0)),
     )
     return pl.pallas_call(
-        send_kernel,
+        functools.partial(send_kernel, slot),
         grid_spec=grid_spec,
         out_shape=jax.ShapeDtypeStruct((owners, 2, plen, hd), jnp.bfloat16),
         compiler_params=pltpu.CompilerParams(dimension_semantics=("arbitrary",)),
@@ -71,7 +73,7 @@
             flops=4 * owners * plen * hd, transcendentals=0,
             bytes_accessed=owners * plen * hd * 2 * 2 + 2 * passage_keys.size * 2,
         ),
-    )(loc, passage_keys, passage_values, cos_full, sin_full)
+    )(req, passage_keys, passage_values, cos_tab, sin_tab)
 
 
 ROW_TILE = 1024
@@ -190,14 +192,13 @@
     )
     incoming = lax.all_to_all(request, "store", split_axis=0, concat_axis=0, tiled=True)
 
-    sends = []
-    for c in range(CAP):
-        loc = incoming[:, c, 0]
-        pos = incoming[:, c, 1]
-        cs, sn = angles((pos * PLEN).astype(jnp.float32))
-        cos_full = jnp.concatenate([cs, cs], axis=-1)
-        sin_full = jnp.concatenate([-sn, sn], axis=-1)
-        sends.append(build_send(loc, cos_full, sin_full, passage_keys, passage_values))
+    cs, sn = angles((jnp.arange(RETR, dtype=jnp.int32) * PLEN).astype(jnp.float32))
+    cos_tab = jnp.concatenate([cs, cs], axis=-1)
+    sin_tab = jnp.concatenate([-sn, sn], axis=-1)
+    req = incoming.reshape(-1)
+    sends = [
+        build_send(c, req, cos_tab, sin_tab, passage_keys, passage_values) for c in range(CAP)
+    ]
 
     recvs = [
         lax.all_to_all(s, "store", split_axis=0, concat_axis=0, tiled=True) for s in sends

time: 304 us -> 302 us (level)
  matrix products: 15 us -> 18.2 us
  transfers between devices with their start and end apart: 6 -> 6, of which waited for: 3 -> 3; matrix products, arithmetic and copies ran while one was open for 10% -> 11% of each run, Pallas kernels for 11% -> 12%
where the time goes in v8:
time: 302 us; the launch traced here: 298 us
  waiting for transfers between devices  172 us (57%)
  Pallas kernels  52.2 us (17%)
  starting transfers between devices  25.1 us (8%)
  matrix products  18.2 us (6%)
  local copies, waits for them, and re-layouts  12.6 us (4%)
  other arithmetic  9.69 us (3%)
  between operations  8.16 us (3%)
    all_to_all x2, waiting for transfers between devices, per_device(): lax.all_to_all(s, 'store', split_axis=0, concat_axis=0, tiled=True)  166 us
    pallas_call x2, Pallas kernels, attend_chunk(): pl.pallas_call(block_kernel, grid_spec=grid_spec, out_shape=[jax.ShapeDty...  37.4 us
    pallas_call x2, Pallas kernels, build_send(): pl.pallas_call(functools.partial(send_kernel, slot), grid_spec=grid_spec,...  14.9 us
    all_to_all x2, starting transfers between devices, per_device(): lax.all_to_all(s, 'store', split_axis=0, concat_axis=0, tiled=True)  12.5 us
    dot_general x1, matrix products, per_device(): qf = jnp.dot(piece, w_query, preferred_element_type=jnp.float32)  11.8 us
    all_to_all x1, starting transfers between devices, per_device(): lax.all_to_all(request, 'store', split_axis=0, concat_axis=0, tiled=True)  7.53 us
  transfers between devices with their start and end apart: 6, of which 3 were waited for; matrix products, arithmetic and copies ran while one was open for 11% of the time, Pallas kernels for 12%

profile of v8, /device:TPU:40, one launch (start us, length us, event | category | flops | bytes accessed | tf_op | source)
XLA Modules:
  0.0 297.8 jit_solution(8857005433867105379)
XLA Ops:
  2.9 7.5 %all-to-all-start = ((s32[32,2,2]{2,1,0:T(2,128)}), s32[32,2,2]{2,1,0:T(2,128)S(1)}, u32[]{:S(2)}, u32[]{:S(2)}) async-start(s32[32,2,2]{2,1,0:T(2,128)} %copy.37), calls=%async_computation | async-start | bytes 65536 | tf_op jit(solution)/shard_map/all_to_all | solution.py:193
  11.2 5.4 %all-to-all-done = s32[32,2,2]{2,1,0:T(2,128)S(1)} async-done(((s32[32,2,2]{2,1,0:T(2,128)}), s32[32,2,2]{2,1,0:T(2,128)S(1)}, u32[]{:S(2)}, u32[]{:S(2)}) %all-to-all-start) | async-done | bytes 544 | tf_op jit(solution)/shard_map/all_to_all | solution.py:193
  17.3 7.4 %shard_map.83 = bf16[32,2,512,128]{3,2,1,0:T(8,128)(2,1)} custom-call(s32[128]{0:T(128)} %reshape.215.req_ref, bf16[4,512,128]{2,1,0:T(8,128)(2,1)} %k_ref.3, bf16[4,512,128]{2,1,0:T(8,128)(2,1)} %v_ref.3, f32[16,128]{1,0:T(8,128)} %get-tuple-element.57.c_ref, f32[16,128]{1,0:T(8,128)} %get-tuple-element.58.s_ref), custom_call_target="tpu_custom_call" | custom-call | flops 8388608 | bytes 9437184 | tf_op jit(solution)/shard_map/pallas_call | solution.py:67
  24.7 6.1 %all-to-all-start.2 = ((bf16[32,2,512,128]{3,2,1,0:T(8,128)(2,1)}), bf16[32,2,512,128]{3,2,1,0:T(8,128)(2,1)}, u32[]{:S(2)}, u32[]{:S(2)}) async-start(bf16[32,2,512,128]{3,2,1,0:T(8,128)(2,1)} %shard_map.83), calls=%async_computation.2 | async-start | bytes 16777216 | tf_op jit(solution)/shard_map/all_to_all | solution.py:204
  30.9 2.0 collective-permute-start
  33.0 3.0 collective-permute-start.1
  35.9 7.5 %shard_map.82 = bf16[32,2,512,128]{3,2,1,0:T(8,128)(2,1)} custom-call(s32[128]{0:T(128)} %reshape.215.req_ref, bf16[4,512,128]{2,1,0:T(8,128)(2,1)} %k_ref.3, bf16[4,512,128]{2,1,0:T(8,128)(2,1)} %v_ref.3, f32[16,128]{1,0:T(8,128)} %get-tuple-element.57.c_ref, f32[16,128]{1,0:T(8,128)} %get-tuple-element.58.s_ref), custom_call_target="tpu_custom_call" | custom-call | flops 8388608 | bytes 9437184 | tf_op jit(solution)/shard_map/pallas_call | solution.py:67
  43.4 111.4 %all-to-all-done.2.kv0_ref.kv1_ref = bf16[32,2,512,128]{3,2,1,0:T(8,128)(2,1)} async-done(((bf16[32,2,512,128]{3,2,1,0:T(8,128)(2,1)}), bf16[32,2,512,128]{3,2,1,0:T(8,128)(2,1)}, u32[]{:S(2)}, u32[]{:S(2)}) %all-to-all-start.2) | async-done | bytes 8388640 | tf_op jit(solution)/shard_map/all_to_all | solution.py:204
  154.8 6.4 %all-to-all-start.1 = ((bf16[32,2,512,128]{3,2,1,0:T(8,128)(2,1)}), bf16[32,2,512,128]{3,2,1,0:T(8,128)(2,1)}, u32[]{:S(2)}, u32[]{:S(2)}) async-start(bf16[32,2,512,128]{3,2,1,0:T(8,128)(2,1)} %shard_map.82), calls=%async_computation.1 | async-start | bytes 16777216 | tf_op jit(solution)/shard_map/all_to_all | solution.py:204
  161.2 1.6 sort.31
  169.6 1.6 sort.32
  175.1 2.1 pad_maximum_fusion
  177.6 11.8 %convolution_bitcast_fusion = f32[32,8,8,128]{3,1,2,0:T(8,128)S(1)} fusion(bf16[8192,1024]{1,0:T(8,128)(2,1)} %param.9, bf16[256,2048]{1,0:T(8,128)(2,1)S(1)} %get-tuple-element.28, bf16[256,2048]{1,0:T(8,128)(2,1)S(1)} %get-tuple-element.29, bf16[256,2048]{1,0:T(8,128)(2,1)S(1)} %get-tuple-element.30, bf16[256,2048]{1,0:T(8,128)(2,1)S(1)} %get-tuple-element.27), kind=kOutput, calls=%fused_computation.4 | convolution fusion | flops 4311744512 | bytes 22020096 | tf_op jit(solution)/shard_map/dot_general | solution.py:219
  190.8 1.0 copy.45.q_ref
  191.9 3.2 %fusion.26 = f32[256,128]{1,0:T(8,128)S(1)} fusion(bf16[8192,128]{1,0:T(8,128)(2,1)S(1)} %copy-done, bf16[256,2048]{1,0:T(8,128)(2,1)} %copy-done.6, bf16[256,2048]{1,0:T(8,128)(2,1)} %copy-done.8, bf16[256,2048]{1,0:T(8,128)(2,1)} %copy-done.10, bf16[256,2048]{1,0:T(8,128)(2,1)} %copy-done.4), kind=kOutput, calls=%fused_computation.94 | convolution fusion | flops 553648128 | bytes 6422528 | tf_op jit(solution)/shard_map/dot_general | solution.py:220
  196.0 1.4 convolution_convert_fusion
  197.4 1.3 fusion.3
  198.7 1.6 copy.46.a_in
  200.3 1.4 fusion.2
  201.7 1.0 copy-done.1
  202.8 27.9 %shard_map.84 = (f32[2,1,1024]{2,1,0:T(1,128)S(1)}, f32[2,1,1024]{2,1,0:T(1,128)S(1)}, f32[2,128,1024]{2,1,0:T(8,128)S(1)}) custom-call(s32[32]{0:T(128)S(1)} %gather_fusion.1, s32[32]{0:T(128)S(1)} %reduce.1.remap_ref, bf16[2,128,1024]{2,1,0:T(8,128)(2,1)S(1)} %copy-done.1, ...), custom_call_target="tpu_custom_call", output_to_operand_aliasing={{0}: (5, {}), {1}: (6, {}), {2}: (7, {})} | custom-call | flops 8589934592 | bytes 10485760 | tf_op jit(solution)/shard_map/pallas_call | solution.py:139
  230.7 55.0 %all-to-all-done.1.kv0_ref.kv1_ref = bf16[32,2,512,128]{3,2,1,0:T(8,128)(2,1)} async-done(((bf16[32,2,512,128]{3,2,1,0:T(8,128)(2,1)}), bf16[32,2,512,128]{3,2,1,0:T(8,128)(2,1)}, u32[]{:S(2)}, u32[]{:S(2)}) %all-to-all-start.1) | async-done | bytes 8388640 | tf_op jit(solution)/shard_map/all_to_all | solution.py:204
  285.7 1.0 copy-done.2
  286.7 9.5 %shard_map.85 = (f32[2,1,1024]{2,1,0:T(1,128)S(1)}, f32[2,1,1024]{2,1,0:T(1,128)S(1)}, f32[2,128,1024]{2,1,0:T(8,128)S(1)}) custom-call(s32[16]{0:T(128)S(1)} %gather_fusion, s32[16]{0:T(128)S(1)} %reduce.remap_ref, bf16[2,128,1024]{2,1,0:T(8,128)(2,1)S(1)} %copy-done.2, ...), custom_call_target="tpu_custom_call", output_to_operand_aliasing={{0}: (5, {}), {1}: (6, {}), {2}: (7, {})} | custom-call | flops 4294967296 | bytes 10485760 | tf_op jit(solution)/shard_map/pallas_call | solution.py:139
  (83 shorter events, 11.4 us)
Async XLA Ops:
  0.0 191.8 %copy-start = (bf16[8192,128]{1,0:T(8,128)(2,1)S(1)}, bf16[8192,128]{1,0:T(8,128)(2,1)}, u32[]{:S(2)}) copy-start(bf16[8192,128]{1,0:T(8,128)(2,1)} %param.10) | copy-start | bytes 6291460
  2.9 13.7 %all-to-all-start = ((s32[32,2,2]{2,1,0:T(2,128)}), s32[32,2,2]{2,1,0:T(2,128)S(1)}, u32[]{:S(2)}, u32[]{:S(2)}) async-start(s32[32,2,2]{2,1,0:T(2,128)} %copy.37), calls=%async_computation | async-start | bytes 65536 | tf_op jit(solution)/shard_map/all_to_all | solution.py:193
  24.7 6.1 %copy-start.12 = (bf16[256,2048]{1,0:T(8,128)(2,1)S(1)}, bf16[256,2048]{1,0:T(8,128)(2,1)}, u32[]{:S(2)}) copy-start(bf16[256,2048]{1,0:T(8,128)(2,1)} %param.8) | copy-start | bytes 3145732
  24.7 130.1 %all-to-all-start.2 = ((bf16[32,2,512,128]{3,2,1,0:T(8,128)(2,1)}), bf16[32,2,512,128]{3,2,1,0:T(8,128)(2,1)}, u32[]{:S(2)}, u32[]{:S(2)}) async-start(bf16[32,2,512,128]{3,2,1,0:T(8,128)(2,1)} %shard_map.83), calls=%async_computation.2 | async-start | bytes 16777216 | tf_op jit(solution)/shard_map/all_to_all | solution.py:204
  30.9 144.3 %collective-permute-start = (bf16[256,2048]{1,0:T(8,128)(2,1)S(1)}, bf16[256,2048]{1,0:T(8,128)(2,1)}, u32[]{:S(2)}, u32[]{:S(2)}) collective-permute-start(bf16[256,2048]{1,0:T(8,128)(2,1)S(1)} %copy-done.12), channel_id=1, source_target_pairs={{0,1},{1,2},{2,3},{3,0},{4,5},{5,6},{6,7},{7,4},{8,9},{9,10},{10,1... | collective-permute-start | bytes 3145736 | tf_op jit(solution)/shard_map/ppermute | solution.py:210
  32.9 142.3 %collective-permute-start.2 = (bf16[256,2048]{1,0:T(8,128)(2,1)S(1)}, bf16[256,2048]{1,0:T(8,128)(2,1)}, u32[]{:S(2)}, u32[]{:S(2)}) collective-permute-start(bf16[256,2048]{1,0:T(8,128)(2,1)S(1)} %copy-done.12), channel_id=1, source_target_pairs={{0,3},{1,0},{2,1},{3,2},{4,7},{5,4},{6,5},{7,6},{8,11},{9,8},{10,9... | collective-permute-start | bytes 3145736 | tf_op jit(solution)/shard_map/ppermute | solution.py:210
  33.0 142.2 %collective-permute-start.1 = (bf16[256,2048]{1,0:T(8,128)(2,1)S(1)}, bf16[256,2048]{1,0:T(8,128)(2,1)}, u32[]{:S(2)}, u32[]{:S(2)}) collective-permute-start(bf16[256,2048]{1,0:T(8,128)(2,1)S(1)} %copy-done.12), channel_id=1, source_target_pairs={{0,2},{1,3},{2,0},{3,1},{4,6},{5,7},{6,4},{7,5},{8,10},{9,11},{10,... | collective-permute-start | bytes 3145736 | tf_op jit(solution)/shard_map/ppermute | solution.py:210
  154.8 130.8 %all-to-all-start.1 = ((bf16[32,2,512,128]{3,2,1,0:T(8,128)(2,1)}), bf16[32,2,512,128]{3,2,1,0:T(8,128)(2,1)}, u32[]{:S(2)}, u32[]{:S(2)}) async-start(bf16[32,2,512,128]{3,2,1,0:T(8,128)(2,1)} %shard_map.82), calls=%async_computation.1 | async-start | bytes 16777216 | tf_op jit(solution)/shard_map/all_to_all | solution.py:204
  177.6 11.9 %copy-start.4 = (bf16[256,2048]{1,0:T(8,128)(2,1)}, bf16[256,2048]{1,0:T(8,128)(2,1)S(1)}, u32[]{:S(2)}) copy-start(bf16[256,2048]{1,0:T(8,128)(2,1)S(1)} %get-tuple-element.27) | copy-start | bytes 3145732
  177.6 11.9 %copy-start.6 = (bf16[256,2048]{1,0:T(8,128)(2,1)}, bf16[256,2048]{1,0:T(8,128)(2,1)S(1)}, u32[]{:S(2)}) copy-start(bf16[256,2048]{1,0:T(8,128)(2,1)S(1)} %get-tuple-element.28) | copy-start | bytes 3145732
  177.6 11.9 %copy-start.8 = (bf16[256,2048]{1,0:T(8,128)(2,1)}, bf16[256,2048]{1,0:T(8,128)(2,1)S(1)}, u32[]{:S(2)}) copy-start(bf16[256,2048]{1,0:T(8,128)(2,1)S(1)} %get-tuple-element.29) | copy-start | bytes 3145732
  177.6 11.9 %copy-start.10 = (bf16[256,2048]{1,0:T(8,128)(2,1)}, bf16[256,2048]{1,0:T(8,128)(2,1)S(1)}, u32[]{:S(2)}) copy-start(bf16[256,2048]{1,0:T(8,128)(2,1)S(1)} %get-tuple-element.30) | copy-start | bytes 3145732
  191.8 3.7 %copy-start.5 = (bf16[256,2048]{1,0:T(8,128)(2,1)S(1)}, bf16[256,2048]{1,0:T(8,128)(2,1)}, u32[]{:S(2)}) copy-start(bf16[256,2048]{1,0:T(8,128)(2,1)} %copy-done.4) | copy-start | bytes 3145732
  191.8 3.7 %copy-start.7 = (bf16[256,2048]{1,0:T(8,128)(2,1)S(1)}, bf16[256,2048]{1,0:T(8,128)(2,1)}, u32[]{:S(2)}) copy-start(bf16[256,2048]{1,0:T(8,128)(2,1)} %copy-done.6) | copy-start | bytes 3145732
  191.8 3.8 %copy-start.9 = (bf16[256,2048]{1,0:T(8,128)(2,1)S(1)}, bf16[256,2048]{1,0:T(8,128)(2,1)}, u32[]{:S(2)}) copy-start(bf16[256,2048]{1,0:T(8,128)(2,1)} %copy-done.8) | copy-start | bytes 3145732
  191.8 3.8 %copy-start.11 = (bf16[256,2048]{1,0:T(8,128)(2,1)S(1)}, bf16[256,2048]{1,0:T(8,128)(2,1)}, u32[]{:S(2)}) copy-start(bf16[256,2048]{1,0:T(8,128)(2,1)} %copy-done.10) | copy-start | bytes 3145732
  191.8 4.1 %copy-start.13 = (bf16[8192,128]{1,0:T(8,128)(2,1)S(1)}, bf16[8192,128]{1,0:T(8,128)(2,1)}, u32[]{:S(2)}) copy-start(bf16[8192,128]{1,0:T(8,128)(2,1)} %param.11) | copy-start | bytes 6291460
  196.0 1.4 copy-start.3
  201.7 1.0 copy-start.1
  285.7 1.0 copy-start.2

commit v9 on v8

--- a/solution.py
+++ b/solution.py
@@ -37,11 +37,14 @@
         at = ((base + j) * CAP + slot) * 2
         loc = req_ref[at]
         pos = req_ref[at + 1]
-        k = k_ref[loc].astype(jnp.float32)
-        turned = pltpu.roll(k, k.shape[-1] // 2, 1)
-        cos_row = c_ref[pl.ds(pos, 1), :]
-        sin_row = s_ref[pl.ds(pos, 1), :]
-        out_ref[j, 0] = (k * cos_row + turned * sin_row).astype(jnp.bfloat16)
+        if slot == 0:
+            out_ref[j, 0] = k_ref[loc]
+        else:
+            k = k_ref[loc].astype(jnp.float32)
+            turned = pltpu.roll(k, k.shape[-1] // 2, 1)
+            cos_row = c_ref[pl.ds(pos, 1), :]
+            sin_row = s_ref[pl.ds(pos, 1), :]
+            out_ref[j, 0] = (k * cos_row + turned * sin_row).astype(jnp.bfloat16)
         out_ref[j, 1] = v_ref[loc]
         return carry
 
@@ -80,7 +83,10 @@
 LOG2E = 1.4426950408889634
 
 
-def block_kernel(tab_ref, remap_ref, q_ref, kv0_ref, kv1_ref, m_in, l_in, a_in, m_ref, l_ref, a_ref):
+def block_kernel(
+    rotate_keys, tab_ref, remap_ref, pos_ref, q_ref, kv0_ref, kv1_ref, c_ref, s_ref,
+    m_in, l_in, a_in, m_ref, l_ref, a_ref,
+):
     o = pl.program_id(0)
 
     @pl.when(o == 0)
@@ -96,6 +102,13 @@
         @pl.when(qi >= 0)
         def _():
             k = kv_ref[0, 0]
+            if rotate_keys:
+                pos = pos_ref[2 * o + j]
+                kf = k.astype(jnp.float32)
+                turned = pltpu.roll(kf, kf.shape[-1] // 2, 1)
+                k = (
+                    kf * c_ref[pl.ds(pos, 1), :] + turned * s_ref[pl.ds(pos, 1), :]
+                ).astype(jnp.bfloat16)
             v = kv_ref[0, 1]
             for r0 in range(0, q_ref.shape[2], ROW_TILE):
                 cols = pl.ds(r0, ROW_TILE)
@@ -117,18 +130,20 @@
                 m_ref[qi, :, cols] = m_new
 
 
-def attend_chunk(tab, remap, query_t, recv, m, l, acc):
+def attend_chunk(rotate_keys, tab, remap, pos, cos_tab, sin_tab, query_t, recv, m, l, acc):
     owners = tab.shape[0] // 2
     nq, hd, rows = query_t.shape
     plen = recv.shape[2]
-    full3 = lambda shape: pl.BlockSpec(shape, lambda o, t, r: (0, 0, 0))
+    full3 = lambda shape: pl.BlockSpec(shape, lambda o, t, r, p: (0, 0, 0))
     grid_spec = pltpu.PrefetchScalarGridSpec(
-        num_scalar_prefetch=2,
+        num_scalar_prefetch=3,
         grid=(owners,),
         in_specs=[
             full3((nq, hd, rows)),
-            pl.BlockSpec((1, 2, plen, hd), lambda o, t, r: (r[2 * o], 0, 0, 0)),
-            pl.BlockSpec((1, 2, plen, hd), lambda o, t, r: (r[2 * o + 1], 0, 0, 0)),
+            pl.BlockSpec((1, 2, plen, hd), lambda o, t, r, p: (r[2 * o], 0, 0, 0)),
+            pl.BlockSpec((1, 2, plen, hd), lambda o, t, r, p: (r[2 * o + 1], 0, 0, 0)),
+            pl.BlockSpec(cos_tab.shape, lambda o, t, r, p: (0, 0)),
+            pl.BlockSpec(sin_tab.shape, lambda o, t, r, p: (0, 0)),
             full3((nq, 1, rows)),
             full3((nq, 1, rows)),
             full3((nq, hd, rows)),
@@ -137,14 +152,14 @@
     )
     flops = 4 * nq * rows * plen * hd * owners
     return pl.pallas_call(
-        block_kernel,
+        functools.partial(block_kernel, rotate_keys),
         grid_spec=grid_spec,
         out_shape=[
             jax.ShapeDtypeStruct(m.shape, jnp.float32),
             jax.ShapeDtypeStruct(l.shape, jnp.float32),
             jax.ShapeDtypeStruct(acc.shape, jnp.float32),
         ],
-        input_output_aliases={5: 0, 6: 1, 7: 2},
+        input_output_aliases={8: 0, 9: 1, 10: 2},
         compiler_params=pltpu.CompilerParams(
             dimension_semantics=("arbitrary",), vmem_limit_bytes=48 * 1024 * 1024
         ),
@@ -153,7 +168,7 @@
             transcendentals=nq * rows * plen * owners,
             bytes_accessed=recv.size * 2 + 2 * acc.size * 4,
         ),
-    )(tab, remap, query_t, recv, recv, m, l, acc)
+    )(tab, remap, pos, query_t, recv, recv, cos_tab, sin_tab, m, l, acc)
 
 
 def per_device(
@@ -254,9 +269,12 @@
         tab = jnp.sum(hit * qidx[:, None], axis=0) + valid - 1
         steps = owners_count if c == 0 else min(owners_count, listed // CAP)
         order = jnp.argsort(1 - valid, stable=True).astype(jnp.int32)[:steps]
+        pos = jnp.sum(hit * my_pos[:, None], axis=0)[order]
         tab = tab[order]
         remap = lax.cummax(jnp.where(tab >= 0, order, 0), axis=0)
-        m, l, acc = attend_chunk(tab, remap, query_t, recvs[c], m, l, acc)
+        m, l, acc = attend_chunk(
+            c == 0, tab, remap, pos, cos_tab, sin_tab, query_t, recvs[c], m, l, acc
+        )
 
     ctx = (acc / l).reshape(count, HD, q_heads, QLEN)
     ctx = jnp.transpose(ctx, (0, 3, 2, 1)).reshape(tok_rows, q_heads * HD)

time: 302 us -> 299 us (0.990)
  transfers between devices with their start and end apart: 6 -> 6, of which waited for: 3 -> 3; matrix products, arithmetic and copies ran while one was open for 11% -> 12% of each run, Pallas kernels for 12% -> 12%
where the time goes in v9:
time: 299 us; the launch traced here: 296 us
  waiting for transfers between devices  169 us (57%)
  Pallas kernels  51.1 us (17%)
  starting transfers between devices  25.1 us (8%)
  matrix products  19.2 us (6%)
  local copies, waits for them, and re-layouts  13.6 us (5%)
  other arithmetic  9.65 us (3%)
  between operations  8.21 us (3%)
    all_to_all x2, waiting for transfers between devices, per_device(): lax.all_to_all(s, 'store', split_axis=0, concat_axis=0, tiled=True)  164 us
    pallas_call x2, Pallas kernels, attend_chunk(): pl.pallas_call(functools.partial(block_kernel, rotate_keys), grid_spec=gr...  38.1 us
    pallas_call x2, Pallas kernels, build_send(): pl.pallas_call(functools.partial(send_kernel, slot), grid_spec=grid_spec,...  13 us
    all_to_all x2, starting transfers between devices, per_device(): lax.all_to_all(s, 'store', split_axis=0, concat_axis=0, tiled=True)  12.5 us
    dot_general x1, matrix products, per_device(): qf = jnp.dot(piece, w_query, preferred_element_type=jnp.float32)  11.8 us
    all_to_all x1, starting transfers between devices, per_device(): lax.all_to_all(request, 'store', split_axis=0, concat_axis=0, tiled=True)  7.53 us
  transfers between devices with their start and end apart: 6, of which 3 were waited for; matrix products, arithmetic and copies ran while one was open for 12% of the time, Pallas kernels for 12%

profile of v9, /device:TPU:40, one launch (start us, length us, event | category | flops | bytes accessed | tf_op | source)
XLA Modules:
  0.0 295.8 jit_solution(4731541852348836356)
XLA Ops:
  2.9 7.5 %all-to-all-start = ((s32[32,2,2]{2,1,0:T(2,128)}), s32[32,2,2]{2,1,0:T(2,128)S(1)}, u32[]{:S(2)}, u32[]{:S(2)}) async-start(s32[32,2,2]{2,1,0:T(2,128)} %copy.37), calls=%async_computation | async-start | bytes 65536 | tf_op jit(solution)/shard_map/all_to_all | solution.py:208
  11.2 5.4 %all-to-all-done = s32[32,2,2]{2,1,0:T(2,128)S(1)} async-done(((s32[32,2,2]{2,1,0:T(2,128)}), s32[32,2,2]{2,1,0:T(2,128)S(1)}, u32[]{:S(2)}, u32[]{:S(2)}) %all-to-all-start) | async-done | bytes 544 | tf_op jit(solution)/shard_map/all_to_all | solution.py:208
  17.3 5.6 %shard_map.83 = bf16[32,2,512,128]{3,2,1,0:T(8,128)(2,1)} custom-call(s32[128]{0:T(128)} %reshape.215.req_ref, bf16[4,512,128]{2,1,0:T(8,128)(2,1)} %k_ref.3, bf16[4,512,128]{2,1,0:T(8,128)(2,1)} %v_ref.3, f32[16,128]{1,0:T(8,128)} %get-tuple-element.57.c_ref, f32[16,128]{1,0:T(8,128)} %get-tuple-element.58.s_ref), custom_call_target="tpu_custom_call" | custom-call | flops 8388608 | bytes 9437184 | tf_op jit(solution)/shard_map/pallas_call | solution.py:70
  22.8 6.1 %all-to-all-start.2 = ((bf16[32,2,512,128]{3,2,1,0:T(8,128)(2,1)}), bf16[32,2,512,128]{3,2,1,0:T(8,128)(2,1)}, u32[]{:S(2)}, u32[]{:S(2)}) async-start(bf16[32,2,512,128]{3,2,1,0:T(8,128)(2,1)} %shard_map.83), calls=%async_computation.2 | async-start | bytes 16777216 | tf_op jit(solution)/shard_map/all_to_all | solution.py:219
  29.0 2.0 collective-permute-start
  31.1 3.0 %collective-permute-start.1 = (bf16[256,2048]{1,0:T(8,128)(2,1)S(1)}, bf16[256,2048]{1,0:T(8,128)(2,1)}, u32[]{:S(2)}, u32[]{:S(2)}) collective-permute-start(bf16[256,2048]{1,0:T(8,128)(2,1)S(1)} %copy-done.15), channel_id=1, source_target_pairs={{0,2},{1,3},{2,0},{3,1},{4,6},{5,7},{6,4},{7,5},{8,10},{9,11},{10,... | collective-permute-start | bytes 3145736 | tf_op jit(solution)/shard_map/ppermute | solution.py:225
  34.1 7.5 %shard_map.82 = bf16[32,2,512,128]{3,2,1,0:T(8,128)(2,1)} custom-call(s32[128]{0:T(128)} %reshape.215.req_ref, bf16[4,512,128]{2,1,0:T(8,128)(2,1)} %k_ref.3, bf16[4,512,128]{2,1,0:T(8,128)(2,1)} %v_ref.3, f32[16,128]{1,0:T(8,128)} %get-tuple-element.57.c_ref, f32[16,128]{1,0:T(8,128)} %get-tuple-element.58.s_ref), custom_call_target="tpu_custom_call" | custom-call | flops 8388608 | bytes 9437184 | tf_op jit(solution)/shard_map/pallas_call | solution.py:70
  41.5 111.4 %all-to-all-done.2.kv0_ref.kv1_ref = bf16[32,2,512,128]{3,2,1,0:T(8,128)(2,1)} async-done(((bf16[32,2,512,128]{3,2,1,0:T(8,128)(2,1)}), bf16[32,2,512,128]{3,2,1,0:T(8,128)(2,1)}, u32[]{:S(2)}, u32[]{:S(2)}) %all-to-all-start.2) | async-done | bytes 8388640 | tf_op jit(solution)/shard_map/all_to_all | solution.py:219
  153.0 6.4 %all-to-all-start.1 = ((bf16[32,2,512,128]{3,2,1,0:T(8,128)(2,1)}), bf16[32,2,512,128]{3,2,1,0:T(8,128)(2,1)}, u32[]{:S(2)}, u32[]{:S(2)}) async-start(bf16[32,2,512,128]{3,2,1,0:T(8,128)(2,1)} %shard_map.82), calls=%async_computation.1 | async-start | bytes 16777216 | tf_op jit(solution)/shard_map/all_to_all | solution.py:219
  159.4 1.6 sort.32
  161.0 1.6 sort.31
  174.6 2.1 pad_maximum_fusion
  177.1 11.8 %convolution_bitcast_fusion = f32[32,8,8,128]{3,1,2,0:T(8,128)S(1)} fusion(bf16[8192,1024]{1,0:T(8,128)(2,1)} %param.9, bf16[256,2048]{1,0:T(8,128)(2,1)S(1)} %get-tuple-element.28, bf16[256,2048]{1,0:T(8,128)(2,1)S(1)} %get-tuple-element.29, bf16[256,2048]{1,0:T(8,128)(2,1)S(1)} %get-tuple-element.30, bf16[256,2048]{1,0:T(8,128)(2,1)S(1)} %get-tuple-element.27), kind=kOutput, calls=%fused_computation.6 | convolution fusion | flops 4311744512 | bytes 22020096 | tf_op jit(solution)/shard_map/dot_general | solution.py:234
  191.3 3.2 %fusion.26 = f32[256,128]{1,0:T(8,128)S(1)} fusion(bf16[8192,128]{1,0:T(8,128)(2,1)S(1)} %copy-done, bf16[256,2048]{1,0:T(8,128)(2,1)} %copy-done.9, bf16[256,2048]{1,0:T(8,128)(2,1)} %copy-done.11, bf16[256,2048]{1,0:T(8,128)(2,1)} %copy-done.13, bf16[256,2048]{1,0:T(8,128)(2,1)} %copy-done.7), kind=kOutput, calls=%fused_computation.96 | convolution fusion | flops 553648128 | bytes 6422528 | tf_op jit(solution)/shard_map/dot_general | solution.py:235
  194.7 1.4 fusion.29
  196.1 1.4 convolution_convert_fusion
  197.6 1.4 fusion.3
  198.9 1.6 copy.46.a_in
  200.5 1.4 fusion.2
  202.0 1.0 copy-done.1
  203.0 28.7 %shard_map.84 = (f32[2,1,1024]{2,1,0:T(1,128)S(1)}, f32[2,1,1024]{2,1,0:T(1,128)S(1)}, f32[2,128,1024]{2,1,0:T(8,128)S(1)}) custom-call(s32[32]{0:T(128)S(1)} %gather_fusion.2, s32[32]{0:T(128)S(1)} %reduce.1.remap_ref, s32[32]{0:T(128)S(1)} %gather_fusion.3, ...), custom_call_target="tpu_custom_call", output_to_operand_aliasing={{0}: (8, {}), {1}: (9, {}), {2}: (10, {})} | custom-call | flops 8589934592 | bytes 10485760 | tf_op jit(solution)/shard_map/pallas_call | solution.py:154
  231.7 52.1 %all-to-all-done.1.kv0_ref.kv1_ref = bf16[32,2,512,128]{3,2,1,0:T(8,128)(2,1)} async-done(((bf16[32,2,512,128]{3,2,1,0:T(8,128)(2,1)}), bf16[32,2,512,128]{3,2,1,0:T(8,128)(2,1)}, u32[]{:S(2)}, u32[]{:S(2)}) %all-to-all-start.1) | async-done | bytes 8388640 | tf_op jit(solution)/shard_map/all_to_all | solution.py:219
  283.8 1.0 copy-done.2
  284.8 9.4 %shard_map.85 = (f32[2,1,1024]{2,1,0:T(1,128)S(1)}, f32[2,1,1024]{2,1,0:T(1,128)S(1)}, f32[2,128,1024]{2,1,0:T(8,128)S(1)}) custom-call(s32[16]{0:T(128)S(1)} %gather_fusion, s32[16]{0:T(128)S(1)} %reduce.remap_ref, s32[16]{0:T(128)S(1)} %gather_fusion.1, ...), custom_call_target="tpu_custom_call", output_to_operand_aliasing={{0}: (8, {}), {1}: (9, {}), {2}: (10, {})} | custom-call | flops 4294967296 | bytes 10485760 | tf_op jit(solution)/shard_map/pallas_call | solution.py:154
  (91 shorter events, 13.0 us)
Async XLA Ops:
  0.0 191.3 %copy-start = (bf16[8192,128]{1,0:T(8,128)(2,1)S(1)}, bf16[8192,128]{1,0:T(8,128)(2,1)}, u32[]{:S(2)}) copy-start(bf16[8192,128]{1,0:T(8,128)(2,1)} %param.10) | copy-start | bytes 6291460
  2.9 13.7 %all-to-all-start = ((s32[32,2,2]{2,1,0:T(2,128)}), s32[32,2,2]{2,1,0:T(2,128)S(1)}, u32[]{:S(2)}, u32[]{:S(2)}) async-start(s32[32,2,2]{2,1,0:T(2,128)} %copy.37), calls=%async_computation | async-start | bytes 65536 | tf_op jit(solution)/shard_map/all_to_all | solution.py:208
  22.8 6.1 %copy-start.15 = (bf16[256,2048]{1,0:T(8,128)(2,1)S(1)}, bf16[256,2048]{1,0:T(8,128)(2,1)}, u32[]{:S(2)}) copy-start(bf16[256,2048]{1,0:T(8,128)(2,1)} %param.8) | copy-start | bytes 3145732
  22.8 130.1 %all-to-all-start.2 = ((bf16[32,2,512,128]{3,2,1,0:T(8,128)(2,1)}), bf16[32,2,512,128]{3,2,1,0:T(8,128)(2,1)}, u32[]{:S(2)}, u32[]{:S(2)}) async-start(bf16[32,2,512,128]{3,2,1,0:T(8,128)(2,1)} %shard_map.83), calls=%async_computation.2 | async-start | bytes 16777216 | tf_op jit(solution)/shard_map/all_to_all | solution.py:219
  29.0 145.6 %collective-permute-start = (bf16[256,2048]{1,0:T(8,128)(2,1)S(1)}, bf16[256,2048]{1,0:T(8,128)(2,1)}, u32[]{:S(2)}, u32[]{:S(2)}) collective-permute-start(bf16[256,2048]{1,0:T(8,128)(2,1)S(1)} %copy-done.15), channel_id=1, source_target_pairs={{0,1},{1,2},{2,3},{3,0},{4,5},{5,6},{6,7},{7,4},{8,9},{9,10},{10,1... | collective-permute-start | bytes 3145736 | tf_op jit(solution)/shard_map/ppermute | solution.py:225
  31.0 143.6 %collective-permute-start.2 = (bf16[256,2048]{1,0:T(8,128)(2,1)S(1)}, bf16[256,2048]{1,0:T(8,128)(2,1)}, u32[]{:S(2)}, u32[]{:S(2)}) collective-permute-start(bf16[256,2048]{1,0:T(8,128)(2,1)S(1)} %copy-done.15), channel_id=1, source_target_pairs={{0,3},{1,0},{2,1},{3,2},{4,7},{5,4},{6,5},{7,6},{8,11},{9,8},{10,9... | collective-permute-start | bytes 3145736 | tf_op jit(solution)/shard_map/ppermute | solution.py:225
  31.1 143.5 %collective-permute-start.1 = (bf16[256,2048]{1,0:T(8,128)(2,1)S(1)}, bf16[256,2048]{1,0:T(8,128)(2,1)}, u32[]{:S(2)}, u32[]{:S(2)}) collective-permute-start(bf16[256,2048]{1,0:T(8,128)(2,1)S(1)} %copy-done.15), channel_id=1, source_target_pairs={{0,2},{1,3},{2,0},{3,1},{4,6},{5,7},{6,4},{7,5},{8,10},{9,11},{10,... | collective-permute-start | bytes 3145736 | tf_op jit(solution)/shard_map/ppermute | solution.py:225
  153.0 130.8 %all-to-all-start.1 = ((bf16[32,2,512,128]{3,2,1,0:T(8,128)(2,1)}), bf16[32,2,512,128]{3,2,1,0:T(8,128)(2,1)}, u32[]{:S(2)}, u32[]{:S(2)}) async-start(bf16[32,2,512,128]{3,2,1,0:T(8,128)(2,1)} %shard_map.82), calls=%async_computation.1 | async-start | bytes 16777216 | tf_op jit(solution)/shard_map/all_to_all | solution.py:219
  177.1 11.9 %copy-start.7 = (bf16[256,2048]{1,0:T(8,128)(2,1)}, bf16[256,2048]{1,0:T(8,128)(2,1)S(1)}, u32[]{:S(2)}) copy-start(bf16[256,2048]{1,0:T(8,128)(2,1)S(1)} %get-tuple-element.27) | copy-start | bytes 3145732
  177.1 11.9 %copy-start.9 = (bf16[256,2048]{1,0:T(8,128)(2,1)}, bf16[256,2048]{1,0:T(8,128)(2,1)S(1)}, u32[]{:S(2)}) copy-start(bf16[256,2048]{1,0:T(8,128)(2,1)S(1)} %get-tuple-element.28) | copy-start | bytes 3145732
  177.1 11.9 %copy-start.11 = (bf16[256,2048]{1,0:T(8,128)(2,1)}, bf16[256,2048]{1,0:T(8,128)(2,1)S(1)}, u32[]{:S(2)}) copy-start(bf16[256,2048]{1,0:T(8,128)(2,1)S(1)} %get-tuple-element.29) | copy-start | bytes 3145732
  177.1 11.9 %copy-start.13 = (bf16[256,2048]{1,0:T(8,128)(2,1)}, bf16[256,2048]{1,0:T(8,128)(2,1)S(1)}, u32[]{:S(2)}) copy-start(bf16[256,2048]{1,0:T(8,128)(2,1)S(1)} %get-tuple-element.30) | copy-start | bytes 3145732
  190.3 4.3 %copy-start.6 = (bf16[2,128,8,128]{3,1,2,0:T(8,128)(2,1)}, bf16[2,128,8,128]{3,1,2,0:T(8,128)(2,1)S(1)}, u32[]{:S(2)}) copy-start(bf16[2,128,8,128]{3,1,2,0:T(8,128)(2,1)S(1)} %pad_maximum_fusion.2) | copy-start | bytes 1572868
  191.3 4.8 %copy-start.8 = (bf16[256,2048]{1,0:T(8,128)(2,1)S(1)}, bf16[256,2048]{1,0:T(8,128)(2,1)}, u32[]{:S(2)}) copy-start(bf16[256,2048]{1,0:T(8,128)(2,1)} %copy-done.7) | copy-start | bytes 3145732
  191.3 4.8 %copy-start.10 = (bf16[256,2048]{1,0:T(8,128)(2,1)S(1)}, bf16[256,2048]{1,0:T(8,128)(2,1)}, u32[]{:S(2)}) copy-start(bf16[256,2048]{1,0:T(8,128)(2,1)} %copy-done.9) | copy-start | bytes 3145732
  191.3 4.8 %copy-start.12 = (bf16[256,2048]{1,0:T(8,128)(2,1)S(1)}, bf16[256,2048]{1,0:T(8,128)(2,1)}, u32[]{:S(2)}) copy-start(bf16[256,2048]{1,0:T(8,128)(2,1)} %copy-done.11) | copy-start | bytes 3145732
  191.3 4.8 %copy-start.14 = (bf16[256,2048]{1,0:T(8,128)(2,1)S(1)}, bf16[256,2048]{1,0:T(8,128)(2,1)}, u32[]{:S(2)}) copy-start(bf16[256,2048]{1,0:T(8,128)(2,1)} %copy-done.13) | copy-start | bytes 3145732
  191.3 4.8 %copy-start.16 = (bf16[8192,128]{1,0:T(8,128)(2,1)S(1)}, bf16[8192,128]{1,0:T(8,128)(2,1)}, u32[]{:S(2)}) copy-start(bf16[8192,128]{1,0:T(8,128)(2,1)} %param.11) | copy-start | bytes 6291460
  196.1 1.5 copy-start.5
  197.6 4.4 %copy-start.3 = (f32[16,128]{1,0:T(8,128)S(1)}, f32[16,128]{1,0:T(8,128)}, u32[]{:S(2)}) copy-start(f32[16,128]{1,0:T(8,128)} %get-tuple-element.57.c_ref) | copy-start | bytes 24580
  197.6 4.4 %copy-start.4 = (f32[16,128]{1,0:T(8,128)S(1)}, f32[16,128]{1,0:T(8,128)}, u32[]{:S(2)}) copy-start(f32[16,128]{1,0:T(8,128)} %get-tuple-element.58.s_ref) | copy-start | bytes 24580
  202.0 1.0 copy-start.1
  283.8 1.0 copy-start.2

commit v10 on v9

--- a/solution.py
+++ b/solution.py
@@ -83,10 +83,12 @@
 LOG2E = 1.4426950408889634
 
 
-def block_kernel(
-    rotate_keys, tab_ref, remap_ref, pos_ref, q_ref, kv0_ref, kv1_ref, c_ref, s_ref,
-    m_in, l_in, a_in, m_ref, l_ref, a_ref,
-):
+PER_STEP = 4
+
+
+def block_kernel(rotate_keys, tab_ref, remap_ref, pos_ref, q_ref, *refs):
+    kv_refs = refs[:PER_STEP]
+    c_ref, s_ref, m_in, l_in, a_in, m_ref, l_ref, a_ref = refs[PER_STEP:]
     o = pl.program_id(0)
 
     @pl.when(o == 0)
@@ -96,14 +98,14 @@
         a_ref[...] = a_in[...]
 
     c = (HD ** (-0.5)) * LOG2E
-    for j, kv_ref in enumerate((kv0_ref, kv1_ref)):
-        qi = tab_ref[2 * o + j]
+    for j, kv_ref in enumerate(kv_refs):
+        qi = tab_ref[PER_STEP * o + j]
 
         @pl.when(qi >= 0)
         def _():
             k = kv_ref[0, 0]
             if rotate_keys:
-                pos = pos_ref[2 * o + j]
+                pos = pos_ref[PER_STEP * o + j]
                 kf = k.astype(jnp.float32)
                 turned = pltpu.roll(kf, kf.shape[-1] // 2, 1)
                 k = (
@@ -131,7 +133,7 @@
 
 
 def attend_chunk(rotate_keys, tab, remap, pos, cos_tab, sin_tab, query_t, recv, m, l, acc):
-    owners = tab.shape[0] // 2
+    owners = tab.shape[0] // PER_STEP
     nq, hd, rows = query_t.shape
     plen = recv.shape[2]
     full3 = lambda shape: pl.BlockSpec(shape, lambda o, t, r, p: (0, 0, 0))
@@ -140,8 +142,14 @@
         grid=(owners,),
         in_specs=[
             full3((nq, hd, rows)),
-            pl.BlockSpec((1, 2, plen, hd), lambda o, t, r, p: (r[2 * o], 0, 0, 0)),
-            pl.BlockSpec((1, 2, plen, hd), lambda o, t, r, p: (r[2 * o + 1], 0, 0, 0)),
+        ]
+        + [
+            pl.BlockSpec(
+                (1, 2, plen, hd), lambda o, t, r, p, j=j: (r[PER_STEP * o + j], 0, 0, 0)
+            )
+            for j in range(PER_STEP)
+        ]
+        + [
             pl.BlockSpec(cos_tab.shape, lambda o, t, r, p: (0, 0)),
             pl.BlockSpec(sin_tab.shape, lambda o, t, r, p: (0, 0)),
             full3((nq, 1, rows)),
@@ -150,7 +158,7 @@
         ],
         out_specs=[full3((nq, 1, rows)), full3((nq, 1, rows)), full3((nq, hd, rows))],
     )
-    flops = 4 * nq * rows * plen * hd * owners
+    flops = 2 * nq * rows * plen * hd * owners * PER_STEP
     return pl.pallas_call(
         functools.partial(block_kernel, rotate_keys),
         grid_spec=grid_spec,
@@ -159,16 +167,16 @@
             jax.ShapeDtypeStruct(l.shape, jnp.float32),
             jax.ShapeDtypeStruct(acc.shape, jnp.float32),
         ],
-        input_output_aliases={8: 0, 9: 1, 10: 2},
+        input_output_aliases={6 + PER_STEP: 0, 7 + PER_STEP: 1, 8 + PER_STEP: 2},
         compiler_params=pltpu.CompilerParams(
             dimension_semantics=("arbitrary",), vmem_limit_bytes=48 * 1024 * 1024
         ),
         cost_estimate=pl.CostEstimate(
             flops=flops,
-            transcendentals=nq * rows * plen * owners,
+            transcendentals=nq * rows * plen * owners * PER_STEP // 2,
             bytes_accessed=recv.size * 2 + 2 * acc.size * 4,
         ),
-    )(tab, remap, pos, query_t, recv, recv, cos_tab, sin_tab, m, l, acc)
+    )(tab, remap, pos, query_t, *([recv] * PER_STEP), cos_tab, sin_tab, m, l, acc)
 
 
 def per_device(

time: 299 us -> 299 us (level)
  waiting for transfers between devices: 169 us -> 174 us
    all_to_all x2, waiting for transfers between devices: 164 us -> 168 us  [per_device(): lax.all_to_all(s, 'store', split_axis=0, concat_axis=0, tiled=True)]
  transfers between devices with their start and end apart: 6 -> 6, of which waited for: 3 -> 3; matrix products, arithmetic and copies ran while one was open for 12% -> 11% of each run, Pallas kernels for 12% -> 12%
where the time goes in v10:
time: 299 us; the launch traced here: 298 us
  waiting for transfers between devices  174 us (58%)
  Pallas kernels  51.3 us (17%)
  starting transfers between devices  25.1 us (8%)
  matrix products  18.3 us (6%)
  local copies, waits for them, and re-layouts  13 us (4%)
  other arithmetic  8.43 us (3%)
  between operations  8.18 us (3%)
    all_to_all x2, waiting for transfers between devices, per_device(): lax.all_to_all(s, 'store', split_axis=0, concat_axis=0, tiled=True)  168 us
    pallas_call x2, Pallas kernels, attend_chunk(): pl.pallas_call(functools.partial(block_kernel, rotate_keys), grid_spec=gr...  38.2 us
    pallas_call x2, Pallas kernels, build_send(): pl.pallas_call(functools.partial(send_kernel, slot), grid_spec=grid_spec,...  13 us
    all_to_all x2, starting transfers between devices, per_device(): lax.all_to_all(s, 'store', split_axis=0, concat_axis=0, tiled=True)  12.5 us
    dot_general x1, matrix products, per_device(): qf = jnp.dot(piece, w_query, preferred_element_type=jnp.float32)  11.8 us
    all_to_all x1, starting transfers between devices, per_device(): lax.all_to_all(request, 'store', split_axis=0, concat_axis=0, tiled=True)  7.53 us
  transfers between devices with their start and end apart: 6, of which 3 were waited for; matrix products, arithmetic and copies ran while one was open for 11% of the time, Pallas kernels for 12%

profile of v10, /device:TPU:40, one launch (start us, length us, event | category | flops | bytes accessed | tf_op | source)
XLA Modules:
  0.0 297.8 jit_solution(15954668748780138148)
XLA Ops:
  0.0 0.9 reshape.210
  2.9 7.5 %all-to-all-start = ((s32[32,2,2]{2,1,0:T(2,128)}), s32[32,2,2]{2,1,0:T(2,128)S(1)}, u32[]{:S(2)}, u32[]{:S(2)}) async-start(s32[32,2,2]{2,1,0:T(2,128)} %copy.37), calls=%async_computation | async-start | bytes 65536 | tf_op jit(solution)/shard_map/all_to_all | solution.py:216
  11.2 5.4 %all-to-all-done = s32[32,2,2]{2,1,0:T(2,128)S(1)} async-done(((s32[32,2,2]{2,1,0:T(2,128)}), s32[32,2,2]{2,1,0:T(2,128)S(1)}, u32[]{:S(2)}, u32[]{:S(2)}) %all-to-all-start) | async-done | bytes 544 | tf_op jit(solution)/shard_map/all_to_all | solution.py:216
  17.3 5.6 %shard_map.83 = bf16[32,2,512,128]{3,2,1,0:T(8,128)(2,1)} custom-call(s32[128]{0:T(128)} %reshape.215.req_ref, bf16[4,512,128]{2,1,0:T(8,128)(2,1)} %k_ref.3, bf16[4,512,128]{2,1,0:T(8,128)(2,1)} %v_ref.3, f32[16,128]{1,0:T(8,128)} %get-tuple-element.57.c_ref.refs_4_, f32[16,128]{1,0:T(8,128)} %get-tuple-element.58.s_ref.refs_5_), custom_call_target="tpu_custom_call" | custom-call | flops 8388608 | bytes 9437184 | tf_op jit(solution)/shard_map/pallas_call | solution.py:70
  22.8 6.1 %all-to-all-start.2 = ((bf16[32,2,512,128]{3,2,1,0:T(8,128)(2,1)}), bf16[32,2,512,128]{3,2,1,0:T(8,128)(2,1)}, u32[]{:S(2)}, u32[]{:S(2)}) async-start(bf16[32,2,512,128]{3,2,1,0:T(8,128)(2,1)} %shard_map.83), calls=%async_computation.2 | async-start | bytes 16777216 | tf_op jit(solution)/shard_map/all_to_all | solution.py:227
  29.0 2.0 collective-permute-start
  31.1 3.0 collective-permute-start.1
  34.1 7.5 %shard_map.82 = bf16[32,2,512,128]{3,2,1,0:T(8,128)(2,1)} custom-call(s32[128]{0:T(128)} %reshape.215.req_ref, bf16[4,512,128]{2,1,0:T(8,128)(2,1)} %k_ref.3, bf16[4,512,128]{2,1,0:T(8,128)(2,1)} %v_ref.3, f32[16,128]{1,0:T(8,128)} %get-tuple-element.57.c_ref.refs_4_, f32[16,128]{1,0:T(8,128)} %get-tuple-element.58.s_ref.refs_5_), custom_call_target="tpu_custom_call" | custom-call | flops 8388608 | bytes 9437184 | tf_op jit(solution)/shard_map/pallas_call | solution.py:70
  41.5 111.4 %all-to-all-done.2.refs_0_.refs_1_.refs_2_.refs_3_ = bf16[32,2,512,128]{3,2,1,0:T(8,128)(2,1)} async-done(((bf16[32,2,512,128]{3,2,1,0:T(8,128)(2,1)}), bf16[32,2,512,128]{3,2,1,0:T(8,128)(2,1)}, u32[]{:S(2)}, u32[]{:S(2)}) %all-to-all-start.2) | async-done | bytes 8388640 | tf_op jit(solution)/shard_map/all_to_all | solution.py:227
  153.0 6.4 %all-to-all-start.1 = ((bf16[32,2,512,128]{3,2,1,0:T(8,128)(2,1)}), bf16[32,2,512,128]{3,2,1,0:T(8,128)(2,1)}, u32[]{:S(2)}, u32[]{:S(2)}) async-start(bf16[32,2,512,128]{3,2,1,0:T(8,128)(2,1)} %shard_map.82), calls=%async_computation.1 | async-start | bytes 16777216 | tf_op jit(solution)/shard_map/all_to_all | solution.py:227
  159.4 1.6 sort.32
  161.0 1.6 sort.31
  174.6 2.1 pad_maximum_fusion
  177.1 11.8 %convolution_bitcast_fusion = f32[32,8,8,128]{3,1,2,0:T(8,128)S(1)} fusion(bf16[8192,1024]{1,0:T(8,128)(2,1)} %param.9, bf16[256,2048]{1,0:T(8,128)(2,1)S(1)} %get-tuple-element.28, bf16[256,2048]{1,0:T(8,128)(2,1)S(1)} %get-tuple-element.29, bf16[256,2048]{1,0:T(8,128)(2,1)S(1)} %get-tuple-element.30, bf16[256,2048]{1,0:T(8,128)(2,1)S(1)} %get-tuple-element.27), kind=kOutput, calls=%fused_computation.6 | convolution fusion | flops 4311744512 | bytes 22020096 | tf_op jit(solution)/shard_map/dot_general | solution.py:242
  190.3 1.0 copy.45.q_ref
  191.3 3.2 %fusion.26 = f32[256,128]{1,0:T(8,128)S(1)} fusion(bf16[8192,128]{1,0:T(8,128)(2,1)S(1)} %copy-done, bf16[256,2048]{1,0:T(8,128)(2,1)} %copy-done.8, bf16[256,2048]{1,0:T(8,128)(2,1)} %copy-done.10, bf16[256,2048]{1,0:T(8,128)(2,1)} %copy-done.12, bf16[256,2048]{1,0:T(8,128)(2,1)} %copy-done.6), kind=kOutput, calls=%fused_computation.96 | convolution fusion | flops 553648128 | bytes 6422528 | tf_op jit(solution)/shard_map/dot_general | solution.py:243
  195.4 1.4 convolution_convert_fusion
  196.9 1.4 fusion.3
  198.3 1.6 copy.46.refs_8_
  200.1 26.9 %shard_map.84 = (f32[2,1,1024]{2,1,0:T(1,128)S(1)}, f32[2,1,1024]{2,1,0:T(1,128)S(1)}, f32[2,128,1024]{2,1,0:T(8,128)S(1)}) custom-call(s32[32]{0:T(128)S(1)} %gather_fusion.2, s32[32]{0:T(128)S(1)} %reduce.1.remap_ref, s32[32]{0:T(128)S(1)} %gather_fusion.3, ...), custom_call_target="tpu_custom_call", output_to_operand_aliasing={{0}: (10, {}), {1}: (11, {}), {2}: (12, {})} | custom-call | flops 8589934592 | bytes 10485760 | tf_op jit(solution)/shard_map/pallas_call | solution.py:162
  227.0 56.8 %all-to-all-done.1.refs_0_.refs_1_.refs_2_.refs_3_ = bf16[32,2,512,128]{3,2,1,0:T(8,128)(2,1)} async-done(((bf16[32,2,512,128]{3,2,1,0:T(8,128)(2,1)}), bf16[32,2,512,128]{3,2,1,0:T(8,128)(2,1)}, u32[]{:S(2)}, u32[]{:S(2)}) %all-to-all-start.1) | async-done | bytes 8388640 | tf_op jit(solution)/shard_map/all_to_all | solution.py:227
  283.8 1.0 copy-done.3
  284.8 11.3 %shard_map.85 = (f32[2,1,1024]{2,1,0:T(1,128)S(1)}, f32[2,1,1024]{2,1,0:T(1,128)S(1)}, f32[2,128,1024]{2,1,0:T(8,128)S(1)}) custom-call(s32[16]{0:T(128)S(1)} %gather_fusion, s32[16]{0:T(128)S(1)} %reduce.remap_ref, s32[16]{0:T(128)S(1)} %gather_fusion.1, ...), custom_call_target="tpu_custom_call", output_to_operand_aliasing={{0}: (10, {}), {1}: (11, {}), {2}: (12, {})} | custom-call | flops 4294967296 | bytes 10485760 | tf_op jit(solution)/shard_map/pallas_call | solution.py:162
  296.9 0.9 copy.59
  (89 shorter events, 11.1 us)
Async XLA Ops:
  0.0 191.3 %copy-start = (bf16[8192,128]{1,0:T(8,128)(2,1)S(1)}, bf16[8192,128]{1,0:T(8,128)(2,1)}, u32[]{:S(2)}) copy-start(bf16[8192,128]{1,0:T(8,128)(2,1)} %param.10) | copy-start | bytes 6291460
  2.9 13.7 %all-to-all-start = ((s32[32,2,2]{2,1,0:T(2,128)}), s32[32,2,2]{2,1,0:T(2,128)S(1)}, u32[]{:S(2)}, u32[]{:S(2)}) async-start(s32[32,2,2]{2,1,0:T(2,128)} %copy.37), calls=%async_computation | async-start | bytes 65536 | tf_op jit(solution)/shard_map/all_to_all | solution.py:216
  22.8 6.1 %copy-start.14 = (bf16[256,2048]{1,0:T(8,128)(2,1)S(1)}, bf16[256,2048]{1,0:T(8,128)(2,1)}, u32[]{:S(2)}) copy-start(bf16[256,2048]{1,0:T(8,128)(2,1)} %param.8) | copy-start | bytes 3145732
  22.8 130.1 %all-to-all-start.2 = ((bf16[32,2,512,128]{3,2,1,0:T(8,128)(2,1)}), bf16[32,2,512,128]{3,2,1,0:T(8,128)(2,1)}, u32[]{:S(2)}, u32[]{:S(2)}) async-start(bf16[32,2,512,128]{3,2,1,0:T(8,128)(2,1)} %shard_map.83), calls=%async_computation.2 | async-start | bytes 16777216 | tf_op jit(solution)/shard_map/all_to_all | solution.py:227
  29.0 145.6 %collective-permute-start = (bf16[256,2048]{1,0:T(8,128)(2,1)S(1)}, bf16[256,2048]{1,0:T(8,128)(2,1)}, u32[]{:S(2)}, u32[]{:S(2)}) collective-permute-start(bf16[256,2048]{1,0:T(8,128)(2,1)S(1)} %copy-done.14), channel_id=1, source_target_pairs={{0,1},{1,2},{2,3},{3,0},{4,5},{5,6},{6,7},{7,4},{8,9},{9,10},{10,1... | collective-permute-start | bytes 3145736 | tf_op jit(solution)/shard_map/ppermute | solution.py:233
  31.0 143.6 %collective-permute-start.2 = (bf16[256,2048]{1,0:T(8,128)(2,1)S(1)}, bf16[256,2048]{1,0:T(8,128)(2,1)}, u32[]{:S(2)}, u32[]{:S(2)}) collective-permute-start(bf16[256,2048]{1,0:T(8,128)(2,1)S(1)} %copy-done.14), channel_id=1, source_target_pairs={{0,3},{1,0},{2,1},{3,2},{4,7},{5,4},{6,5},{7,6},{8,11},{9,8},{10,9... | collective-permute-start | bytes 3145736 | tf_op jit(solution)/shard_map/ppermute | solution.py:233
  31.1 143.5 %collective-permute-start.1 = (bf16[256,2048]{1,0:T(8,128)(2,1)S(1)}, bf16[256,2048]{1,0:T(8,128)(2,1)}, u32[]{:S(2)}, u32[]{:S(2)}) collective-permute-start(bf16[256,2048]{1,0:T(8,128)(2,1)S(1)} %copy-done.14), channel_id=1, source_target_pairs={{0,2},{1,3},{2,0},{3,1},{4,6},{5,7},{6,4},{7,5},{8,10},{9,11},{10,... | collective-permute-start | bytes 3145736 | tf_op jit(solution)/shard_map/ppermute | solution.py:233
  153.0 130.8 %all-to-all-start.1 = ((bf16[32,2,512,128]{3,2,1,0:T(8,128)(2,1)}), bf16[32,2,512,128]{3,2,1,0:T(8,128)(2,1)}, u32[]{:S(2)}, u32[]{:S(2)}) async-start(bf16[32,2,512,128]{3,2,1,0:T(8,128)(2,1)} %shard_map.82), calls=%async_computation.1 | async-start | bytes 16777216 | tf_op jit(solution)/shard_map/all_to_all | solution.py:227
  177.1 11.9 %copy-start.6 = (bf16[256,2048]{1,0:T(8,128)(2,1)}, bf16[256,2048]{1,0:T(8,128)(2,1)S(1)}, u32[]{:S(2)}) copy-start(bf16[256,2048]{1,0:T(8,128)(2,1)S(1)} %get-tuple-element.27) | copy-start | bytes 3145732
  177.1 11.9 %copy-start.8 = (bf16[256,2048]{1,0:T(8,128)(2,1)}, bf16[256,2048]{1,0:T(8,128)(2,1)S(1)}, u32[]{:S(2)}) copy-start(bf16[256,2048]{1,0:T(8,128)(2,1)S(1)} %get-tuple-element.28) | copy-start | bytes 3145732
  177.1 11.9 %copy-start.10 = (bf16[256,2048]{1,0:T(8,128)(2,1)}, bf16[256,2048]{1,0:T(8,128)(2,1)S(1)}, u32[]{:S(2)}) copy-start(bf16[256,2048]{1,0:T(8,128)(2,1)S(1)} %get-tuple-element.29) | copy-start | bytes 3145732
  177.1 11.9 %copy-start.12 = (bf16[256,2048]{1,0:T(8,128)(2,1)}, bf16[256,2048]{1,0:T(8,128)(2,1)S(1)}, u32[]{:S(2)}) copy-start(bf16[256,2048]{1,0:T(8,128)(2,1)S(1)} %get-tuple-element.30) | copy-start | bytes 3145732
  191.3 3.7 %copy-start.7 = (bf16[256,2048]{1,0:T(8,128)(2,1)S(1)}, bf16[256,2048]{1,0:T(8,128)(2,1)}, u32[]{:S(2)}) copy-start(bf16[256,2048]{1,0:T(8,128)(2,1)} %copy-done.6) | copy-start | bytes 3145732
  191.3 3.8 %copy-start.9 = (bf16[256,2048]{1,0:T(8,128)(2,1)S(1)}, bf16[256,2048]{1,0:T(8,128)(2,1)}, u32[]{:S(2)}) copy-start(bf16[256,2048]{1,0:T(8,128)(2,1)} %copy-done.8) | copy-start | bytes 3145732
  191.3 3.8 %copy-start.11 = (bf16[256,2048]{1,0:T(8,128)(2,1)S(1)}, bf16[256,2048]{1,0:T(8,128)(2,1)}, u32[]{:S(2)}) copy-start(bf16[256,2048]{1,0:T(8,128)(2,1)} %copy-done.10) | copy-start | bytes 3145732
  191.3 3.8 %copy-start.13 = (bf16[256,2048]{1,0:T(8,128)(2,1)S(1)}, bf16[256,2048]{1,0:T(8,128)(2,1)}, u32[]{:S(2)}) copy-start(bf16[256,2048]{1,0:T(8,128)(2,1)} %copy-done.12) | copy-start | bytes 3145732
  191.3 4.1 %copy-start.15 = (bf16[8192,128]{1,0:T(8,128)(2,1)S(1)}, bf16[8192,128]{1,0:T(8,128)(2,1)}, u32[]{:S(2)}) copy-start(bf16[8192,128]{1,0:T(8,128)(2,1)} %param.11) | copy-start | bytes 6291460
  196.8 3.2 %copy-start.2 = (bf16[2,128,1024]{2,1,0:T(8,128)(2,1)S(1)}, bf16[2,128,1024]{2,1,0:T(8,128)(2,1)}, u32[]{:S(2)}) copy-start(bf16[2,128,1024]{2,1,0:T(8,128)(2,1)} %copy.45.q_ref) | copy-start | bytes 1572868
  196.8 3.2 %copy-start.4 = (f32[16,128]{1,0:T(8,128)S(1)}, f32[16,128]{1,0:T(8,128)}, u32[]{:S(2)}) copy-start(f32[16,128]{1,0:T(8,128)} %get-tuple-element.57.c_ref.refs_4_) | copy-start | bytes 24580
  196.9 3.2 %copy-start.5 = (f32[16,128]{1,0:T(8,128)S(1)}, f32[16,128]{1,0:T(8,128)}, u32[]{:S(2)}) copy-start(f32[16,128]{1,0:T(8,128)} %get-tuple-element.58.s_ref.refs_5_) | copy-start | bytes 24580
  283.8 1.0 copy-start.3
  284.8 13.0 %copy-start.1 = (bf16[8192,128]{1,0:T(8,128)(2,1)S(1)}, bf16[8192,128]{1,0:T(8,128)(2,1)}, u32[]{:S(2)}) copy-start(bf16[8192,128]{1,0:T(8,128)(2,1)} %param.10) | copy-start | bytes 6291460

commit v11 on v10

--- a/solution.py
+++ b/solution.py
@@ -88,7 +88,7 @@
 
 def block_kernel(rotate_keys, tab_ref, remap_ref, pos_ref, q_ref, *refs):
     kv_refs = refs[:PER_STEP]
-    c_ref, s_ref, m_in, l_in, a_in, m_ref, l_ref, a_ref = refs[PER_STEP:]
+    c_ref, s_ref, m_in, l_in, a_in, m_ref, l_ref, a_ref, *out = refs[PER_STEP:]
     o = pl.program_id(0)
 
     @pl.when(o == 0)
@@ -131,8 +131,17 @@
                 a_ref[qi, :, cols] = w_old * a_ref[qi, :, cols] + w_new * p
                 m_ref[qi, :, cols] = m_new
 
-
-def attend_chunk(rotate_keys, tab, remap, pos, cos_tab, sin_tab, query_t, recv, m, l, acc):
+    if out:
+        (ctx_ref,) = out
+
+        @pl.when(o == pl.num_programs(0) - 1)
+        def _():
+            ctx_ref[...] = (a_ref[...] / l_ref[...]).astype(ctx_ref.dtype)
+
+
+def attend_chunk(
+    rotate_keys, tab, remap, pos, cos_tab, sin_tab, query_t, recv, m, l, acc, final=False
+):
     owners = tab.shape[0] // PER_STEP
     nq, hd, rows = query_t.shape
     plen = recv.shape[2]
@@ -156,7 +165,8 @@
             full3((nq, 1, rows)),
             full3((nq, hd, rows)),
         ],
-        out_specs=[full3((nq, 1, rows)), full3((nq, 1, rows)), full3((nq, hd, rows))],
+        out_specs=[full3((nq, 1, rows)), full3((nq, 1, rows)), full3((nq, hd, rows))]
+        + ([full3((nq, hd, rows))] if final else []),
     )
     flops = 2 * nq * rows * plen * hd * owners * PER_STEP
     return pl.pallas_call(
@@ -166,7 +176,8 @@
             jax.ShapeDtypeStruct(m.shape, jnp.float32),
             jax.ShapeDtypeStruct(l.shape, jnp.float32),
             jax.ShapeDtypeStruct(acc.shape, jnp.float32),
-        ],
+        ]
+        + ([jax.ShapeDtypeStruct(acc.shape, jnp.bfloat16)] if final else []),
         input_output_aliases={6 + PER_STEP: 0, 7 + PER_STEP: 1, 8 + PER_STEP: 2},
         compiler_params=pltpu.CompilerParams(
             dimension_semantics=("arbitrary",), vmem_limit_bytes=48 * 1024 * 1024
@@ -280,13 +291,14 @@
         pos = jnp.sum(hit * my_pos[:, None], axis=0)[order]
         tab = tab[order]
         remap = lax.cummax(jnp.where(tab >= 0, order, 0), axis=0)
-        m, l, acc = attend_chunk(
-            c == 0, tab, remap, pos, cos_tab, sin_tab, query_t, recvs[c], m, l, acc
+        outs = attend_chunk(
+            c == 0, tab, remap, pos, cos_tab, sin_tab, query_t, recvs[c], m, l, acc,
+            final=c == CAP - 1,
         )
-
-    ctx = (acc / l).reshape(count, HD, q_heads, QLEN)
-    ctx = jnp.transpose(ctx, (0, 3, 2, 1)).reshape(tok_rows, q_heads * HD)
-    return ctx.astype(jnp.bfloat16)
+        m, l, acc = outs[:3]
+
+    ctx = outs[3].reshape(count, HD, q_heads, QLEN)
+    return jnp.transpose(ctx, (0, 3, 2, 1)).reshape(tok_rows, q_heads * HD)
 
 
 def solution(mesh):

time: 299 us -> 299 us (level)
  no operation moved by 1% of the time
where the time goes in v11:
time: 299 us; the launch traced here: 298 us
  waiting for transfers between devices  174 us (58%)
  Pallas kernels  51.4 us (17%)
  starting transfers between devices  25.1 us (8%)
  matrix products  18.2 us (6%)
  local copies, waits for them, and re-layouts  13 us (4%)
  other arithmetic  8.33 us (3%)
  between operations  8.16 us (3%)
    all_to_all x2, waiting for transfers between devices, per_device(): lax.all_to_all(s, 'store', split_axis=0, concat_axis=0, tiled=True)  168 us
    pallas_call x2, Pallas kernels, attend_chunk(): pl.pallas_call(functools.partial(block_kernel, rotate_keys), grid_spec=gr...  38.4 us
    pallas_call x2, Pallas kernels, build_send(): pl.pallas_call(functools.partial(send_kernel, slot), grid_spec=grid_spec,...  13 us
    all_to_all x2, starting transfers between devices, per_device(): lax.all_to_all(s, 'store', split_axis=0, concat_axis=0, tiled=True)  12.5 us
    dot_general x1, matrix products, per_device(): qf = jnp.dot(piece, w_query, preferred_element_type=jnp.float32)  11.7 us
    all_to_all x1, starting transfers between devices, per_device(): lax.all_to_all(request, 'store', split_axis=0, concat_axis=0, tiled=True)  7.53 us
  transfers between devices with their start and end apart: 6, of which 3 were waited for; matrix products, arithmetic and copies ran while one was open for 11% of the time, Pallas kernels for 12%

profile of v11, /device:TPU:40, one launch (start us, length us, event | category | flops | bytes accessed | tf_op | source)
XLA Modules:
  0.0 297.8 jit_solution(17872764753633329607)
XLA Ops:
  0.0 0.9 reshape.212
  2.9 7.5 %all-to-all-start = ((s32[32,2,2]{2,1,0:T(2,128)}), s32[32,2,2]{2,1,0:T(2,128)S(1)}, u32[]{:S(2)}, u32[]{:S(2)}) async-start(s32[32,2,2]{2,1,0:T(2,128)} %copy.37), calls=%async_computation | async-start | bytes 65536 | tf_op jit(solution)/shard_map/all_to_all | solution.py:227
  11.2 5.4 %all-to-all-done = s32[32,2,2]{2,1,0:T(2,128)S(1)} async-done(((s32[32,2,2]{2,1,0:T(2,128)}), s32[32,2,2]{2,1,0:T(2,128)S(1)}, u32[]{:S(2)}, u32[]{:S(2)}) %all-to-all-start) | async-done | bytes 544 | tf_op jit(solution)/shard_map/all_to_all | solution.py:227
  17.3 5.6 %shard_map.83 = bf16[32,2,512,128]{3,2,1,0:T(8,128)(2,1)} custom-call(s32[128]{0:T(128)} %reshape.217.req_ref, bf16[4,512,128]{2,1,0:T(8,128)(2,1)} %k_ref.3, bf16[4,512,128]{2,1,0:T(8,128)(2,1)} %v_ref.3, f32[16,128]{1,0:T(8,128)} %get-tuple-element.55.c_ref.refs_4_, f32[16,128]{1,0:T(8,128)} %get-tuple-element.56.s_ref.refs_5_), custom_call_target="tpu_custom_call" | custom-call | flops 8388608 | bytes 9437184 | tf_op jit(solution)/shard_map/pallas_call | solution.py:70
  22.8 6.1 %all-to-all-start.2 = ((bf16[32,2,512,128]{3,2,1,0:T(8,128)(2,1)}), bf16[32,2,512,128]{3,2,1,0:T(8,128)(2,1)}, u32[]{:S(2)}, u32[]{:S(2)}) async-start(bf16[32,2,512,128]{3,2,1,0:T(8,128)(2,1)} %shard_map.83), calls=%async_computation.2 | async-start | bytes 16777216 | tf_op jit(solution)/shard_map/all_to_all | solution.py:238
  29.0 2.0 collective-permute-start
  31.1 3.0 collective-permute-start.1
  34.1 7.5 %shard_map.82 = bf16[32,2,512,128]{3,2,1,0:T(8,128)(2,1)} custom-call(s32[128]{0:T(128)} %reshape.217.req_ref, bf16[4,512,128]{2,1,0:T(8,128)(2,1)} %k_ref.3, bf16[4,512,128]{2,1,0:T(8,128)(2,1)} %v_ref.3, f32[16,128]{1,0:T(8,128)} %get-tuple-element.55.c_ref.refs_4_, f32[16,128]{1,0:T(8,128)} %get-tuple-element.56.s_ref.refs_5_), custom_call_target="tpu_custom_call" | custom-call | flops 8388608 | bytes 9437184 | tf_op jit(solution)/shard_map/pallas_call | solution.py:70
  41.5 111.4 %all-to-all-done.2.refs_0_.refs_1_.refs_2_.refs_3_ = bf16[32,2,512,128]{3,2,1,0:T(8,128)(2,1)} async-done(((bf16[32,2,512,128]{3,2,1,0:T(8,128)(2,1)}), bf16[32,2,512,128]{3,2,1,0:T(8,128)(2,1)}, u32[]{:S(2)}, u32[]{:S(2)}) %all-to-all-start.2) | async-done | bytes 8388640 | tf_op jit(solution)/shard_map/all_to_all | solution.py:238
  153.0 6.4 %all-to-all-start.1 = ((bf16[32,2,512,128]{3,2,1,0:T(8,128)(2,1)}), bf16[32,2,512,128]{3,2,1,0:T(8,128)(2,1)}, u32[]{:S(2)}, u32[]{:S(2)}) async-start(bf16[32,2,512,128]{3,2,1,0:T(8,128)(2,1)} %shard_map.82), calls=%async_computation.1 | async-start | bytes 16777216 | tf_op jit(solution)/shard_map/all_to_all | solution.py:238
  159.4 1.6 sort.32
  161.0 1.6 sort.31
  174.6 2.1 pad_maximum_fusion
  177.1 11.7 %convolution_bitcast_fusion = f32[32,8,8,128]{3,1,2,0:T(8,128)S(1)} fusion(bf16[8192,1024]{1,0:T(8,128)(2,1)} %param.9, bf16[256,2048]{1,0:T(8,128)(2,1)S(1)} %get-tuple-element.26, bf16[256,2048]{1,0:T(8,128)(2,1)S(1)} %get-tuple-element.27, bf16[256,2048]{1,0:T(8,128)(2,1)S(1)} %get-tuple-element.28, bf16[256,2048]{1,0:T(8,128)(2,1)S(1)} %get-tuple-element.25), kind=kOutput, calls=%fused_computation.6 | convolution fusion | flops 4311744512 | bytes 22020096 | tf_op jit(solution)/shard_map/dot_general | solution.py:253
  190.2 1.0 copy.45.q_ref
  191.2 3.2 %fusion.26 = f32[256,128]{1,0:T(8,128)S(1)} fusion(bf16[8192,128]{1,0:T(8,128)(2,1)S(1)} %copy-done, bf16[256,2048]{1,0:T(8,128)(2,1)} %copy-done.8, bf16[256,2048]{1,0:T(8,128)(2,1)} %copy-done.10, bf16[256,2048]{1,0:T(8,128)(2,1)} %copy-done.12, bf16[256,2048]{1,0:T(8,128)(2,1)} %copy-done.6), kind=kOutput, calls=%fused_computation.94 | convolution fusion | flops 553648128 | bytes 6422528 | tf_op jit(solution)/shard_map/dot_general | solution.py:254
  195.3 1.4 convolution_convert_fusion
  196.8 1.4 fusion.3
  198.2 1.6 copy.46.refs_8_
  200.0 26.9 %shard_map.84 = (f32[2,1,1024]{2,1,0:T(1,128)S(1)}, f32[2,1,1024]{2,1,0:T(1,128)S(1)}, f32[2,128,1024]{2,1,0:T(8,128)S(1)}) custom-call(s32[32]{0:T(128)S(1)} %gather_fusion.2, s32[32]{0:T(128)S(1)} %reduce.1.remap_ref, s32[32]{0:T(128)S(1)} %gather_fusion.3, ...), custom_call_target="tpu_custom_call", output_to_operand_aliasing={{0}: (10, {}), {1}: (11, {}), {2}: (12, {})} | custom-call | flops 8589934592 | bytes 10485760 | tf_op jit(solution)/shard_map/pallas_call | solution.py:172
  226.9 56.9 %all-to-all-done.1.refs_0_.refs_1_.refs_2_.refs_3_ = bf16[32,2,512,128]{3,2,1,0:T(8,128)(2,1)} async-done(((bf16[32,2,512,128]{3,2,1,0:T(8,128)(2,1)}), bf16[32,2,512,128]{3,2,1,0:T(8,128)(2,1)}, u32[]{:S(2)}, u32[]{:S(2)}) %all-to-all-start.1) | async-done | bytes 8388640 | tf_op jit(solution)/shard_map/all_to_all | solution.py:238
  283.8 1.0 copy-done.3
  284.8 11.5 %shard_map.85 = (f32[2,1,1024]{2,1,0:T(1,128)S(1)}, f32[2,1,1024]{2,1,0:T(1,128)S(1)}, f32[2,128,1024]{2,1,0:T(8,128)S(1)}, bf16[2,128,1024]{2,1,0:T(8,128)(2,1)S(1)}) custom-call(s32[16]{0:T(128)S(1)} %gather_fusion, s32[16]{0:T(128)S(1)} %reduce.remap_ref, s32[16]{0:T(128)S(1)} %gather_fusion.1, ...), custom_call_target="tpu_custom_call", output_to_operand_aliasing={{0}: (10, {}), {1}: (11, {}), {2}: (12, {})} | custom-call | flops 4294967296 | bytes 10485760 | tf_op jit(solution)/shard_map/pallas_call | solution.py:172
  296.9 0.9 copy.57
  (87 shorter events, 11.0 us)
Async XLA Ops:
  0.0 191.2 %copy-start = (bf16[8192,128]{1,0:T(8,128)(2,1)S(1)}, bf16[8192,128]{1,0:T(8,128)(2,1)}, u32[]{:S(2)}) copy-start(bf16[8192,128]{1,0:T(8,128)(2,1)} %param.10) | copy-start | bytes 6291460
  2.9 13.7 %all-to-all-start = ((s32[32,2,2]{2,1,0:T(2,128)}), s32[32,2,2]{2,1,0:T(2,128)S(1)}, u32[]{:S(2)}, u32[]{:S(2)}) async-start(s32[32,2,2]{2,1,0:T(2,128)} %copy.37), calls=%async_computation | async-start | bytes 65536 | tf_op jit(solution)/shard_map/all_to_all | solution.py:227
  22.8 6.1 %copy-start.14 = (bf16[256,2048]{1,0:T(8,128)(2,1)S(1)}, bf16[256,2048]{1,0:T(8,128)(2,1)}, u32[]{:S(2)}) copy-start(bf16[256,2048]{1,0:T(8,128)(2,1)} %param.8) | copy-start | bytes 3145732
  22.8 130.1 %all-to-all-start.2 = ((bf16[32,2,512,128]{3,2,1,0:T(8,128)(2,1)}), bf16[32,2,512,128]{3,2,1,0:T(8,128)(2,1)}, u32[]{:S(2)}, u32[]{:S(2)}) async-start(bf16[32,2,512,128]{3,2,1,0:T(8,128)(2,1)} %shard_map.83), calls=%async_computation.2 | async-start | bytes 16777216 | tf_op jit(solution)/shard_map/all_to_all | solution.py:238
  29.0 145.6 %collective-permute-start = (bf16[256,2048]{1,0:T(8,128)(2,1)S(1)}, bf16[256,2048]{1,0:T(8,128)(2,1)}, u32[]{:S(2)}, u32[]{:S(2)}) collective-permute-start(bf16[256,2048]{1,0:T(8,128)(2,1)S(1)} %copy-done.14), channel_id=1, source_target_pairs={{0,1},{1,2},{2,3},{3,0},{4,5},{5,6},{6,7},{7,4},{8,9},{9,10},{10,1... | collective-permute-start | bytes 3145736 | tf_op jit(solution)/shard_map/ppermute | solution.py:244
  31.0 143.6 %collective-permute-start.2 = (bf16[256,2048]{1,0:T(8,128)(2,1)S(1)}, bf16[256,2048]{1,0:T(8,128)(2,1)}, u32[]{:S(2)}, u32[]{:S(2)}) collective-permute-start(bf16[256,2048]{1,0:T(8,128)(2,1)S(1)} %copy-done.14), channel_id=1, source_target_pairs={{0,3},{1,0},{2,1},{3,2},{4,7},{5,4},{6,5},{7,6},{8,11},{9,8},{10,9... | collective-permute-start | bytes 3145736 | tf_op jit(solution)/shard_map/ppermute | solution.py:244
  31.1 143.5 %collective-permute-start.1 = (bf16[256,2048]{1,0:T(8,128)(2,1)S(1)}, bf16[256,2048]{1,0:T(8,128)(2,1)}, u32[]{:S(2)}, u32[]{:S(2)}) collective-permute-start(bf16[256,2048]{1,0:T(8,128)(2,1)S(1)} %copy-done.14), channel_id=1, source_target_pairs={{0,2},{1,3},{2,0},{3,1},{4,6},{5,7},{6,4},{7,5},{8,10},{9,11},{10,... | collective-permute-start | bytes 3145736 | tf_op jit(solution)/shard_map/ppermute | solution.py:244
  153.0 130.8 %all-to-all-start.1 = ((bf16[32,2,512,128]{3,2,1,0:T(8,128)(2,1)}), bf16[32,2,512,128]{3,2,1,0:T(8,128)(2,1)}, u32[]{:S(2)}, u32[]{:S(2)}) async-start(bf16[32,2,512,128]{3,2,1,0:T(8,128)(2,1)} %shard_map.82), calls=%async_computation.1 | async-start | bytes 16777216 | tf_op jit(solution)/shard_map/all_to_all | solution.py:238
  177.1 11.8 %copy-start.6 = (bf16[256,2048]{1,0:T(8,128)(2,1)}, bf16[256,2048]{1,0:T(8,128)(2,1)S(1)}, u32[]{:S(2)}) copy-start(bf16[256,2048]{1,0:T(8,128)(2,1)S(1)} %get-tuple-element.25) | copy-start | bytes 3145732
  177.1 11.8 %copy-start.8 = (bf16[256,2048]{1,0:T(8,128)(2,1)}, bf16[256,2048]{1,0:T(8,128)(2,1)S(1)}, u32[]{:S(2)}) copy-start(bf16[256,2048]{1,0:T(8,128)(2,1)S(1)} %get-tuple-element.26) | copy-start | bytes 3145732
  177.1 11.8 %copy-start.10 = (bf16[256,2048]{1,0:T(8,128)(2,1)}, bf16[256,2048]{1,0:T(8,128)(2,1)S(1)}, u32[]{:S(2)}) copy-start(bf16[256,2048]{1,0:T(8,128)(2,1)S(1)} %get-tuple-element.27) | copy-start | bytes 3145732
  177.1 11.8 %copy-start.12 = (bf16[256,2048]{1,0:T(8,128)(2,1)}, bf16[256,2048]{1,0:T(8,128)(2,1)S(1)}, u32[]{:S(2)}) copy-start(bf16[256,2048]{1,0:T(8,128)(2,1)S(1)} %get-tuple-element.28) | copy-start | bytes 3145732
  191.2 3.7 %copy-start.7 = (bf16[256,2048]{1,0:T(8,128)(2,1)S(1)}, bf16[256,2048]{1,0:T(8,128)(2,1)}, u32[]{:S(2)}) copy-start(bf16[256,2048]{1,0:T(8,128)(2,1)} %copy-done.6) | copy-start | bytes 3145732
  191.2 3.8 %copy-start.9 = (bf16[256,2048]{1,0:T(8,128)(2,1)S(1)}, bf16[256,2048]{1,0:T(8,128)(2,1)}, u32[]{:S(2)}) copy-start(bf16[256,2048]{1,0:T(8,128)(2,1)} %copy-done.8) | copy-start | bytes 3145732
  191.2 3.8 %copy-start.11 = (bf16[256,2048]{1,0:T(8,128)(2,1)S(1)}, bf16[256,2048]{1,0:T(8,128)(2,1)}, u32[]{:S(2)}) copy-start(bf16[256,2048]{1,0:T(8,128)(2,1)} %copy-done.10) | copy-start | bytes 3145732
  191.2 3.8 %copy-start.13 = (bf16[256,2048]{1,0:T(8,128)(2,1)S(1)}, bf16[256,2048]{1,0:T(8,128)(2,1)}, u32[]{:S(2)}) copy-start(bf16[256,2048]{1,0:T(8,128)(2,1)} %copy-done.12) | copy-start | bytes 3145732
  191.2 4.1 %copy-start.15 = (bf16[8192,128]{1,0:T(8,128)(2,1)S(1)}, bf16[8192,128]{1,0:T(8,128)(2,1)}, u32[]{:S(2)}) copy-start(bf16[8192,128]{1,0:T(8,128)(2,1)} %param.11) | copy-start | bytes 6291460
  196.7 3.2 %copy-start.2 = (bf16[2,128,1024]{2,1,0:T(8,128)(2,1)S(1)}, bf16[2,128,1024]{2,1,0:T(8,128)(2,1)}, u32[]{:S(2)}) copy-start(bf16[2,128,1024]{2,1,0:T(8,128)(2,1)} %copy.45.q_ref) | copy-start | bytes 1572868
  196.7 3.2 %copy-start.4 = (f32[16,128]{1,0:T(8,128)S(1)}, f32[16,128]{1,0:T(8,128)}, u32[]{:S(2)}) copy-start(f32[16,128]{1,0:T(8,128)} %get-tuple-element.55.c_ref.refs_4_) | copy-start | bytes 24580
  196.7 3.2 %copy-start.5 = (f32[16,128]{1,0:T(8,128)S(1)}, f32[16,128]{1,0:T(8,128)}, u32[]{:S(2)}) copy-start(f32[16,128]{1,0:T(8,128)} %get-tuple-element.56.s_ref.refs_5_) | copy-start | bytes 24580
  283.8 1.0 copy-start.3
  284.8 13.0 %copy-start.1 = (bf16[8192,128]{1,0:T(8,128)(2,1)S(1)}, bf16[8192,128]{1,0:T(8,128)(2,1)}, u32[]{:S(2)}) copy-start(bf16[8192,128]{1,0:T(8,128)(2,1)} %param.10) | copy-start | bytes 6291460

commit v12 on v11

--- a/solution.py
+++ b/solution.py
@@ -54,7 +54,7 @@
 def build_send(slot, req, cos_tab, sin_tab, passage_keys, passage_values):
     owners = req.shape[0] // (CAP * 2)
     stored, plen, hd = passage_keys.shape
-    per = 8
+    per = 16 if slot == 0 else 8
     full = lambda shape: pl.BlockSpec(shape, lambda i, req: (0,) * len(shape))
     grid_spec = pltpu.PrefetchScalarGridSpec(
         num_scalar_prefetch=1,

time: 299 us -> 299 us (level)
  no operation moved by 1% of the time
where the time goes in v12:
time: 299 us; the launch traced here: 297 us
  waiting for transfers between devices  173 us (58%)
  Pallas kernels  51.4 us (17%)
  starting transfers between devices  25.1 us (8%)
  matrix products  18.2 us (6%)
  local copies, waits for them, and re-layouts  13 us (4%)
  other arithmetic  8.33 us (3%)
  between operations  8.16 us (3%)
    all_to_all x2, waiting for transfers between devices, per_device(): lax.all_to_all(s, 'store', split_axis=0, concat_axis=0, tiled=True)  167 us
    pallas_call x2, Pallas kernels, attend_chunk(): pl.pallas_call(functools.partial(block_kernel, rotate_keys), grid_spec=gr...  38.4 us
    pallas_call x2, Pallas kernels, build_send(): pl.pallas_call(functools.partial(send_kernel, slot), grid_spec=grid_spec,...  12.9 us
    all_to_all x2, starting transfers between devices, per_device(): lax.all_to_all(s, 'store', split_axis=0, concat_axis=0, tiled=True)  12.5 us
    dot_general x1, matrix products, per_device(): qf = jnp.dot(piece, w_query, preferred_element_type=jnp.float32)  11.7 us
    all_to_all x1, starting transfers between devices, per_device(): lax.all_to_all(request, 'store', split_axis=0, concat_axis=0, tiled=True)  7.53 us
  transfers between devices with their start and end apart: 6, of which 3 were waited for; matrix products, arithmetic and copies ran while one was open for 11% of the time, Pallas kernels for 12%

profile of v12, /device:TPU:40, one launch (start us, length us, event | category | flops | bytes accessed | tf_op | source)
XLA Modules:
  0.0 296.7 jit_solution(2497685918289013111)
XLA Ops:
  0.0 0.9 reshape.212
  2.9 7.5 %all-to-all-start = ((s32[32,2,2]{2,1,0:T(2,128)}), s32[32,2,2]{2,1,0:T(2,128)S(1)}, u32[]{:S(2)}, u32[]{:S(2)}) async-start(s32[32,2,2]{2,1,0:T(2,128)} %copy.37), calls=%async_computation | async-start | bytes 65536 | tf_op jit(solution)/shard_map/all_to_all | solution.py:227
  11.2 5.4 %all-to-all-done = s32[32,2,2]{2,1,0:T(2,128)S(1)} async-done(((s32[32,2,2]{2,1,0:T(2,128)}), s32[32,2,2]{2,1,0:T(2,128)S(1)}, u32[]{:S(2)}, u32[]{:S(2)}) %all-to-all-start) | async-done | bytes 544 | tf_op jit(solution)/shard_map/all_to_all | solution.py:227
  17.3 5.5 %shard_map.83 = bf16[32,2,512,128]{3,2,1,0:T(8,128)(2,1)} custom-call(s32[128]{0:T(128)} %reshape.217.req_ref, bf16[4,512,128]{2,1,0:T(8,128)(2,1)} %k_ref.3, bf16[4,512,128]{2,1,0:T(8,128)(2,1)} %v_ref.3, f32[16,128]{1,0:T(8,128)} %get-tuple-element.55.c_ref.refs_4_, f32[16,128]{1,0:T(8,128)} %get-tuple-element.56.s_ref.refs_5_), custom_call_target="tpu_custom_call" | custom-call | flops 8388608 | bytes 9437184 | tf_op jit(solution)/shard_map/pallas_call | solution.py:70
  22.8 6.1 %all-to-all-start.2 = ((bf16[32,2,512,128]{3,2,1,0:T(8,128)(2,1)}), bf16[32,2,512,128]{3,2,1,0:T(8,128)(2,1)}, u32[]{:S(2)}, u32[]{:S(2)}) async-start(bf16[32,2,512,128]{3,2,1,0:T(8,128)(2,1)} %shard_map.83), calls=%async_computation.2 | async-start | bytes 16777216 | tf_op jit(solution)/shard_map/all_to_all | solution.py:238
  28.9 2.0 collective-permute-start
  31.0 3.0 %collective-permute-start.1 = (bf16[256,2048]{1,0:T(8,128)(2,1)S(1)}, bf16[256,2048]{1,0:T(8,128)(2,1)}, u32[]{:S(2)}, u32[]{:S(2)}) collective-permute-start(bf16[256,2048]{1,0:T(8,128)(2,1)S(1)} %copy-done.14), channel_id=1, source_target_pairs={{0,2},{1,3},{2,0},{3,1},{4,6},{5,7},{6,4},{7,5},{8,10},{9,11},{10,... | collective-permute-start | bytes 3145736 | tf_op jit(solution)/shard_map/ppermute | solution.py:244
  34.0 7.5 %shard_map.82 = bf16[32,2,512,128]{3,2,1,0:T(8,128)(2,1)} custom-call(s32[128]{0:T(128)} %reshape.217.req_ref, bf16[4,512,128]{2,1,0:T(8,128)(2,1)} %k_ref.3, bf16[4,512,128]{2,1,0:T(8,128)(2,1)} %v_ref.3, f32[16,128]{1,0:T(8,128)} %get-tuple-element.55.c_ref.refs_4_, f32[16,128]{1,0:T(8,128)} %get-tuple-element.56.s_ref.refs_5_), custom_call_target="tpu_custom_call" | custom-call | flops 8388608 | bytes 9437184 | tf_op jit(solution)/shard_map/pallas_call | solution.py:70
  41.4 111.4 %all-to-all-done.2.refs_0_.refs_1_.refs_2_.refs_3_ = bf16[32,2,512,128]{3,2,1,0:T(8,128)(2,1)} async-done(((bf16[32,2,512,128]{3,2,1,0:T(8,128)(2,1)}), bf16[32,2,512,128]{3,2,1,0:T(8,128)(2,1)}, u32[]{:S(2)}, u32[]{:S(2)}) %all-to-all-start.2) | async-done | bytes 8388640 | tf_op jit(solution)/shard_map/all_to_all | solution.py:238
  152.9 6.4 %all-to-all-start.1 = ((bf16[32,2,512,128]{3,2,1,0:T(8,128)(2,1)}), bf16[32,2,512,128]{3,2,1,0:T(8,128)(2,1)}, u32[]{:S(2)}, u32[]{:S(2)}) async-start(bf16[32,2,512,128]{3,2,1,0:T(8,128)(2,1)} %shard_map.82), calls=%async_computation.1 | async-start | bytes 16777216 | tf_op jit(solution)/shard_map/all_to_all | solution.py:238
  159.3 1.6 sort.32
  160.9 1.6 sort.31
  174.5 2.1 pad_maximum_fusion
  177.0 11.7 %convolution_bitcast_fusion = f32[32,8,8,128]{3,1,2,0:T(8,128)S(1)} fusion(bf16[8192,1024]{1,0:T(8,128)(2,1)} %param.9, bf16[256,2048]{1,0:T(8,128)(2,1)S(1)} %get-tuple-element.26, bf16[256,2048]{1,0:T(8,128)(2,1)S(1)} %get-tuple-element.27, bf16[256,2048]{1,0:T(8,128)(2,1)S(1)} %get-tuple-element.28, bf16[256,2048]{1,0:T(8,128)(2,1)S(1)} %get-tuple-element.25), kind=kOutput, calls=%fused_computation.6 | convolution fusion | flops 4311744512 | bytes 22020096 | tf_op jit(solution)/shard_map/dot_general | solution.py:253
  190.1 1.0 copy.45.q_ref
  191.1 3.2 %fusion.26 = f32[256,128]{1,0:T(8,128)S(1)} fusion(bf16[8192,128]{1,0:T(8,128)(2,1)S(1)} %copy-done, bf16[256,2048]{1,0:T(8,128)(2,1)} %copy-done.8, bf16[256,2048]{1,0:T(8,128)(2,1)} %copy-done.10, bf16[256,2048]{1,0:T(8,128)(2,1)} %copy-done.12, bf16[256,2048]{1,0:T(8,128)(2,1)} %copy-done.6), kind=kOutput, calls=%fused_computation.94 | convolution fusion | flops 553648128 | bytes 6422528 | tf_op jit(solution)/shard_map/dot_general | solution.py:254
  195.2 1.4 convolution_convert_fusion
  196.7 1.4 fusion.3
  198.1 1.6 copy.46.refs_8_
  199.9 28.0 %shard_map.84 = (f32[2,1,1024]{2,1,0:T(1,128)S(1)}, f32[2,1,1024]{2,1,0:T(1,128)S(1)}, f32[2,128,1024]{2,1,0:T(8,128)S(1)}) custom-call(s32[32]{0:T(128)S(1)} %gather_fusion.2, s32[32]{0:T(128)S(1)} %reduce.1.remap_ref, s32[32]{0:T(128)S(1)} %gather_fusion.3, ...), custom_call_target="tpu_custom_call", output_to_operand_aliasing={{0}: (10, {}), {1}: (11, {}), {2}: (12, {})} | custom-call | flops 8589934592 | bytes 10485760 | tf_op jit(solution)/shard_map/pallas_call | solution.py:172
  227.9 55.8 %all-to-all-done.1.refs_0_.refs_1_.refs_2_.refs_3_ = bf16[32,2,512,128]{3,2,1,0:T(8,128)(2,1)} async-done(((bf16[32,2,512,128]{3,2,1,0:T(8,128)(2,1)}), bf16[32,2,512,128]{3,2,1,0:T(8,128)(2,1)}, u32[]{:S(2)}, u32[]{:S(2)}) %all-to-all-start.1) | async-done | bytes 8388640 | tf_op jit(solution)/shard_map/all_to_all | solution.py:238
  283.7 1.0 copy-done.3
  284.8 10.5 %shard_map.85 = (f32[2,1,1024]{2,1,0:T(1,128)S(1)}, f32[2,1,1024]{2,1,0:T(1,128)S(1)}, f32[2,128,1024]{2,1,0:T(8,128)S(1)}, bf16[2,128,1024]{2,1,0:T(8,128)(2,1)S(1)}) custom-call(s32[16]{0:T(128)S(1)} %gather_fusion, s32[16]{0:T(128)S(1)} %reduce.remap_ref, s32[16]{0:T(128)S(1)} %gather_fusion.1, ...), custom_call_target="tpu_custom_call", output_to_operand_aliasing={{0}: (10, {}), {1}: (11, {}), {2}: (12, {})} | custom-call | flops 4294967296 | bytes 10485760 | tf_op jit(solution)/shard_map/pallas_call | solution.py:172
  295.8 0.9 copy.57
  (87 shorter events, 11.0 us)
Async XLA Ops:
  0.0 191.1 %copy-start = (bf16[8192,128]{1,0:T(8,128)(2,1)S(1)}, bf16[8192,128]{1,0:T(8,128)(2,1)}, u32[]{:S(2)}) copy-start(bf16[8192,128]{1,0:T(8,128)(2,1)} %param.10) | copy-start | bytes 6291460
  2.9 13.7 %all-to-all-start = ((s32[32,2,2]{2,1,0:T(2,128)}), s32[32,2,2]{2,1,0:T(2,128)S(1)}, u32[]{:S(2)}, u32[]{:S(2)}) async-start(s32[32,2,2]{2,1,0:T(2,128)} %copy.37), calls=%async_computation | async-start | bytes 65536 | tf_op jit(solution)/shard_map/all_to_all | solution.py:227
  22.8 6.1 %copy-start.14 = (bf16[256,2048]{1,0:T(8,128)(2,1)S(1)}, bf16[256,2048]{1,0:T(8,128)(2,1)}, u32[]{:S(2)}) copy-start(bf16[256,2048]{1,0:T(8,128)(2,1)} %param.8) | copy-start | bytes 3145732
  22.8 130.1 %all-to-all-start.2 = ((bf16[32,2,512,128]{3,2,1,0:T(8,128)(2,1)}), bf16[32,2,512,128]{3,2,1,0:T(8,128)(2,1)}, u32[]{:S(2)}, u32[]{:S(2)}) async-start(bf16[32,2,512,128]{3,2,1,0:T(8,128)(2,1)} %shard_map.83), calls=%async_computation.2 | async-start | bytes 16777216 | tf_op jit(solution)/shard_map/all_to_all | solution.py:238
  28.9 145.6 %collective-permute-start = (bf16[256,2048]{1,0:T(8,128)(2,1)S(1)}, bf16[256,2048]{1,0:T(8,128)(2,1)}, u32[]{:S(2)}, u32[]{:S(2)}) collective-permute-start(bf16[256,2048]{1,0:T(8,128)(2,1)S(1)} %copy-done.14), channel_id=1, source_target_pairs={{0,1},{1,2},{2,3},{3,0},{4,5},{5,6},{6,7},{7,4},{8,9},{9,10},{10,1... | collective-permute-start | bytes 3145736 | tf_op jit(solution)/shard_map/ppermute | solution.py:244
  30.9 143.6 %collective-permute-start.2 = (bf16[256,2048]{1,0:T(8,128)(2,1)S(1)}, bf16[256,2048]{1,0:T(8,128)(2,1)}, u32[]{:S(2)}, u32[]{:S(2)}) collective-permute-start(bf16[256,2048]{1,0:T(8,128)(2,1)S(1)} %copy-done.14), channel_id=1, source_target_pairs={{0,3},{1,0},{2,1},{3,2},{4,7},{5,4},{6,5},{7,6},{8,11},{9,8},{10,9... | collective-permute-start | bytes 3145736 | tf_op jit(solution)/shard_map/ppermute | solution.py:244
  31.0 143.5 %collective-permute-start.1 = (bf16[256,2048]{1,0:T(8,128)(2,1)S(1)}, bf16[256,2048]{1,0:T(8,128)(2,1)}, u32[]{:S(2)}, u32[]{:S(2)}) collective-permute-start(bf16[256,2048]{1,0:T(8,128)(2,1)S(1)} %copy-done.14), channel_id=1, source_target_pairs={{0,2},{1,3},{2,0},{3,1},{4,6},{5,7},{6,4},{7,5},{8,10},{9,11},{10,... | collective-permute-start | bytes 3145736 | tf_op jit(solution)/shard_map/ppermute | solution.py:244
  152.9 130.8 %all-to-all-start.1 = ((bf16[32,2,512,128]{3,2,1,0:T(8,128)(2,1)}), bf16[32,2,512,128]{3,2,1,0:T(8,128)(2,1)}, u32[]{:S(2)}, u32[]{:S(2)}) async-start(bf16[32,2,512,128]{3,2,1,0:T(8,128)(2,1)} %shard_map.82), calls=%async_computation.1 | async-start | bytes 16777216 | tf_op jit(solution)/shard_map/all_to_all | solution.py:238
  177.0 11.8 %copy-start.6 = (bf16[256,2048]{1,0:T(8,128)(2,1)}, bf16[256,2048]{1,0:T(8,128)(2,1)S(1)}, u32[]{:S(2)}) copy-start(bf16[256,2048]{1,0:T(8,128)(2,1)S(1)} %get-tuple-element.25) | copy-start | bytes 3145732
  177.0 11.8 %copy-start.8 = (bf16[256,2048]{1,0:T(8,128)(2,1)}, bf16[256,2048]{1,0:T(8,128)(2,1)S(1)}, u32[]{:S(2)}) copy-start(bf16[256,2048]{1,0:T(8,128)(2,1)S(1)} %get-tuple-element.26) | copy-start | bytes 3145732
  177.0 11.8 %copy-start.10 = (bf16[256,2048]{1,0:T(8,128)(2,1)}, bf16[256,2048]{1,0:T(8,128)(2,1)S(1)}, u32[]{:S(2)}) copy-start(bf16[256,2048]{1,0:T(8,128)(2,1)S(1)} %get-tuple-element.27) | copy-start | bytes 3145732
  177.0 11.8 %copy-start.12 = (bf16[256,2048]{1,0:T(8,128)(2,1)}, bf16[256,2048]{1,0:T(8,128)(2,1)S(1)}, u32[]{:S(2)}) copy-start(bf16[256,2048]{1,0:T(8,128)(2,1)S(1)} %get-tuple-element.28) | copy-start | bytes 3145732
  191.1 3.7 %copy-start.7 = (bf16[256,2048]{1,0:T(8,128)(2,1)S(1)}, bf16[256,2048]{1,0:T(8,128)(2,1)}, u32[]{:S(2)}) copy-start(bf16[256,2048]{1,0:T(8,128)(2,1)} %copy-done.6) | copy-start | bytes 3145732
  191.1 3.7 %copy-start.9 = (bf16[256,2048]{1,0:T(8,128)(2,1)S(1)}, bf16[256,2048]{1,0:T(8,128)(2,1)}, u32[]{:S(2)}) copy-start(bf16[256,2048]{1,0:T(8,128)(2,1)} %copy-done.8) | copy-start | bytes 3145732
  191.1 3.7 %copy-start.11 = (bf16[256,2048]{1,0:T(8,128)(2,1)S(1)}, bf16[256,2048]{1,0:T(8,128)(2,1)}, u32[]{:S(2)}) copy-start(bf16[256,2048]{1,0:T(8,128)(2,1)} %copy-done.10) | copy-start | bytes 3145732
  191.1 3.8 %copy-start.13 = (bf16[256,2048]{1,0:T(8,128)(2,1)S(1)}, bf16[256,2048]{1,0:T(8,128)(2,1)}, u32[]{:S(2)}) copy-start(bf16[256,2048]{1,0:T(8,128)(2,1)} %copy-done.12) | copy-start | bytes 3145732
  191.1 4.1 %copy-start.15 = (bf16[8192,128]{1,0:T(8,128)(2,1)S(1)}, bf16[8192,128]{1,0:T(8,128)(2,1)}, u32[]{:S(2)}) copy-start(bf16[8192,128]{1,0:T(8,128)(2,1)} %param.11) | copy-start | bytes 6291460
  196.6 3.2 %copy-start.2 = (bf16[2,128,1024]{2,1,0:T(8,128)(2,1)S(1)}, bf16[2,128,1024]{2,1,0:T(8,128)(2,1)}, u32[]{:S(2)}) copy-start(bf16[2,128,1024]{2,1,0:T(8,128)(2,1)} %copy.45.q_ref) | copy-start | bytes 1572868
  196.6 3.2 %copy-start.4 = (f32[16,128]{1,0:T(8,128)S(1)}, f32[16,128]{1,0:T(8,128)}, u32[]{:S(2)}) copy-start(f32[16,128]{1,0:T(8,128)} %get-tuple-element.55.c_ref.refs_4_) | copy-start | bytes 24580
  196.7 3.2 %copy-start.5 = (f32[16,128]{1,0:T(8,128)S(1)}, f32[16,128]{1,0:T(8,128)}, u32[]{:S(2)}) copy-start(f32[16,128]{1,0:T(8,128)} %get-tuple-element.56.s_ref.refs_5_) | copy-start | bytes 24580
  283.7 1.0 copy-start.3
  284.7 12.0 %copy-start.1 = (bf16[8192,128]{1,0:T(8,128)(2,1)S(1)}, bf16[8192,128]{1,0:T(8,128)(2,1)}, u32[]{:S(2)}) copy-start(bf16[8192,128]{1,0:T(8,128)(2,1)} %param.10) | copy-start | bytes 6291460

commit v13 on v11

--- a/solution.py
+++ b/solution.py
@@ -83,7 +83,7 @@
 LOG2E = 1.4426950408889634
 
 
-PER_STEP = 4
+PER_STEP = 8
 
 
 def block_kernel(rotate_keys, tab_ref, remap_ref, pos_ref, q_ref, *refs):

time: 299 us -> 300 us (level)
  no operation moved by 1% of the time
where the time goes in v13:
time: 300 us; the launch traced here: 297 us
  waiting for transfers between devices  172 us (57%)
  Pallas kernels  52.4 us (17%)
  starting transfers between devices  25.1 us (8%)
  matrix products  18.2 us (6%)
  local copies, waits for them, and re-layouts  13 us (4%)
  other arithmetic  8.33 us (3%)
  between operations  8.16 us (3%)
    all_to_all x2, waiting for transfers between devices, per_device(): lax.all_to_all(s, 'store', split_axis=0, concat_axis=0, tiled=True)  167 us
    pallas_call x2, Pallas kernels, attend_chunk(): pl.pallas_call(functools.partial(block_kernel, rotate_keys), grid_spec=gr...  39.4 us
    pallas_call x2, Pallas kernels, build_send(): pl.pallas_call(functools.partial(send_kernel, slot), grid_spec=grid_spec,...  13 us
    all_to_all x2, starting transfers between devices, per_device(): lax.all_to_all(s, 'store', split_axis=0, concat_axis=0, tiled=True)  12.5 us
    dot_general x1, matrix products, per_device(): qf = jnp.dot(piece, w_query, preferred_element_type=jnp.float32)  11.7 us
    all_to_all x1, starting transfers between devices, per_device(): lax.all_to_all(request, 'store', split_axis=0, concat_axis=0, tiled=True)  7.53 us
  transfers between devices with their start and end apart: 6, of which 3 were waited for; matrix products, arithmetic and copies ran while one was open for 11% of the time, Pallas kernels for 12%

profile of v13, /device:TPU:40, one launch (start us, length us, event | category | flops | bytes accessed | tf_op | source)
XLA Modules:
  0.0 297.3 jit_solution(4795734123674655464)
XLA Ops:
  0.0 0.9 reshape.212
  2.9 7.5 %all-to-all-start = ((s32[32,2,2]{2,1,0:T(2,128)}), s32[32,2,2]{2,1,0:T(2,128)S(1)}, u32[]{:S(2)}, u32[]{:S(2)}) async-start(s32[32,2,2]{2,1,0:T(2,128)} %copy.37), calls=%async_computation | async-start | bytes 65536 | tf_op jit(solution)/shard_map/all_to_all | solution.py:227
  11.2 5.4 %all-to-all-done = s32[32,2,2]{2,1,0:T(2,128)S(1)} async-done(((s32[32,2,2]{2,1,0:T(2,128)}), s32[32,2,2]{2,1,0:T(2,128)S(1)}, u32[]{:S(2)}, u32[]{:S(2)}) %all-to-all-start) | async-done | bytes 544 | tf_op jit(solution)/shard_map/all_to_all | solution.py:227
  17.3 5.6 %shard_map.83 = bf16[32,2,512,128]{3,2,1,0:T(8,128)(2,1)} custom-call(s32[128]{0:T(128)} %reshape.217.req_ref, bf16[4,512,128]{2,1,0:T(8,128)(2,1)} %k_ref.3, bf16[4,512,128]{2,1,0:T(8,128)(2,1)} %v_ref.3, f32[16,128]{1,0:T(8,128)} %get-tuple-element.55.c_ref.refs_8_, f32[16,128]{1,0:T(8,128)} %get-tuple-element.56.s_ref.refs_9_), custom_call_target="tpu_custom_call" | custom-call | flops 8388608 | bytes 9437184 | tf_op jit(solution)/shard_map/pallas_call | solution.py:70
  22.8 6.1 %all-to-all-start.2 = ((bf16[32,2,512,128]{3,2,1,0:T(8,128)(2,1)}), bf16[32,2,512,128]{3,2,1,0:T(8,128)(2,1)}, u32[]{:S(2)}, u32[]{:S(2)}) async-start(bf16[32,2,512,128]{3,2,1,0:T(8,128)(2,1)} %shard_map.83), calls=%async_computation.2 | async-start | bytes 16777216 | tf_op jit(solution)/shard_map/all_to_all | solution.py:238
  29.0 2.0 collective-permute-start
  31.1 3.0 %collective-permute-start.1 = (bf16[256,2048]{1,0:T(8,128)(2,1)S(1)}, bf16[256,2048]{1,0:T(8,128)(2,1)}, u32[]{:S(2)}, u32[]{:S(2)}) collective-permute-start(bf16[256,2048]{1,0:T(8,128)(2,1)S(1)} %copy-done.14), channel_id=1, source_target_pairs={{0,2},{1,3},{2,0},{3,1},{4,6},{5,7},{6,4},{7,5},{8,10},{9,11},{10,... | collective-permute-start | bytes 3145736 | tf_op jit(solution)/shard_map/ppermute | solution.py:244
  34.1 7.5 %shard_map.82 = bf16[32,2,512,128]{3,2,1,0:T(8,128)(2,1)} custom-call(s32[128]{0:T(128)} %reshape.217.req_ref, bf16[4,512,128]{2,1,0:T(8,128)(2,1)} %k_ref.3, bf16[4,512,128]{2,1,0:T(8,128)(2,1)} %v_ref.3, f32[16,128]{1,0:T(8,128)} %get-tuple-element.55.c_ref.refs_8_, f32[16,128]{1,0:T(8,128)} %get-tuple-element.56.s_ref.refs_9_), custom_call_target="tpu_custom_call" | custom-call | flops 8388608 | bytes 9437184 | tf_op jit(solution)/shard_map/pallas_call | solution.py:70
  41.5 111.4 %all-to-all-done.2.refs_0_.refs_1_.refs_2_.refs_3_.refs_4_.refs_5_.refs_6_.refs_7_ = bf16[32,2,512,128]{3,2,1,0:T(8,128)(2,1)} async-done(((bf16[32,2,512,128]{3,2,1,0:T(8,128)(2,1)}), bf16[32,2,512,128]{3,2,1,0:T(8,128)(2,1)}, u32[]{:S(2)}, u32[]{:S(2)}) %all-to-all-start.2) | async-done | bytes 8388640 | tf_op jit(solution)/shard_map/all_to_all | solution.py:238
  153.0 6.4 %all-to-all-start.1 = ((bf16[32,2,512,128]{3,2,1,0:T(8,128)(2,1)}), bf16[32,2,512,128]{3,2,1,0:T(8,128)(2,1)}, u32[]{:S(2)}, u32[]{:S(2)}) async-start(bf16[32,2,512,128]{3,2,1,0:T(8,128)(2,1)} %shard_map.82), calls=%async_computation.1 | async-start | bytes 16777216 | tf_op jit(solution)/shard_map/all_to_all | solution.py:238
  159.4 1.6 sort.32
  161.0 1.6 sort.31
  174.6 2.1 pad_maximum_fusion
  177.1 11.7 %convolution_bitcast_fusion = f32[32,8,8,128]{3,1,2,0:T(8,128)S(1)} fusion(bf16[8192,1024]{1,0:T(8,128)(2,1)} %param.9, bf16[256,2048]{1,0:T(8,128)(2,1)S(1)} %get-tuple-element.26, bf16[256,2048]{1,0:T(8,128)(2,1)S(1)} %get-tuple-element.27, bf16[256,2048]{1,0:T(8,128)(2,1)S(1)} %get-tuple-element.28, bf16[256,2048]{1,0:T(8,128)(2,1)S(1)} %get-tuple-element.25), kind=kOutput, calls=%fused_computation.6 | convolution fusion | flops 4311744512 | bytes 22020096 | tf_op jit(solution)/shard_map/dot_general | solution.py:253
  190.2 1.0 copy.45.q_ref
  191.2 3.2 %fusion.26 = f32[256,128]{1,0:T(8,128)S(1)} fusion(bf16[8192,128]{1,0:T(8,128)(2,1)S(1)} %copy-done, bf16[256,2048]{1,0:T(8,128)(2,1)} %copy-done.8, bf16[256,2048]{1,0:T(8,128)(2,1)} %copy-done.10, bf16[256,2048]{1,0:T(8,128)(2,1)} %copy-done.12, bf16[256,2048]{1,0:T(8,128)(2,1)} %copy-done.6), kind=kOutput, calls=%fused_computation.94 | convolution fusion | flops 553648128 | bytes 6422528 | tf_op jit(solution)/shard_map/dot_general | solution.py:254
  195.3 1.4 convolution_convert_fusion
  196.8 1.4 fusion.3
  198.2 1.6 copy.46.refs_12_
  200.0 28.4 %shard_map.84 = (f32[2,1,1024]{2,1,0:T(1,128)S(1)}, f32[2,1,1024]{2,1,0:T(1,128)S(1)}, f32[2,128,1024]{2,1,0:T(8,128)S(1)}) custom-call(s32[32]{0:T(128)S(1)} %gather_fusion.2, s32[32]{0:T(128)S(1)} %reduce.1.remap_ref, s32[32]{0:T(128)S(1)} %gather_fusion.3, ...), custom_call_target="tpu_custom_call", output_to_operand_aliasing={{0}: (14, {}), {1}: (15, {}), {2}: (16, {})} | custom-call | flops 8589934592 | bytes 10485760 | tf_op jit(solution)/shard_map/pallas_call | solution.py:172
  228.4 55.4 %all-to-all-done.1.refs_0_.refs_1_.refs_2_.refs_3_.refs_4_.refs_5_.refs_6_.refs_7_ = bf16[32,2,512,128]{3,2,1,0:T(8,128)(2,1)} async-done(((bf16[32,2,512,128]{3,2,1,0:T(8,128)(2,1)}), bf16[32,2,512,128]{3,2,1,0:T(8,128)(2,1)}, u32[]{:S(2)}, u32[]{:S(2)}) %all-to-all-start.1) | async-done | bytes 8388640 | tf_op jit(solution)/shard_map/all_to_all | solution.py:238
  283.8 1.0 copy-done.3
  284.8 11.0 %shard_map.85 = (f32[2,1,1024]{2,1,0:T(1,128)S(1)}, f32[2,1,1024]{2,1,0:T(1,128)S(1)}, f32[2,128,1024]{2,1,0:T(8,128)S(1)}, bf16[2,128,1024]{2,1,0:T(8,128)(2,1)S(1)}) custom-call(s32[16]{0:T(128)S(1)} %gather_fusion, s32[16]{0:T(128)S(1)} %reduce.remap_ref, s32[16]{0:T(128)S(1)} %gather_fusion.1, ...), custom_call_target="tpu_custom_call", output_to_operand_aliasing={{0}: (14, {}), {1}: (15, {}), {2}: (16, {})} | custom-call | flops 4294967296 | bytes 10485760 | tf_op jit(solution)/shard_map/pallas_call | solution.py:172
  296.4 0.9 copy.57
  (87 shorter events, 11.0 us)
Async XLA Ops:
  0.0 191.2 %copy-start = (bf16[8192,128]{1,0:T(8,128)(2,1)S(1)}, bf16[8192,128]{1,0:T(8,128)(2,1)}, u32[]{:S(2)}) copy-start(bf16[8192,128]{1,0:T(8,128)(2,1)} %param.10) | copy-start | bytes 6291460
  2.9 13.7 %all-to-all-start = ((s32[32,2,2]{2,1,0:T(2,128)}), s32[32,2,2]{2,1,0:T(2,128)S(1)}, u32[]{:S(2)}, u32[]{:S(2)}) async-start(s32[32,2,2]{2,1,0:T(2,128)} %copy.37), calls=%async_computation | async-start | bytes 65536 | tf_op jit(solution)/shard_map/all_to_all | solution.py:227
  22.8 6.1 %copy-start.14 = (bf16[256,2048]{1,0:T(8,128)(2,1)S(1)}, bf16[256,2048]{1,0:T(8,128)(2,1)}, u32[]{:S(2)}) copy-start(bf16[256,2048]{1,0:T(8,128)(2,1)} %param.8) | copy-start | bytes 3145732
  22.8 130.1 %all-to-all-start.2 = ((bf16[32,2,512,128]{3,2,1,0:T(8,128)(2,1)}), bf16[32,2,512,128]{3,2,1,0:T(8,128)(2,1)}, u32[]{:S(2)}, u32[]{:S(2)}) async-start(bf16[32,2,512,128]{3,2,1,0:T(8,128)(2,1)} %shard_map.83), calls=%async_computation.2 | async-start | bytes 16777216 | tf_op jit(solution)/shard_map/all_to_all | solution.py:238
  29.0 145.6 %collective-permute-start = (bf16[256,2048]{1,0:T(8,128)(2,1)S(1)}, bf16[256,2048]{1,0:T(8,128)(2,1)}, u32[]{:S(2)}, u32[]{:S(2)}) collective-permute-start(bf16[256,2048]{1,0:T(8,128)(2,1)S(1)} %copy-done.14), channel_id=1, source_target_pairs={{0,1},{1,2},{2,3},{3,0},{4,5},{5,6},{6,7},{7,4},{8,9},{9,10},{10,1... | collective-permute-start | bytes 3145736 | tf_op jit(solution)/shard_map/ppermute | solution.py:244
  31.0 143.6 %collective-permute-start.2 = (bf16[256,2048]{1,0:T(8,128)(2,1)S(1)}, bf16[256,2048]{1,0:T(8,128)(2,1)}, u32[]{:S(2)}, u32[]{:S(2)}) collective-permute-start(bf16[256,2048]{1,0:T(8,128)(2,1)S(1)} %copy-done.14), channel_id=1, source_target_pairs={{0,3},{1,0},{2,1},{3,2},{4,7},{5,4},{6,5},{7,6},{8,11},{9,8},{10,9... | collective-permute-start | bytes 3145736 | tf_op jit(solution)/shard_map/ppermute | solution.py:244
  31.1 143.5 %collective-permute-start.1 = (bf16[256,2048]{1,0:T(8,128)(2,1)S(1)}, bf16[256,2048]{1,0:T(8,128)(2,1)}, u32[]{:S(2)}, u32[]{:S(2)}) collective-permute-start(bf16[256,2048]{1,0:T(8,128)(2,1)S(1)} %copy-done.14), channel_id=1, source_target_pairs={{0,2},{1,3},{2,0},{3,1},{4,6},{5,7},{6,4},{7,5},{8,10},{9,11},{10,... | collective-permute-start | bytes 3145736 | tf_op jit(solution)/shard_map/ppermute | solution.py:244
  153.0 130.8 %all-to-all-start.1 = ((bf16[32,2,512,128]{3,2,1,0:T(8,128)(2,1)}), bf16[32,2,512,128]{3,2,1,0:T(8,128)(2,1)}, u32[]{:S(2)}, u32[]{:S(2)}) async-start(bf16[32,2,512,128]{3,2,1,0:T(8,128)(2,1)} %shard_map.82), calls=%async_computation.1 | async-start | bytes 16777216 | tf_op jit(solution)/shard_map/all_to_all | solution.py:238
  177.1 11.8 %copy-start.6 = (bf16[256,2048]{1,0:T(8,128)(2,1)}, bf16[256,2048]{1,0:T(8,128)(2,1)S(1)}, u32[]{:S(2)}) copy-start(bf16[256,2048]{1,0:T(8,128)(2,1)S(1)} %get-tuple-element.25) | copy-start | bytes 3145732
  177.1 11.8 %copy-start.8 = (bf16[256,2048]{1,0:T(8,128)(2,1)}, bf16[256,2048]{1,0:T(8,128)(2,1)S(1)}, u32[]{:S(2)}) copy-start(bf16[256,2048]{1,0:T(8,128)(2,1)S(1)} %get-tuple-element.26) | copy-start | bytes 3145732
  177.1 11.8 %copy-start.10 = (bf16[256,2048]{1,0:T(8,128)(2,1)}, bf16[256,2048]{1,0:T(8,128)(2,1)S(1)}, u32[]{:S(2)}) copy-start(bf16[256,2048]{1,0:T(8,128)(2,1)S(1)} %get-tuple-element.27) | copy-start | bytes 3145732
  177.1 11.8 %copy-start.12 = (bf16[256,2048]{1,0:T(8,128)(2,1)}, bf16[256,2048]{1,0:T(8,128)(2,1)S(1)}, u32[]{:S(2)}) copy-start(bf16[256,2048]{1,0:T(8,128)(2,1)S(1)} %get-tuple-element.28) | copy-start | bytes 3145732
  191.2 3.7 %copy-start.7 = (bf16[256,2048]{1,0:T(8,128)(2,1)S(1)}, bf16[256,2048]{1,0:T(8,128)(2,1)}, u32[]{:S(2)}) copy-start(bf16[256,2048]{1,0:T(8,128)(2,1)} %copy-done.6) | copy-start | bytes 3145732
  191.2 3.8 %copy-start.9 = (bf16[256,2048]{1,0:T(8,128)(2,1)S(1)}, bf16[256,2048]{1,0:T(8,128)(2,1)}, u32[]{:S(2)}) copy-start(bf16[256,2048]{1,0:T(8,128)(2,1)} %copy-done.8) | copy-start | bytes 3145732
  191.2 3.8 %copy-start.11 = (bf16[256,2048]{1,0:T(8,128)(2,1)S(1)}, bf16[256,2048]{1,0:T(8,128)(2,1)}, u32[]{:S(2)}) copy-start(bf16[256,2048]{1,0:T(8,128)(2,1)} %copy-done.10) | copy-start | bytes 3145732
  191.2 3.8 %copy-start.13 = (bf16[256,2048]{1,0:T(8,128)(2,1)S(1)}, bf16[256,2048]{1,0:T(8,128)(2,1)}, u32[]{:S(2)}) copy-start(bf16[256,2048]{1,0:T(8,128)(2,1)} %copy-done.12) | copy-start | bytes 3145732
  191.2 4.1 %copy-start.15 = (bf16[8192,128]{1,0:T(8,128)(2,1)S(1)}, bf16[8192,128]{1,0:T(8,128)(2,1)}, u32[]{:S(2)}) copy-start(bf16[8192,128]{1,0:T(8,128)(2,1)} %param.11) | copy-start | bytes 6291460
  196.7 3.2 %copy-start.2 = (bf16[2,128,1024]{2,1,0:T(8,128)(2,1)S(1)}, bf16[2,128,1024]{2,1,0:T(8,128)(2,1)}, u32[]{:S(2)}) copy-start(bf16[2,128,1024]{2,1,0:T(8,128)(2,1)} %copy.45.q_ref) | copy-start | bytes 1572868
  196.7 3.2 %copy-start.4 = (f32[16,128]{1,0:T(8,128)S(1)}, f32[16,128]{1,0:T(8,128)}, u32[]{:S(2)}) copy-start(f32[16,128]{1,0:T(8,128)} %get-tuple-element.55.c_ref.refs_8_) | copy-start | bytes 24580
  196.7 3.2 %copy-start.5 = (f32[16,128]{1,0:T(8,128)S(1)}, f32[16,128]{1,0:T(8,128)}, u32[]{:S(2)}) copy-start(f32[16,128]{1,0:T(8,128)} %get-tuple-element.56.s_ref.refs_9_) | copy-start | bytes 24580
  283.8 1.0 copy-start.3
  284.8 12.5 %copy-start.1 = (bf16[8192,128]{1,0:T(8,128)(2,1)S(1)}, bf16[8192,128]{1,0:T(8,128)(2,1)}, u32[]{:S(2)}) copy-start(bf16[8192,128]{1,0:T(8,128)(2,1)} %param.10) | copy-start | bytes 6291460

commit v14 on v11

--- a/solution.py
+++ b/solution.py
@@ -86,9 +86,9 @@
 PER_STEP = 4
 
 
-def block_kernel(rotate_keys, tab_ref, remap_ref, pos_ref, q_ref, *refs):
-    kv_refs = refs[:PER_STEP]
-    c_ref, s_ref, m_in, l_in, a_in, m_ref, l_ref, a_ref, *out = refs[PER_STEP:]
+def block_kernel(rotate_keys, per_step, tab_ref, remap_ref, pos_ref, q_ref, *refs):
+    kv_refs = refs[:per_step]
+    c_ref, s_ref, m_in, l_in, a_in, m_ref, l_ref, a_ref, *out = refs[per_step:]
     o = pl.program_id(0)
 
     @pl.when(o == 0)
@@ -99,13 +99,13 @@
 
     c = (HD ** (-0.5)) * LOG2E
     for j, kv_ref in enumerate(kv_refs):
-        qi = tab_ref[PER_STEP * o + j]
+        qi = tab_ref[per_step * o + j]
 
         @pl.when(qi >= 0)
         def _():
             k = kv_ref[0, 0]
             if rotate_keys:
-                pos = pos_ref[PER_STEP * o + j]
+                pos = pos_ref[per_step * o + j]
                 kf = k.astype(jnp.float32)
                 turned = pltpu.roll(kf, kf.shape[-1] // 2, 1)
                 k = (
@@ -142,7 +142,8 @@
 def attend_chunk(
     rotate_keys, tab, remap, pos, cos_tab, sin_tab, query_t, recv, m, l, acc, final=False
 ):
-    owners = tab.shape[0] // PER_STEP
+    per_step = PER_STEP if rotate_keys else 2 * PER_STEP
+    owners = tab.shape[0] // per_step
     nq, hd, rows = query_t.shape
     plen = recv.shape[2]
     full3 = lambda shape: pl.BlockSpec(shape, lambda o, t, r, p: (0, 0, 0))
@@ -154,9 +155,9 @@
         ]
         + [
             pl.BlockSpec(
-                (1, 2, plen, hd), lambda o, t, r, p, j=j: (r[PER_STEP * o + j], 0, 0, 0)
+                (1, 2, plen, hd), lambda o, t, r, p, j=j: (r[per_step * o + j], 0, 0, 0)
             )
-            for j in range(PER_STEP)
+            for j in range(per_step)
         ]
         + [
             pl.BlockSpec(cos_tab.shape, lambda o, t, r, p: (0, 0)),
@@ -168,9 +169,9 @@
         out_specs=[full3((nq, 1, rows)), full3((nq, 1, rows)), full3((nq, hd, rows))]
         + ([full3((nq, hd, rows))] if final else []),
     )
-    flops = 2 * nq * rows * plen * hd * owners * PER_STEP
+    flops = 2 * nq * rows * plen * hd * owners * per_step
     return pl.pallas_call(
-        functools.partial(block_kernel, rotate_keys),
+        functools.partial(block_kernel, rotate_keys, per_step),
         grid_spec=grid_spec,
         out_shape=[
             jax.ShapeDtypeStruct(m.shape, jnp.float32),
@@ -178,16 +179,16 @@
             jax.ShapeDtypeStruct(acc.shape, jnp.float32),
         ]
         + ([jax.ShapeDtypeStruct(acc.shape, jnp.bfloat16)] if final else []),
-        input_output_aliases={6 + PER_STEP: 0, 7 + PER_STEP: 1, 8 + PER_STEP: 2},
+        input_output_aliases={6 + per_step: 0, 7 + per_step: 1, 8 + per_step: 2},
         compiler_params=pltpu.CompilerParams(
             dimension_semantics=("arbitrary",), vmem_limit_bytes=48 * 1024 * 1024
         ),
         cost_estimate=pl.CostEstimate(
             flops=flops,
-            transcendentals=nq * rows * plen * owners * PER_STEP // 2,
+            transcendentals=nq * rows * plen * owners * per_step // 2,
             bytes_accessed=recv.size * 2 + 2 * acc.size * 4,
         ),
-    )(tab, remap, pos, query_t, *([recv] * PER_STEP), cos_tab, sin_tab, m, l, acc)
+    )(tab, remap, pos, query_t, *([recv] * per_step), cos_tab, sin_tab, m, l, acc)
 
 
 def per_device(

time: 299 us -> 299 us (level)
  no operation moved by 1% of the time
where the time goes in v14:
time: 299 us; the launch traced here: 297 us
  waiting for transfers between devices  173 us (58%)
  Pallas kernels  51.8 us (17%)
  starting transfers between devices  25.1 us (8%)
  matrix products  18.2 us (6%)
  local copies, waits for them, and re-layouts  13 us (4%)
  other arithmetic  8.33 us (3%)
  between operations  8.16 us (3%)
    all_to_all x2, waiting for transfers between devices, per_device(): lax.all_to_all(s, 'store', split_axis=0, concat_axis=0, tiled=True)  167 us
    pallas_call x2, Pallas kernels, attend_chunk(): pl.pallas_call(functools.partial(block_kernel, rotate_keys, per_step), gr...  38.8 us
    pallas_call x2, Pallas kernels, build_send(): pl.pallas_call(functools.partial(send_kernel, slot), grid_spec=grid_spec,...  13 us
    all_to_all x2, starting transfers between devices, per_device(): lax.all_to_all(s, 'store', split_axis=0, concat_axis=0, tiled=True)  12.5 us
    dot_general x1, matrix products, per_device(): qf = jnp.dot(piece, w_query, preferred_element_type=jnp.float32)  11.7 us
    all_to_all x1, starting transfers between devices, per_device(): lax.all_to_all(request, 'store', split_axis=0, concat_axis=0, tiled=True)  7.53 us
  transfers between devices with their start and end apart: 6, of which 3 were waited for; matrix products, arithmetic and copies ran while one was open for 11% of the time, Pallas kernels for 12%

profile of v14, /device:TPU:40, one launch (start us, length us, event | category | flops | bytes accessed | tf_op | source)
XLA Modules:
  0.0 297.1 jit_solution(9592922170033965325)
XLA Ops:
  0.0 0.9 reshape.212
  2.9 7.5 %all-to-all-start = ((s32[32,2,2]{2,1,0:T(2,128)}), s32[32,2,2]{2,1,0:T(2,128)S(1)}, u32[]{:S(2)}, u32[]{:S(2)}) async-start(s32[32,2,2]{2,1,0:T(2,128)} %copy.37), calls=%async_computation | async-start | bytes 65536 | tf_op jit(solution)/shard_map/all_to_all | solution.py:228
  11.2 5.4 %all-to-all-done = s32[32,2,2]{2,1,0:T(2,128)S(1)} async-done(((s32[32,2,2]{2,1,0:T(2,128)}), s32[32,2,2]{2,1,0:T(2,128)S(1)}, u32[]{:S(2)}, u32[]{:S(2)}) %all-to-all-start) | async-done | bytes 544 | tf_op jit(solution)/shard_map/all_to_all | solution.py:228
  17.3 5.6 %shard_map.83 = bf16[32,2,512,128]{3,2,1,0:T(8,128)(2,1)} custom-call(s32[128]{0:T(128)} %reshape.217.req_ref, bf16[4,512,128]{2,1,0:T(8,128)(2,1)} %k_ref.3, bf16[4,512,128]{2,1,0:T(8,128)(2,1)} %v_ref.3, f32[16,128]{1,0:T(8,128)} %get-tuple-element.55.c_ref.refs_4_.refs_8_, f32[16,128]{1,0:T(8,128)} %get-tuple-element.56.s_ref.refs_5_.refs_9_), custom_call_target="tpu_custom_call" | custom-call | flops 8388608 | bytes 9437184 | tf_op jit(solution)/shard_map/pallas_call | solution.py:70
  22.8 6.1 %all-to-all-start.2 = ((bf16[32,2,512,128]{3,2,1,0:T(8,128)(2,1)}), bf16[32,2,512,128]{3,2,1,0:T(8,128)(2,1)}, u32[]{:S(2)}, u32[]{:S(2)}) async-start(bf16[32,2,512,128]{3,2,1,0:T(8,128)(2,1)} %shard_map.83), calls=%async_computation.2 | async-start | bytes 16777216 | tf_op jit(solution)/shard_map/all_to_all | solution.py:239
  29.0 2.0 collective-permute-start
  31.1 3.0 %collective-permute-start.1 = (bf16[256,2048]{1,0:T(8,128)(2,1)S(1)}, bf16[256,2048]{1,0:T(8,128)(2,1)}, u32[]{:S(2)}, u32[]{:S(2)}) collective-permute-start(bf16[256,2048]{1,0:T(8,128)(2,1)S(1)} %copy-done.14), channel_id=1, source_target_pairs={{0,2},{1,3},{2,0},{3,1},{4,6},{5,7},{6,4},{7,5},{8,10},{9,11},{10,... | collective-permute-start | bytes 3145736 | tf_op jit(solution)/shard_map/ppermute | solution.py:245
  34.1 7.5 %shard_map.82 = bf16[32,2,512,128]{3,2,1,0:T(8,128)(2,1)} custom-call(s32[128]{0:T(128)} %reshape.217.req_ref, bf16[4,512,128]{2,1,0:T(8,128)(2,1)} %k_ref.3, bf16[4,512,128]{2,1,0:T(8,128)(2,1)} %v_ref.3, f32[16,128]{1,0:T(8,128)} %get-tuple-element.55.c_ref.refs_4_.refs_8_, f32[16,128]{1,0:T(8,128)} %get-tuple-element.56.s_ref.refs_5_.refs_9_), custom_call_target="tpu_custom_call" | custom-call | flops 8388608 | bytes 9437184 | tf_op jit(solution)/shard_map/pallas_call | solution.py:70
  41.5 111.4 %all-to-all-done.2.refs_0_.refs_1_.refs_2_.refs_3_ = bf16[32,2,512,128]{3,2,1,0:T(8,128)(2,1)} async-done(((bf16[32,2,512,128]{3,2,1,0:T(8,128)(2,1)}), bf16[32,2,512,128]{3,2,1,0:T(8,128)(2,1)}, u32[]{:S(2)}, u32[]{:S(2)}) %all-to-all-start.2) | async-done | bytes 8388640 | tf_op jit(solution)/shard_map/all_to_all | solution.py:239
  153.0 6.4 %all-to-all-start.1 = ((bf16[32,2,512,128]{3,2,1,0:T(8,128)(2,1)}), bf16[32,2,512,128]{3,2,1,0:T(8,128)(2,1)}, u32[]{:S(2)}, u32[]{:S(2)}) async-start(bf16[32,2,512,128]{3,2,1,0:T(8,128)(2,1)} %shard_map.82), calls=%async_computation.1 | async-start | bytes 16777216 | tf_op jit(solution)/shard_map/all_to_all | solution.py:239
  159.4 1.6 sort.32
  161.0 1.6 sort.31
  174.6 2.1 pad_maximum_fusion
  177.1 11.7 %convolution_bitcast_fusion = f32[32,8,8,128]{3,1,2,0:T(8,128)S(1)} fusion(bf16[8192,1024]{1,0:T(8,128)(2,1)} %param.9, bf16[256,2048]{1,0:T(8,128)(2,1)S(1)} %get-tuple-element.26, bf16[256,2048]{1,0:T(8,128)(2,1)S(1)} %get-tuple-element.27, bf16[256,2048]{1,0:T(8,128)(2,1)S(1)} %get-tuple-element.28, bf16[256,2048]{1,0:T(8,128)(2,1)S(1)} %get-tuple-element.25), kind=kOutput, calls=%fused_computation.6 | convolution fusion | flops 4311744512 | bytes 22020096 | tf_op jit(solution)/shard_map/dot_general | solution.py:254
  190.2 1.0 copy.45.q_ref
  191.2 3.2 %fusion.26 = f32[256,128]{1,0:T(8,128)S(1)} fusion(bf16[8192,128]{1,0:T(8,128)(2,1)S(1)} %copy-done, bf16[256,2048]{1,0:T(8,128)(2,1)} %copy-done.8, bf16[256,2048]{1,0:T(8,128)(2,1)} %copy-done.10, bf16[256,2048]{1,0:T(8,128)(2,1)} %copy-done.12, bf16[256,2048]{1,0:T(8,128)(2,1)} %copy-done.6), kind=kOutput, calls=%fused_computation.94 | convolution fusion | flops 553648128 | bytes 6422528 | tf_op jit(solution)/shard_map/dot_general | solution.py:255
  195.3 1.4 convolution_convert_fusion
  196.8 1.4 fusion.3
  198.2 1.6 copy.46.refs_8_
  200.0 28.0 %shard_map.84 = (f32[2,1,1024]{2,1,0:T(1,128)S(1)}, f32[2,1,1024]{2,1,0:T(1,128)S(1)}, f32[2,128,1024]{2,1,0:T(8,128)S(1)}) custom-call(s32[32]{0:T(128)S(1)} %gather_fusion.2, s32[32]{0:T(128)S(1)} %reduce.1.remap_ref, s32[32]{0:T(128)S(1)} %gather_fusion.3, ...), custom_call_target="tpu_custom_call", output_to_operand_aliasing={{0}: (10, {}), {1}: (11, {}), {2}: (12, {})} | custom-call | flops 8589934592 | bytes 10485760 | tf_op jit(solution)/shard_map/pallas_call | solution.py:173
  228.0 55.8 %all-to-all-done.1.refs_0_.refs_1_.refs_2_.refs_3_.refs_4_.refs_5_.refs_6_.refs_7_ = bf16[32,2,512,128]{3,2,1,0:T(8,128)(2,1)} async-done(((bf16[32,2,512,128]{3,2,1,0:T(8,128)(2,1)}), bf16[32,2,512,128]{3,2,1,0:T(8,128)(2,1)}, u32[]{:S(2)}, u32[]{:S(2)}) %all-to-all-start.1) | async-done | bytes 8388640 | tf_op jit(solution)/shard_map/all_to_all | solution.py:239
  283.8 1.0 copy-done.3
  284.8 10.8 %shard_map.85 = (f32[2,1,1024]{2,1,0:T(1,128)S(1)}, f32[2,1,1024]{2,1,0:T(1,128)S(1)}, f32[2,128,1024]{2,1,0:T(8,128)S(1)}, bf16[2,128,1024]{2,1,0:T(8,128)(2,1)S(1)}) custom-call(s32[16]{0:T(128)S(1)} %gather_fusion, s32[16]{0:T(128)S(1)} %reduce.remap_ref, s32[16]{0:T(128)S(1)} %gather_fusion.1, ...), custom_call_target="tpu_custom_call", output_to_operand_aliasing={{0}: (14, {}), {1}: (15, {}), {2}: (16, {})} | custom-call | flops 4294967296 | bytes 10485760 | tf_op jit(solution)/shard_map/pallas_call | solution.py:173
  296.2 0.9 copy.57
  (87 shorter events, 11.0 us)
Async XLA Ops:
  0.0 191.2 %copy-start = (bf16[8192,128]{1,0:T(8,128)(2,1)S(1)}, bf16[8192,128]{1,0:T(8,128)(2,1)}, u32[]{:S(2)}) copy-start(bf16[8192,128]{1,0:T(8,128)(2,1)} %param.10) | copy-start | bytes 6291460
  2.9 13.7 %all-to-all-start = ((s32[32,2,2]{2,1,0:T(2,128)}), s32[32,2,2]{2,1,0:T(2,128)S(1)}, u32[]{:S(2)}, u32[]{:S(2)}) async-start(s32[32,2,2]{2,1,0:T(2,128)} %copy.37), calls=%async_computation | async-start | bytes 65536 | tf_op jit(solution)/shard_map/all_to_all | solution.py:228
  22.8 6.1 %copy-start.14 = (bf16[256,2048]{1,0:T(8,128)(2,1)S(1)}, bf16[256,2048]{1,0:T(8,128)(2,1)}, u32[]{:S(2)}) copy-start(bf16[256,2048]{1,0:T(8,128)(2,1)} %param.8) | copy-start | bytes 3145732
  22.8 130.1 %all-to-all-start.2 = ((bf16[32,2,512,128]{3,2,1,0:T(8,128)(2,1)}), bf16[32,2,512,128]{3,2,1,0:T(8,128)(2,1)}, u32[]{:S(2)}, u32[]{:S(2)}) async-start(bf16[32,2,512,128]{3,2,1,0:T(8,128)(2,1)} %shard_map.83), calls=%async_computation.2 | async-start | bytes 16777216 | tf_op jit(solution)/shard_map/all_to_all | solution.py:239
  29.0 145.6 %collective-permute-start = (bf16[256,2048]{1,0:T(8,128)(2,1)S(1)}, bf16[256,2048]{1,0:T(8,128)(2,1)}, u32[]{:S(2)}, u32[]{:S(2)}) collective-permute-start(bf16[256,2048]{1,0:T(8,128)(2,1)S(1)} %copy-done.14), channel_id=1, source_target_pairs={{0,1},{1,2},{2,3},{3,0},{4,5},{5,6},{6,7},{7,4},{8,9},{9,10},{10,1... | collective-permute-start | bytes 3145736 | tf_op jit(solution)/shard_map/ppermute | solution.py:245
  31.0 143.6 %collective-permute-start.2 = (bf16[256,2048]{1,0:T(8,128)(2,1)S(1)}, bf16[256,2048]{1,0:T(8,128)(2,1)}, u32[]{:S(2)}, u32[]{:S(2)}) collective-permute-start(bf16[256,2048]{1,0:T(8,128)(2,1)S(1)} %copy-done.14), channel_id=1, source_target_pairs={{0,3},{1,0},{2,1},{3,2},{4,7},{5,4},{6,5},{7,6},{8,11},{9,8},{10,9... | collective-permute-start | bytes 3145736 | tf_op jit(solution)/shard_map/ppermute | solution.py:245
  31.1 143.5 %collective-permute-start.1 = (bf16[256,2048]{1,0:T(8,128)(2,1)S(1)}, bf16[256,2048]{1,0:T(8,128)(2,1)}, u32[]{:S(2)}, u32[]{:S(2)}) collective-permute-start(bf16[256,2048]{1,0:T(8,128)(2,1)S(1)} %copy-done.14), channel_id=1, source_target_pairs={{0,2},{1,3},{2,0},{3,1},{4,6},{5,7},{6,4},{7,5},{8,10},{9,11},{10,... | collective-permute-start | bytes 3145736 | tf_op jit(solution)/shard_map/ppermute | solution.py:245
  153.0 130.8 %all-to-all-start.1 = ((bf16[32,2,512,128]{3,2,1,0:T(8,128)(2,1)}), bf16[32,2,512,128]{3,2,1,0:T(8,128)(2,1)}, u32[]{:S(2)}, u32[]{:S(2)}) async-start(bf16[32,2,512,128]{3,2,1,0:T(8,128)(2,1)} %shard_map.82), calls=%async_computation.1 | async-start | bytes 16777216 | tf_op jit(solution)/shard_map/all_to_all | solution.py:239
  177.1 11.8 %copy-start.6 = (bf16[256,2048]{1,0:T(8,128)(2,1)}, bf16[256,2048]{1,0:T(8,128)(2,1)S(1)}, u32[]{:S(2)}) copy-start(bf16[256,2048]{1,0:T(8,128)(2,1)S(1)} %get-tuple-element.25) | copy-start | bytes 3145732
  177.1 11.8 %copy-start.8 = (bf16[256,2048]{1,0:T(8,128)(2,1)}, bf16[256,2048]{1,0:T(8,128)(2,1)S(1)}, u32[]{:S(2)}) copy-start(bf16[256,2048]{1,0:T(8,128)(2,1)S(1)} %get-tuple-element.26) | copy-start | bytes 3145732
  177.1 11.8 %copy-start.10 = (bf16[256,2048]{1,0:T(8,128)(2,1)}, bf16[256,2048]{1,0:T(8,128)(2,1)S(1)}, u32[]{:S(2)}) copy-start(bf16[256,2048]{1,0:T(8,128)(2,1)S(1)} %get-tuple-element.27) | copy-start | bytes 3145732
  177.1 11.8 %copy-start.12 = (bf16[256,2048]{1,0:T(8,128)(2,1)}, bf16[256,2048]{1,0:T(8,128)(2,1)S(1)}, u32[]{:S(2)}) copy-start(bf16[256,2048]{1,0:T(8,128)(2,1)S(1)} %get-tuple-element.28) | copy-start | bytes 3145732
  191.2 3.7 %copy-start.7 = (bf16[256,2048]{1,0:T(8,128)(2,1)S(1)}, bf16[256,2048]{1,0:T(8,128)(2,1)}, u32[]{:S(2)}) copy-start(bf16[256,2048]{1,0:T(8,128)(2,1)} %copy-done.6) | copy-start | bytes 3145732
  191.2 3.8 %copy-start.9 = (bf16[256,2048]{1,0:T(8,128)(2,1)S(1)}, bf16[256,2048]{1,0:T(8,128)(2,1)}, u32[]{:S(2)}) copy-start(bf16[256,2048]{1,0:T(8,128)(2,1)} %copy-done.8) | copy-start | bytes 3145732
  191.2 3.8 %copy-start.11 = (bf16[256,2048]{1,0:T(8,128)(2,1)S(1)}, bf16[256,2048]{1,0:T(8,128)(2,1)}, u32[]{:S(2)}) copy-start(bf16[256,2048]{1,0:T(8,128)(2,1)} %copy-done.10) | copy-start | bytes 3145732
  191.2 3.8 %copy-start.13 = (bf16[256,2048]{1,0:T(8,128)(2,1)S(1)}, bf16[256,2048]{1,0:T(8,128)(2,1)}, u32[]{:S(2)}) copy-start(bf16[256,2048]{1,0:T(8,128)(2,1)} %copy-done.12) | copy-start | bytes 3145732
  191.2 4.1 %copy-start.15 = (bf16[8192,128]{1,0:T(8,128)(2,1)S(1)}, bf16[8192,128]{1,0:T(8,128)(2,1)}, u32[]{:S(2)}) copy-start(bf16[8192,128]{1,0:T(8,128)(2,1)} %param.11) | copy-start | bytes 6291460
  196.7 3.2 %copy-start.2 = (bf16[2,128,1024]{2,1,0:T(8,128)(2,1)S(1)}, bf16[2,128,1024]{2,1,0:T(8,128)(2,1)}, u32[]{:S(2)}) copy-start(bf16[2,128,1024]{2,1,0:T(8,128)(2,1)} %copy.45.q_ref) | copy-start | bytes 1572868
  196.7 3.2 %copy-start.4 = (f32[16,128]{1,0:T(8,128)S(1)}, f32[16,128]{1,0:T(8,128)}, u32[]{:S(2)}) copy-start(f32[16,128]{1,0:T(8,128)} %get-tuple-element.55.c_ref.refs_4_.refs_8_) | copy-start | bytes 24580
  196.7 3.2 %copy-start.5 = (f32[16,128]{1,0:T(8,128)S(1)}, f32[16,128]{1,0:T(8,128)}, u32[]{:S(2)}) copy-start(f32[16,128]{1,0:T(8,128)} %get-tuple-element.56.s_ref.refs_5_.refs_9_) | copy-start | bytes 24580
  283.8 1.0 copy-start.3
  284.8 12.3 %copy-start.1 = (bf16[8192,128]{1,0:T(8,128)(2,1)S(1)}, bf16[8192,128]{1,0:T(8,128)(2,1)}, u32[]{:S(2)}) copy-start(bf16[8192,128]{1,0:T(8,128)(2,1)} %param.10) | copy-start | bytes 6291460
